TPU v7x, 256 devices: a whole 4x4x8 slice. The times are simulated.
256 devices in a mesh: section: 8 (over x, z_lo), expert: 32 (over z_hi, y, core).
Axes of the slice: x: 4, y: 4, z: 8 (z_hi: 4, z_lo: 2; z = z_hi * 2 + z_lo), core: 2. Of those that a mesh axis runs over, the one named last changes fastest.
Arguments:
- grad_out: bfloat16 [8, 6144, 2048], P('section', 'expert'), may hold values from -6 to 6
- layer_input: bfloat16 [8, 6144, 2048], P('section', 'expert'), may hold values from -6 to 6
- routes: int32 [8, 6144, 8], P('section', 'expert'), may hold values from 0 to 127, as said below
- route_logits: float32 [8, 6144, 8], P('section', 'expert'), may hold values from -6 to 6
- gate_weight: bfloat16 [8, 32, 2048, 768], P('section', 'expert'), may hold values from -0.125 to 0.125
- up_weight: bfloat16 [8, 32, 2048, 768], P('section', 'expert'), may hold values from -0.125 to 0.125
- down_weight: bfloat16 [8, 32, 768, 2048], P('section', 'expert'), may hold values from -0.21875 to 0.21875
- router_weight: bfloat16 [8, 2048, 128], P('section'), may hold values from -0.125 to 0.125
Outputs:
- grad_in: bfloat16 [8, 6144, 2048], P('section', 'expert')
- route_logit_grad: float32 [8, 6144, 8], P('section', 'expert')
Inputs may be any that keep to these rules, and one draw needn't show every extreme that they name: `routes`: each token names 8 different experts. Among the tokens of one device no expert is named more than 24 times, and in every section one expert below 32 is named exactly 24 times by the tokens of every device of that section.
All inputs are finite; a program needn't handle non-finite values.
Results may differ from a plain program's by a relative error of at most 0.004.
Values may be sent and summed in bfloat16 or wider, within the bound.
No kernel may reach another device: no remote copies, remote signals or barrier semaphores. Data moves between devices by JAX's collectives and lax.ppermute only.
A program may use at most 128 MiB of HBM per device.

v0:
```python
import jax
import jax.numpy as jnp
from jax import lax
from jax.sharding import PartitionSpec as P


def from_behind(shard, axis, by):
    size = lax.axis_size(axis)
    return lax.ppermute(shard, axis, [(i, (i + by) % size) for i in range(size)])


def expert_rows(inputs, grad_rows, w_gate, w_up, w_down):
    pre_gate = jnp.dot(inputs, w_gate, preferred_element_type=jnp.float32)
    pre_up = jnp.dot(inputs, w_up, preferred_element_type=jnp.float32)
    hidden_grad = jnp.dot(grad_rows, w_down.T, preferred_element_type=jnp.float32)
    sigmoid_gate = jax.nn.sigmoid(pre_gate)
    activation = pre_gate * sigmoid_gate
    weight_grad = jnp.sum(hidden_grad * activation * pre_up, axis=-1).astype(jnp.bfloat16)
    gate_grad = (
        hidden_grad * pre_up * sigmoid_gate * (1.0 + pre_gate * (1.0 - sigmoid_gate))
    ).astype(jnp.bfloat16)
    up_grad = (hidden_grad * activation).astype(jnp.bfloat16)
    pair_grad = jnp.dot(gate_grad, w_gate.T, preferred_element_type=jnp.float32) + jnp.dot(
        up_grad, w_up.T, preferred_element_type=jnp.float32
    )
    return (pair_grad.astype(jnp.bfloat16), weight_grad)


def per_device(
    grad_out, layer_input, routes, route_logits, gate_weight, up_weight, down_weight, router_weight
):
    token_count = layer_input.shape[1]
    width_model = layer_input.shape[2]
    top_count = routes.shape[2]
    expert_count = lax.axis_size("expert")
    every_expert = router_weight.shape[2]
    capacity = 2 * token_count * top_count // every_expert
    slots_all = expert_count * capacity
    w_gate = gate_weight[0, 0]
    w_up = up_weight[0, 0]
    w_down = down_weight[0, 0]
    w_router = router_weight[0]
    picks = routes[0]
    flat_routes = picks.reshape(-1)
    route_count = flat_routes.shape[0]
    onehot = (flat_routes[:, None] == jnp.arange(expert_count, dtype=jnp.int32)[None, :]).astype(
        jnp.int32
    )
    rank_inside = jnp.sum((jnp.cumsum(onehot, axis=0) - 1) * onehot, axis=1)
    slot_index = jnp.where(
        flat_routes < expert_count, flat_routes * capacity + rank_inside, slots_all
    )
    slot_owner = jnp.full((slots_all + 1,), route_count, jnp.int32)
    slot_owner = slot_owner.at[slot_index].set(jnp.arange(route_count, dtype=jnp.int32))[:slots_all]
    token_index = jnp.where(slot_owner < route_count, slot_owner // top_count, token_count)

    def pack_rows(source):
        padded = jnp.concatenate([source, jnp.zeros((1, width_model), source.dtype)], axis=0)
        return padded[token_index].reshape(expert_count, capacity, width_model)

    sent_inputs = pack_rows(layer_input[0])
    incoming = from_behind(grad_out, "section", -1)[0]
    inputs = lax.all_to_all(sent_inputs, "expert", split_axis=0, concat_axis=0, tiled=True)
    senders = inputs.shape[0]
    per_source = inputs.shape[1]
    pair_grad, weight_grad = expert_rows(
        inputs.reshape(-1, width_model),
        lax.all_to_all(
            pack_rows(incoming), "expert", split_axis=0, concat_axis=0, tiled=True
        ).reshape(-1, width_model),
        w_gate,
        w_up,
        w_down,
    )
    pair_rows = pair_grad.reshape(senders, per_source, width_model)
    pair_dots = weight_grad.reshape(senders, per_source)
    returned_rows, returned_dots = (
        lax.all_to_all(pair_rows, "expert", split_axis=0, concat_axis=0, tiled=True),
        lax.all_to_all(pair_dots, "expert", split_axis=0, concat_axis=0, tiled=True),
    )
    flat_rows = jnp.concatenate(
        [returned_rows.reshape(slots_all, width_model), jnp.zeros((1, width_model), jnp.bfloat16)],
        axis=0,
    )
    flat_dots = jnp.concatenate(
        [returned_dots.reshape(slots_all), jnp.zeros((1,), jnp.bfloat16)], axis=0
    )
    route_rows = flat_rows[slot_index].reshape(token_count, top_count, width_model)
    weight_grad = flat_dots[slot_index].reshape(token_count, top_count).astype(jnp.float32)
    exponent = jnp.exp(route_logits[0])
    route_weight = exponent / jnp.sum(exponent, axis=1, keepdims=True)
    expert_sum = jnp.sum(route_weight[:, :, None] * route_rows, axis=1)
    center = jnp.sum(route_weight * weight_grad, axis=1, keepdims=True)
    logit_grad = route_weight * (weight_grad - center)
    matches = picks[:, :, None] == jnp.arange(every_expert, dtype=jnp.int32)[None, None, :]
    dense_grad = jnp.sum(jnp.where(matches, logit_grad[:, :, None], 0.0), axis=1)
    router_grad = jnp.dot(
        dense_grad, w_router.astype(jnp.float32).T, precision=lax.Precision.HIGHEST
    )
    grad_in = (incoming.astype(jnp.float32) + expert_sum + router_grad).astype(jnp.bfloat16)
    return (grad_in[None], logit_grad[None])


def solution(mesh):
    in_specs = (
        P("section", "expert", None),
        P("section", "expert", None),
        P("section", "expert", None),
        P("section", "expert", None),
        P("section", "expert", None, None),
        P("section", "expert", None, None),
        P("section", "expert", None, None),
        P("section", None, None),
    )
    out_specs = (P("section", "expert", None), P("section", "expert", None))
    return jax.shard_map(
        per_device, mesh=mesh, in_specs=in_specs, out_specs=out_specs, check_vma=False
    )
```

profile of v0, /device:TPU:33, one launch (start us, length us, event | category | flops | bytes accessed | tf_op | source)
XLA Modules:
  0.0 377.4 jit_solution(4195261064766581644)
XLA Ops:
  0.6 0.9 broadcast_compare_fusion
  2.3 0.8 copy.35
  4.5 15.9 %reduce-window.6 = s32[32,12,128]{2,1,0:T(8,128)S(1)} reduce-window(s32[32,12,128]{2,1,0:T(8,128)} %fusion.17, s32[]{:T(128)} %constant.13.clone.1), window={size=1x1x128 pad=0_0x0_0x127_0}, to_apply=%region_1.2 | reduce-window | flops 6242304 | bytes 393220 | tf_op jit(solution)/shard_map/reduce-window
  20.4 0.8 slice.20
  21.3 1.1 copy.37
  22.8 6.2 %scatter_custom_fusion = s32[769]{0:T(1024)S(1)} fusion(s32[1536]{0:T(1024)S(1)} %fusion.20, s32[1536]{0:T(1024)S(1)} %iota.15, s32[]{:T(128)} %constant.12.clone.1), kind=kCustom, calls=%fused_computation.57 | custom fusion | bytes 3080 | tf_op jit(solution)/shard_map/scatter | solution.py:54
  29.0 2.1 concatenate.13
  31.1 8.4 %gather_fusion.1 = bf16[768,2048]{1,0:T(8,128)(2,1)} fusion(bf16[193,2048]{1,0:T(8,128)(2,1)} %concatenate.13, s32[1024]{0:T(1024)S(1)} %pad_clamp_fusion.1), kind=kCustom, calls=%fused_computation.1 | custom fusion | bytes 6294528 | tf_op jit(solution)/shard_map/gather | solution.py:59
  39.5 11.1 %all-to-all-start.1 = ((bf16[32,24,2048]{2,1,0:T(8,128)(2,1)}), bf16[32,24,2048]{2,1,0:T(8,128)(2,1)}, u32[]{:S(2)}, u32[]{:S(2)}) async-start(bf16[32,24,2048]{2,1,0:T(8,128)(2,1)} %bitcast.57), calls=%async_computation.1 | async-start | bytes 6291456 | tf_op jit(solution)/shard_map/all_to_all | solution.py:63
  50.6 0.8 collective-permute-start
  51.4 86.3 %collective-permute-done = bf16[1,192,2048]{2,1,0:T(8,128)(2,1)S(1)} collective-permute-done((bf16[1,192,2048]{2,1,0:T(8,128)(2,1)}, bf16[1,192,2048]{2,1,0:T(8,128)(2,1)S(1)}, u32[]{:S(2)}, u32[]{:S(2)}) %collective-permute-start) | collective-permute-done | bytes 786464 | tf_op jit(solution)/shard_map/ppermute | solution.py:9
  137.7 0.9 copy-done.1
  138.5 1.0 concatenate.12
  139.5 8.4 %gather_fusion = bf16[768,2048]{1,0:T(8,128)(2,1)} fusion(bf16[193,2048]{1,0:T(8,128)(2,1)} %concatenate.12, s32[1024]{0:T(1024)S(1)} %pad_clamp_fusion.1), kind=kCustom, calls=%fused_computation | custom fusion | bytes 6294528 | tf_op jit(solution)/shard_map/gather | solution.py:59
  148.0 9.7 %all-to-all-start = ((bf16[32,24,2048]{2,1,0:T(8,128)(2,1)}), bf16[32,24,2048]{2,1,0:T(8,128)(2,1)}, u32[]{:S(2)}, u32[]{:S(2)}) async-start(bf16[32,24,2048]{2,1,0:T(8,128)(2,1)} %bitcast.58), calls=%async_computation | async-start | bytes 6291456 | tf_op jit(solution)/shard_map/all_to_all | solution.py:68
  157.6 6.9 %fusion.3 = f32[768,768]{0,1:T(8,128)} fusion(bf16[768,2048]{1,0:T(8,128)(2,1)} %bitcast.9, bf16[1,1,2048,768]{3,2,1,0:T(8,128)(2,1)} %param.12), kind=kOutput, calls=%fused_computation.10 | convolution fusion | flops 2415919104 | bytes 8650752 | tf_op jit(solution)/shard_map/dot_general | solution.py:13
  164.5 68.7 %all-to-all-done = bf16[32,24,2048]{2,1,0:T(8,128)(2,1)} async-done(((bf16[32,24,2048]{2,1,0:T(8,128)(2,1)}), bf16[32,24,2048]{2,1,0:T(8,128)(2,1)}, u32[]{:S(2)}, u32[]{:S(2)}) %all-to-all-start) | async-done | bytes 3145760 | tf_op jit(solution)/shard_map/all_to_all | solution.py:68
  233.3 5.6 %fusion.8 = f32[768,768]{0,1:T(8,128)S(1)} fusion(bf16[768,2048]{1,0:T(8,128)(2,1)} %bitcast.5, bf16[1,1,768,2048]{3,2,1,0:T(8,128)(2,1)} %param.14), kind=kOutput, calls=%fused_computation.15 | convolution fusion | flops 2415919104 | bytes 8650752 | tf_op jit(solution)/shard_map/dot_general | solution.py:15
  238.9 6.0 %multiply_reduce_fusion = (bf16[768]{0:T(1024)(128)(2,1)S(1)}, f32[768,768]{0,1:T(8,128)S(1)}) fusion(f32[768,768]{0,1:T(8,128)S(1)} %fusion.8, f32[768,768]{0,1:T(8,128)S(1)} %copy-done.7, bf16[768,2048]{1,0:T(8,128)(2,1)} %bitcast.9, bf16[1,1,2048,768]{3,2,1,0:T(8,128)(2,1)S(1)} %copy-done), kind=kOutput, calls=%fused_computation.17 | convolution fusion | flops 2420047104 | bytes 13370880 | tf_op jit(solution)/shard_map/dot_general | solution.py:14
  245.0 5.8 %fusion.1 = f32[768,2048]{1,0:T(8,128)} fusion(bf16[1,1,2048,768]{3,2,1,0:T(8,128)(2,1)S(1)} %copy-done.6, f32[768,768]{0,1:T(8,128)S(1)} %copy-done.7, f32[768,768]{0,1:T(8,128)S(1)} %fusion.8, f32[768,768]{0,1:T(8,128)S(1)} %get-tuple-element.11), kind=kOutput, calls=%fused_computation.8 | convolution fusion | flops 2421817344 | bytes 16515072 | tf_op jit(solution)/shard_map/dot_general | solution.py:23
  251.5 4.1 %all-to-all-start.3 = ((bf16[32,1,24]{2,1,0:T(2,128)(2,1)}), bf16[32,1,24]{2,1,0:T(2,128)(2,1)S(1)}, u32[]{:S(2)}, u32[]{:S(2)}) async-start(bf16[32,1,24]{2,1,0:T(2,128)(2,1)} %convert_element_type.80), calls=%async_computation.3 | async-start | bytes 32768 | tf_op jit(solution)/shard_map/all_to_all | solution.py:79
  255.6 7.5 %add_convert_fusion = bf16[768,2048]{1,0:T(8,128)(2,1)} fusion(f32[768,2048]{1,0:T(8,128)} %fusion.1, bf16[1,1,2048,768]{3,2,1,0:T(8,128)(2,1)S(1)} %copy-done, f32[768,768]{0,1:T(8,128)} %copy-done.8, f32[768,768]{0,1:T(8,128)} %fusion.3), kind=kOutput, calls=%fused_computation.7 | convolution fusion | flops 2422603776 | bytes 17301504 | tf_op jit(solution)/shard_map/dot_general | solution.py:23
  263.1 1.9 all-to-all-done.3
  264.9 8.1 %all-to-all-start.2 = ((bf16[32,24,2048]{2,1,0:T(8,128)(2,1)}), bf16[32,24,2048]{2,1,0:T(8,128)(2,1)}, u32[]{:S(2)}, u32[]{:S(2)}) async-start(bf16[32,24,2048]{2,1,0:T(8,128)(2,1)} %bitcast.60), calls=%async_computation.2 | async-start | bytes 6291456 | tf_op jit(solution)/shard_map/all_to_all | solution.py:78
  274.2 9.5 %gather_fusion.3 = bf16[1536]{0:T(1024)(128)(2,1)S(1)} fusion(bf16[769]{0:T(1024)(128)(2,1)S(1)} %pad_maximum_fusion, s32[2048]{0:T(1024)S(1)} %pad_clamp_fusion), kind=kCustom, calls=%fused_computation.3 | custom fusion | bytes 12288 | tf_op jit(solution)/shard_map/gather | solution.py:89
  284.9 1.6 copy.41
  286.5 1.8 select_reduce_fusion
  288.3 58.9 %all-to-all-done.2 = bf16[32,24,2048]{2,1,0:T(8,128)(2,1)} async-done(((bf16[32,24,2048]{2,1,0:T(8,128)(2,1)}), bf16[32,24,2048]{2,1,0:T(8,128)(2,1)}, u32[]{:S(2)}, u32[]{:S(2)}) %all-to-all-start.2) | async-done | bytes 3145760 | tf_op jit(solution)/shard_map/all_to_all | solution.py:78
  347.2 4.0 %concatenate.14 = bf16[769,2048]{1,0:T(8,128)(2,1)} pad(bf16[768,2048]{1,0:T(8,128)(2,1)} %bitcast.13, bf16[]{:T(256)} %constant.17.clone.1), padding=0_1x0_0 | pad | bytes 6295554 | tf_op jit(solution)/shard_map/concatenate | solution.py:81
  351.2 15.0 %gather_fusion.2 = bf16[1536,2048]{1,0:T(8,128)(2,1)} fusion(bf16[769,2048]{1,0:T(8,128)(2,1)} %concatenate.14, s32[2048]{0:T(1024)S(1)} %pad_clamp_fusion), kind=kCustom, calls=%fused_computation.2 | custom fusion | bytes 12589056 | tf_op jit(solution)/shard_map/gather | solution.py:88
  366.3 9.3 %fusion = f32[192,2048]{1,0:T(8,128)S(1)} fusion(bf16[1536,2048]{1,0:T(8,128)(2,1)} %gather_fusion.2, f32[192,8]{1,0:T(8,128)S(1)} %get-tuple-element.9), kind=kLoop, calls=%fused_computation.6 | loop fusion | flops 9043968 | bytes 7870464 | tf_op jit(solution)/shard_map/reduce_sum | solution.py:92
  375.6 1.8 fusion.12
  (47 shorter events, 5.7 us)
Async XLA Ops:
  0.6 238.3 %copy-start = (bf16[1,1,2048,768]{3,2,1,0:T(8,128)(2,1)S(1)}, bf16[1,1,2048,768]{3,2,1,0:T(8,128)(2,1)}, u32[]{:S(2)}) copy-start(bf16[1,1,2048,768]{3,2,1,0:T(8,128)(2,1)} %param.13) | copy-start | bytes 9437188
  39.5 108.4 %all-to-all-start.1 = ((bf16[32,24,2048]{2,1,0:T(8,128)(2,1)}), bf16[32,24,2048]{2,1,0:T(8,128)(2,1)}, u32[]{:S(2)}, u32[]{:S(2)}) async-start(bf16[32,24,2048]{2,1,0:T(8,128)(2,1)} %bitcast.57), calls=%async_computation.1 | async-start | bytes 6291456 | tf_op jit(solution)/shard_map/all_to_all | solution.py:63
  50.6 87.1 %collective-permute-start = (bf16[1,192,2048]{2,1,0:T(8,128)(2,1)}, bf16[1,192,2048]{2,1,0:T(8,128)(2,1)S(1)}, u32[]{:S(2)}, u32[]{:S(2)}) collective-permute-start(bf16[1,192,2048]{2,1,0:T(8,128)(2,1)} %param.8), channel_id=1, source_target_pairs={{0,224},{32,0},{64,32},{96,64},{128,96},{160,128},{192,160},{224,1... | collective-permute-start | bytes 2359304 | tf_op jit(solution)/shard_map/ppermute | solution.py:9
  137.7 0.9 copy-start.1
  148.0 85.3 %all-to-all-start = ((bf16[32,24,2048]{2,1,0:T(8,128)(2,1)}), bf16[32,24,2048]{2,1,0:T(8,128)(2,1)}, u32[]{:S(2)}, u32[]{:S(2)}) async-start(bf16[32,24,2048]{2,1,0:T(8,128)(2,1)} %bitcast.58), calls=%async_computation | async-start | bytes 6291456 | tf_op jit(solution)/shard_map/all_to_all | solution.py:68
  233.3 5.6 %copy-start.7 = (f32[768,768]{0,1:T(8,128)S(1)}, f32[768,768]{0,1:T(8,128)}, u32[]{:S(2)}) copy-start(f32[768,768]{0,1:T(8,128)} %fusion.3) | copy-start | bytes 7077892
  238.9 6.0 %copy-start.8 = (f32[768,768]{0,1:T(8,128)}, f32[768,768]{0,1:T(8,128)S(1)}, u32[]{:S(2)}) copy-start(f32[768,768]{0,1:T(8,128)S(1)} %fusion.8) | copy-start | bytes 7077892
  238.9 6.0 %copy-start.6 = (bf16[1,1,2048,768]{3,2,1,0:T(8,128)(2,1)S(1)}, bf16[1,1,2048,768]{3,2,1,0:T(8,128)(2,1)}, u32[]{:S(2)}) copy-start(bf16[1,1,2048,768]{3,2,1,0:T(8,128)(2,1)} %param.12) | copy-start | bytes 9437188
  251.5 13.4 %all-to-all-start.3 = ((bf16[32,1,24]{2,1,0:T(2,128)(2,1)}), bf16[32,1,24]{2,1,0:T(2,128)(2,1)S(1)}, u32[]{:S(2)}, u32[]{:S(2)}) async-start(bf16[32,1,24]{2,1,0:T(2,128)(2,1)} %convert_element_type.80), calls=%async_computation.3 | async-start | bytes 32768 | tf_op jit(solution)/shard_map/all_to_all | solution.py:79
  264.9 8.1 %copy-start.5 = (f32[1,192,8]{1,2,0:T(8,128)S(1)}, f32[1,192,8]{1,2,0:T(8,128)}, u32[]{:S(2)}) copy-start(f32[1,192,8]{1,2,0:T(8,128)} %param.11) | copy-start | bytes 18436
  264.9 8.2 %copy-start.4 = (s32[1,192,8]{1,2,0:T(8,128)S(1)}, s32[1,192,8]{1,2,0:T(8,128)}, u32[]{:S(2)}) copy-start(s32[1,192,8]{1,2,0:T(8,128)} %param.10) | copy-start | bytes 18436
  264.9 82.3 %all-to-all-start.2 = ((bf16[32,24,2048]{2,1,0:T(8,128)(2,1)}), bf16[32,24,2048]{2,1,0:T(8,128)(2,1)}, u32[]{:S(2)}, u32[]{:S(2)}) async-start(bf16[32,24,2048]{2,1,0:T(8,128)(2,1)} %bitcast.60), calls=%async_computation.2 | async-start | bytes 6291456 | tf_op jit(solution)/shard_map/all_to_all | solution.py:78
  366.2 9.3 %copy-start.2 = (bf16[1,192,2048]{2,1,0:T(8,128)(2,1)S(1)}, bf16[1,192,2048]{2,1,0:T(8,128)(2,1)}, u32[]{:S(2)}) copy-start(bf16[1,192,2048]{2,1,0:T(8,128)(2,1)} %copy-done.1) | copy-start | bytes 2359300
  366.2 9.3 %copy-start.3 = (bf16[1,2048,128]{2,1,0:T(8,128)(2,1)S(1)}, bf16[1,2048,128]{2,1,0:T(8,128)(2,1)}, u32[]{:S(2)}) copy-start(bf16[1,2048,128]{2,1,0:T(8,128)(2,1)} %param.15) | copy-start | bytes 1572868
where the time goes:
time: 379 us; the launch traced here: 377 us
  waiting for transfers between devices  216 us (57%)
  local copies, waits for them, and re-layouts  62.4 us (16%)
  starting transfers between devices  33.8 us (9%)
  matrix products  33.6 us (9%)
  other arithmetic  30.9 us (8%)
    ppermute x1, waiting for transfers between devices, from_behind(): lax.ppermute(shard, axis, [(i, (i + by) % size) for i in range(size)])  86.3 us
    all_to_all x1, waiting for transfers between devices, per_device(): lax.all_to_all(pack_rows(incoming), 'expert', split_axis=0, concat_axis=0...  68.7 us
    all_to_all x1, waiting for transfers between devices, per_device(): lax.all_to_all(pair_rows, 'expert', split_axis=0, concat_axis=0, tiled=True)  58.9 us
    gather x2, local copies, waits for them, and re-layouts, pack_rows(): return padded[token_index].reshape(expert_count, capacity, width_model)  16.8 us
    another operation x2, other arithmetic  15.9 us
    gather x1, local copies, waits for them, and re-layouts, per_device(): flat_rows[slot_index].reshape(token_count, top_count, width_model)  15 us
    all_to_all x1, starting transfers between devices, per_device(): lax.all_to_all(sent_inputs, 'expert', split_axis=0, concat_axis=0, tiled=...  11.1 us
    all_to_all x1, starting transfers between devices, per_device(): lax.all_to_all(pack_rows(incoming), 'expert', split_axis=0, concat_axis=0...  9.68 us
  transfers between devices with their start and end apart: 5, of which 4 were waited for; matrix products, arithmetic and copies ran while one was open for 10% of the time, Pallas kernels for 0%

commit v1 on v0

v1 whole, which is shorter than its diff:
```python
import jax
import jax.numpy as jnp
from jax import lax
from jax.sharding import PartitionSpec as P


def from_behind(shard, axis, by):
    size = lax.axis_size(axis)
    return lax.ppermute(shard, axis, [(i, (i + by) % size) for i in range(size)])


def expert_rows(inputs, grad_rows, w_gate, w_up, w_down):
    pre_gate = jnp.dot(inputs, w_gate, preferred_element_type=jnp.float32)
    pre_up = jnp.dot(inputs, w_up, preferred_element_type=jnp.float32)
    hidden_grad = jnp.dot(grad_rows, w_down.T, preferred_element_type=jnp.float32)
    sigmoid_gate = jax.nn.sigmoid(pre_gate)
    activation = pre_gate * sigmoid_gate
    weight_grad = jnp.sum(hidden_grad * activation * pre_up, axis=-1).astype(jnp.bfloat16)
    gate_grad = (
        hidden_grad * pre_up * sigmoid_gate * (1.0 + pre_gate * (1.0 - sigmoid_gate))
    ).astype(jnp.bfloat16)
    up_grad = (hidden_grad * activation).astype(jnp.bfloat16)
    pair_grad = jnp.dot(gate_grad, w_gate.T, preferred_element_type=jnp.float32) + jnp.dot(
        up_grad, w_up.T, preferred_element_type=jnp.float32
    )
    return (pair_grad.astype(jnp.bfloat16), weight_grad)


def split_bf16(values, parts):
    pieces = []
    rest = values
    for _ in range(parts):
        piece = rest.astype(jnp.bfloat16)
        pieces.append(piece)
        rest = rest - piece.astype(jnp.float32)
    return pieces


def per_device(
    grad_out, layer_input, routes, route_logits, gate_weight, up_weight, down_weight, router_weight
):
    incoming = from_behind(grad_out, "section", -1)[0]
    x_in = layer_input[0]
    token_count, width_model = x_in.shape
    top_count = routes.shape[2]
    expert_count = lax.axis_size("expert")
    every_expert = router_weight.shape[2]
    capacity = 2 * token_count * top_count // every_expert
    slots_all = expert_count * capacity
    chunks = 2 if capacity % 2 == 0 else 1
    per_chunk = capacity // chunks
    w_gate = gate_weight[0, 0]
    w_up = up_weight[0, 0]
    w_down = down_weight[0, 0]
    w_router = router_weight[0]
    picks = routes[0]

    experts = jnp.arange(expert_count, dtype=jnp.int32)
    hit = picks[:, :, None] == experts[None, None, :]
    per_token = jnp.sum(hit.astype(jnp.float32), axis=1).astype(jnp.bfloat16)
    token_ids = jnp.arange(token_count, dtype=jnp.int32)
    before = (token_ids[None, :] < token_ids[:, None]).astype(jnp.bfloat16)
    earlier = jnp.dot(before, per_token, preferred_element_type=jnp.float32).astype(jnp.int32)
    rank_inside = jnp.sum(jnp.where(hit, earlier[:, None, :], 0), axis=2)
    slot_index = jnp.where(picks < expert_count, picks * capacity + rank_inside, slots_all)

    exponent = jnp.exp(route_logits[0])
    route_weight = exponent / jnp.sum(exponent, axis=1, keepdims=True)

    slot_ids = jnp.arange(slots_all, dtype=jnp.int32)
    slot_by_pick = slot_index.T
    weight_by_pick = route_weight.T
    pack = jnp.zeros((slots_all, token_count), jnp.float32)
    combine = jnp.zeros((token_count, slots_all), jnp.float32)
    for k in range(top_count):
        pack = pack + (slot_ids[:, None] == slot_by_pick[k][None, :]).astype(jnp.float32)
        combine = combine + jnp.where(
            slot_by_pick[k][:, None] == slot_ids[None, :], weight_by_pick[k][:, None], 0.0
        )
    pack = pack.astype(jnp.bfloat16).reshape(expert_count, capacity, token_count)
    combine = combine.reshape(token_count, expert_count, capacity)
    both_rows = jnp.concatenate([x_in, incoming], axis=1)

    expert_sum = jnp.zeros((token_count, width_model), jnp.float32)
    dots = []
    for c in range(chunks):
        lo = c * per_chunk
        pack_c = pack[:, lo : lo + per_chunk].reshape(-1, token_count)
        sent = jnp.dot(pack_c, both_rows, preferred_element_type=jnp.float32).astype(jnp.bfloat16)
        sent = sent.reshape(expert_count, per_chunk, 2 * width_model)
        got = lax.all_to_all(sent, "expert", split_axis=0, concat_axis=0, tiled=True)
        got = got.reshape(-1, 2 * width_model)
        pair_grad, weight_grad = expert_rows(
            got[:, :width_model], got[:, width_model:], w_gate, w_up, w_down
        )
        back_rows = lax.all_to_all(
            pair_grad.reshape(expert_count, per_chunk, width_model),
            "expert", split_axis=0, concat_axis=0, tiled=True,
        ).reshape(-1, width_model)
        back_dots = lax.all_to_all(
            weight_grad.reshape(expert_count, per_chunk),
            "expert", split_axis=0, concat_axis=0, tiled=True,
        )
        dots.append(back_dots)
        combine_c = combine[:, :, lo : lo + per_chunk].reshape(token_count, -1)
        for part in split_bf16(combine_c, 2):
            expert_sum = expert_sum + jnp.dot(part, back_rows, preferred_element_type=jnp.float32)

    slot_dots = jnp.concatenate(dots, axis=1).reshape(slots_all).astype(jnp.float32)
    weight_grad = jnp.sum(
        jnp.where(slot_index[:, :, None] == slot_ids[None, None, :], slot_dots[None, None, :], 0.0),
        axis=2,
    )
    center = jnp.sum(route_weight * weight_grad, axis=1, keepdims=True)
    logit_grad = route_weight * (weight_grad - center)
    matches = picks[:, :, None] == jnp.arange(every_expert, dtype=jnp.int32)[None, None, :]
    dense_grad = jnp.sum(jnp.where(matches, logit_grad[:, :, None], 0.0), axis=1)
    router_grad = jnp.zeros((token_count, width_model), jnp.float32)
    for part in split_bf16(dense_grad, 3):
        router_grad = router_grad + lax.dot_general(
            part, w_router, (((1,), (1,)), ((), ())), preferred_element_type=jnp.float32
        )
    grad_in = (incoming.astype(jnp.float32) + expert_sum + router_grad).astype(jnp.bfloat16)
    return (grad_in[None], logit_grad[None])


def solution(mesh):
    in_specs = (
        P("section", "expert", None),
        P("section", "expert", None),
        P("section", "expert", None),
        P("section", "expert", None),
        P("section", "expert", None, None),
        P("section", "expert", None, None),
        P("section", "expert", None, None),
        P("section", None, None),
    )
    out_specs = (P("section", "expert", None), P("section", "expert", None))
    return jax.shard_map(
        per_device, mesh=mesh, in_specs=in_specs, out_specs=out_specs, check_vma=False
    )
```

time: 379 us -> 419 us (1.11)
  waiting for transfers between devices: 216 us -> 258 us
  matrix products: 33.6 us -> 62.7 us
  local copies, waits for them, and re-layouts: 62.4 us -> 38.5 us
  other arithmetic: 30.9 us -> 8.69 us
  starting transfers between devices: 33.8 us -> 45.6 us
    all_to_all x4 -> x6, waiting for transfers between devices: 129 us -> 244 us  [the longest x2 171 us: per_device(): lax.all_to_all(sent, 'expert', split_axis=0, concat_axis=0, tiled=True)]
    ppermute x1, waiting for transfers between devices: 86.3 us -> 14.3 us  [from_behind(): lax.ppermute(shard, axis, [(i, (i + by) % size) for i in range(size)])]
    gather x4 -> x0, local copies, waits for them, and re-layouts: 41.3 us -> none  [the longest x2 16.8 us: pack_rows(): return padded[token_index].reshape(expert_count, capacity, width_model)]
    reshape x1 -> x8, local copies, waits for them, and re-layouts: 0.1 us -> 31.5 us  [the longest x2 11.2 us: per_device(): got = got.reshape(-1, 2 * width_model)]
    dot_general x1 -> x10, matrix products: 1.77 us -> 24.5 us  [the longest x4 14.1 us: per_device(): jnp.dot(part, back_rows, preferred_element_type=jnp.float32)]
    another operation x2 -> x0, other arithmetic: 15.9 us -> none
    all_to_all x4 -> x6, starting transfers between devices: 33 us -> 45.5 us  [the longest x2 17.4 us: per_device(): lax.all_to_all(sent, 'expert', split_axis=0, concat_axis=0, tiled=True)]
    concatenate x3 -> x0, local copies, waits for them, and re-layouts: 7.08 us -> none  [the longest x1 4 us: per_device(): jnp.concatenate([returned_rows.reshape(slots_all, width_model), jnp.zeros...]
  transfers between devices with their start and end apart: 5 -> 7, of which waited for: 4 -> 7; matrix products, arithmetic and copies ran while one was open for 10% -> 18% of each run, Pallas kernels for 0% -> 0%
where the time goes in v1:
time: 419 us; the launch traced here: 415 us
  waiting for transfers between devices  258 us (62%)
  matrix products  62.7 us (15%)
  starting transfers between devices  45.6 us (11%)
  local copies, waits for them, and re-layouts  38.5 us (9%)
  other arithmetic  8.69 us (2%)
    all_to_all x2, waiting for transfers between devices, per_device(): lax.all_to_all(sent, 'expert', split_axis=0, concat_axis=0, tiled=True)  171 us
    all_to_all x2, waiting for transfers between devices, per_device(): lax.all_to_all(pair_grad.reshape(expert_count, per_chunk, width_model), '...  71.8 us
    all_to_all x2, starting transfers between devices, per_device(): lax.all_to_all(sent, 'expert', split_axis=0, concat_axis=0, tiled=True)  17.4 us
    ppermute x1, waiting for transfers between devices, from_behind(): lax.ppermute(shard, axis, [(i, (i + by) % size) for i in range(size)])  14.3 us
    all_to_all x2, starting transfers between devices, per_device(): lax.all_to_all(pair_grad.reshape(expert_count, per_chunk, width_model), '...  14.3 us
    dot_general x4, matrix products, per_device(): jnp.dot(part, back_rows, preferred_element_type=jnp.float32)  14.1 us
    all_to_all x2, starting transfers between devices, per_device(): lax.all_to_all(weight_grad.reshape(expert_count, per_chunk), 'expert', sp...  13.8 us
    reshape x2, local copies, waits for them, and re-layouts, per_device(): got = got.reshape(-1, 2 * width_model)  11.2 us
  transfers between devices with their start and end apart: 7, of which 7 were waited for; matrix products, arithmetic and copies ran while one was open for 18% of the time, Pallas kernels for 0%

profile of v1, /device:TPU:33, one launch (start us, length us, event | category | flops | bytes accessed | tf_op | source)
XLA Modules:
  0.0 415.0 jit_solution(2823686679889056910)
XLA Ops:
  6.0 14.3 %collective-permute-done = bf16[1,192,2048]{2,1,0:T(8,128)(2,1)} collective-permute-done((bf16[1,192,2048]{2,1,0:T(8,128)(2,1)}, bf16[1,192,2048]{2,1,0:T(8,128)(2,1)}, u32[]{:S(2)}, u32[]{:S(2)}) %collective-permute-start) | collective-permute-done | bytes 786464 | tf_op jit(solution)/shard_map/ppermute | solution.py:9
  20.3 4.0 convolution_convert_fusion.1
  24.4 5.5 %reshape.355 = bf16[32,12,4096]{2,1,0:T(8,128)(2,1)} reshape(bf16[384,4096]{1,0:T(8,128)(2,1)} %convolution_convert_fusion.1) | data formatting | bytes 6291456 | tf_op jit(solution)/shard_map/reshape | solution.py:90
  29.9 12.0 %all-to-all-start = ((bf16[32,12,4096]{2,1,0:T(8,128)(2,1)}), bf16[32,12,4096]{2,1,0:T(8,128)(2,1)}, u32[]{:S(2)}, u32[]{:S(2)}) async-start(bf16[32,12,4096]{2,1,0:T(8,128)(2,1)} %reshape.355), calls=%async_computation | async-start | bytes 8388608 | tf_op jit(solution)/shard_map/all_to_all | solution.py:91
  42.9 4.0 convolution_convert_fusion
  46.9 5.5 %reshape.359 = bf16[32,12,4096]{2,1,0:T(8,128)(2,1)} reshape(bf16[384,4096]{1,0:T(8,128)(2,1)} %convolution_convert_fusion) | data formatting | bytes 6291456 | tf_op jit(solution)/shard_map/reshape | solution.py:90
  52.4 86.3 %all-to-all-done = bf16[32,12,4096]{2,1,0:T(8,128)(2,1)} async-done(((bf16[32,12,4096]{2,1,0:T(8,128)(2,1)}), bf16[32,12,4096]{2,1,0:T(8,128)(2,1)}, u32[]{:S(2)}, u32[]{:S(2)}) %all-to-all-start) | async-done | bytes 3145760 | tf_op jit(solution)/shard_map/all_to_all | solution.py:91
  138.7 5.5 %all-to-all-start.2 = ((bf16[32,12,4096]{2,1,0:T(8,128)(2,1)}), bf16[32,12,4096]{2,1,0:T(8,128)(2,1)}, u32[]{:S(2)}, u32[]{:S(2)}) async-start(bf16[32,12,4096]{2,1,0:T(8,128)(2,1)} %reshape.359), calls=%async_computation.2 | async-start | bytes 8388608 | tf_op jit(solution)/shard_map/all_to_all | solution.py:91
  144.1 5.6 %reshape.356 = bf16[384,4096]{1,0:T(8,128)(2,1)} reshape(bf16[32,12,4096]{2,1,0:T(8,128)(2,1)} %all-to-all-done) | data formatting | bytes 6291456 | tf_op jit(solution)/shard_map/reshape | solution.py:92
  149.8 5.0 %fusion.18 = f32[384,768]{1,0:T(8,128)} fusion(bf16[1,1,768,2048]{3,2,1,0:T(8,128)(2,1)} %param.14, bf16[384,4096]{1,0:T(8,128)(2,1)} %reshape.356), kind=kOutput, calls=%fused_computation.22 | convolution fusion | flops 1207959552 | bytes 5898240 | tf_op jit(solution)/shard_map/dot_general | solution.py:15
  154.8 2.5 fusion.6
  157.2 85.1 %all-to-all-done.2 = bf16[32,12,4096]{2,1,0:T(8,128)(2,1)} async-done(((bf16[32,12,4096]{2,1,0:T(8,128)(2,1)}), bf16[32,12,4096]{2,1,0:T(8,128)(2,1)}, u32[]{:S(2)}, u32[]{:S(2)}) %all-to-all-start.2) | async-done | bytes 3145760 | tf_op jit(solution)/shard_map/all_to_all | solution.py:91
  242.3 5.6 %reshape.360 = bf16[384,4096]{1,0:T(8,128)(2,1)} reshape(bf16[32,12,4096]{2,1,0:T(8,128)(2,1)} %all-to-all-done.2) | data formatting | bytes 6291456 | tf_op jit(solution)/shard_map/reshape | solution.py:92
  247.9 5.0 %fusion.16 = f32[384,768]{1,0:T(8,128)} fusion(bf16[1,1,768,2048]{3,2,1,0:T(8,128)(2,1)} %param.14, bf16[384,4096]{1,0:T(8,128)(2,1)} %reshape.360), kind=kOutput, calls=%fused_computation.20 | convolution fusion | flops 1207959552 | bytes 5898240 | tf_op jit(solution)/shard_map/dot_general | solution.py:15
  255.8 2.6 multiply_reduce_fusion.1
  259.2 4.4 %all-to-all-start.4 = ((bf16[32,1,12]{2,1,0:T(2,128)(2,1)}), bf16[32,1,12]{2,1,0:T(2,128)(2,1)S(1)}, u32[]{:S(2)}, u32[]{:S(2)}) async-start(bf16[32,1,12]{2,1,0:T(2,128)(2,1)} %convert_element_type.195), calls=%async_computation.4 | async-start | bytes 32768 | tf_op jit(solution)/shard_map/all_to_all | solution.py:100
  263.7 4.7 %multiply_reduce_fusion = (bf16[384]{0:T(512)(128)(2,1)S(1)}, f32[384,768]{1,0:T(8,128)}) fusion(f32[384,768]{1,0:T(8,128)} %fusion.16, f32[384,768]{1,0:T(8,128)} %fusion.2, bf16[1,1,2048,768]{3,2,1,0:T(8,128)(2,1)S(1)} %copy-done, bf16[384,4096]{1,0:T(8,128)(2,1)} %reshape.360), kind=kOutput, calls=%fused_computation.43 | convolution fusion | flops 1210023552 | bytes 8258304 | tf_op jit(solution)/shard_map/dot_general | solution.py:14
  268.4 3.4 fusion.4
  273.0 9.4 %all-to-all-start.5 = ((bf16[32,1,12]{2,1,0:T(2,128)(2,1)}), bf16[32,1,12]{2,1,0:T(2,128)(2,1)S(1)}, u32[]{:S(2)}, u32[]{:S(2)}) async-start(bf16[32,1,12]{2,1,0:T(2,128)(2,1)} %convert_element_type.196), calls=%async_computation.5 | async-start | bytes 32768 | tf_op jit(solution)/shard_map/all_to_all | solution.py:100
  282.3 5.2 %add_convert_fusion.1 = bf16[384,2048]{1,0:T(8,128)(2,1)} fusion(f32[384,2048]{1,0:T(8,128)} %fusion.4, bf16[1,1,2048,768]{3,2,1,0:T(8,128)(2,1)S(1)} %copy-done, f32[384,768]{1,0:T(8,128)} %fusion.18, f32[384,768]{1,0:T(8,128)} %fusion.6), kind=kOutput, calls=%fused_computation.25 | convolution fusion | flops 1211301888 | bytes 10223616 | tf_op jit(solution)/shard_map/dot_general | solution.py:23
  287.5 3.6 reshape.357
  291.6 9.5 %all-to-all-start.1 = ((bf16[32,12,2048]{2,1,0:T(8,128)(2,1)}), bf16[32,12,2048]{2,1,0:T(8,128)(2,1)}, u32[]{:S(2)}, u32[]{:S(2)}) async-start(bf16[32,12,2048]{2,1,0:T(8,128)(2,1)} %reshape.357), calls=%async_computation.1 | async-start | bytes 4194304 | tf_op jit(solution)/shard_map/all_to_all | solution.py:96
  301.6 4.8 %fusion = f32[384,2048]{1,0:T(8,128)S(1)} fusion(bf16[1,1,2048,768]{3,2,1,0:T(8,128)(2,1)} %param.12, f32[384,768]{1,0:T(8,128)} %fusion.2, f32[384,768]{1,0:T(8,128)} %fusion.16, f32[384,768]{1,0:T(8,128)} %get-tuple-element.27), kind=kOutput, calls=%fused_computation.4 | convolution fusion | flops 1210908672 | bytes 9830400 | tf_op jit(solution)/shard_map/dot_general | solution.py:23
  306.5 2.7 add_convert_fusion
  309.1 3.6 reshape.361
  313.7 39.1 %all-to-all-done.1 = bf16[32,12,2048]{2,1,0:T(8,128)(2,1)} async-done(((bf16[32,12,2048]{2,1,0:T(8,128)(2,1)}), bf16[32,12,2048]{2,1,0:T(8,128)(2,1)}, u32[]{:S(2)}, u32[]{:S(2)}) %all-to-all-start.1) | async-done | bytes 1572896 | tf_op jit(solution)/shard_map/all_to_all | solution.py:96
  352.8 4.8 %all-to-all-start.3 = ((bf16[32,12,2048]{2,1,0:T(8,128)(2,1)}), bf16[32,12,2048]{2,1,0:T(8,128)(2,1)}, u32[]{:S(2)}, u32[]{:S(2)}) async-start(bf16[32,12,2048]{2,1,0:T(8,128)(2,1)} %reshape.361), calls=%async_computation.3 | async-start | bytes 4194304 | tf_op jit(solution)/shard_map/all_to_all | solution.py:96
  368.2 2.8 convolution_bitcast_fusion.2
  371.0 3.9 fusion.24
  374.9 32.6 %all-to-all-done.3 = bf16[32,12,2048]{2,1,0:T(8,128)(2,1)} async-done(((bf16[32,12,2048]{2,1,0:T(8,128)(2,1)}), bf16[32,12,2048]{2,1,0:T(8,128)(2,1)}, u32[]{:S(2)}, u32[]{:S(2)}) %all-to-all-start.3) | async-done | bytes 1572896 | tf_op jit(solution)/shard_map/all_to_all | solution.py:96
  407.6 3.5 fusion.25
  411.1 4.0 fusion.37
  (95 shorter events, 23.6 us)
Async XLA Ops:
  0.6 254.6 %copy-start = (bf16[1,1,2048,768]{3,2,1,0:T(8,128)(2,1)S(1)}, bf16[1,1,2048,768]{3,2,1,0:T(8,128)(2,1)}, u32[]{:S(2)}) copy-start(bf16[1,1,2048,768]{3,2,1,0:T(8,128)(2,1)} %param.13) | copy-start | bytes 9437188
  0.6 19.7 %collective-permute-start = (bf16[1,192,2048]{2,1,0:T(8,128)(2,1)}, bf16[1,192,2048]{2,1,0:T(8,128)(2,1)}, u32[]{:S(2)}, u32[]{:S(2)}) collective-permute-start(bf16[1,192,2048]{2,1,0:T(8,128)(2,1)} %param.8), channel_id=1, source_target_pairs={{0,224},{32,0},{64,32},{96,64},{128,96},{160,128},{192,160},{224,1... | collective-permute-start | bytes 2359304 | tf_op jit(solution)/shard_map/ppermute | solution.py:9
  3.3 21.0 %copy-start.10 = (s32[1,192]{1,0:T(1,128)}, s32[1,192]{1,0:T(1,128)S(1)}, u32[]{:S(2)}) copy-start(s32[1,192]{1,0:T(1,128)S(1)} %get-tuple-element.18) | copy-start | bytes 2308
  3.4 21.0 %copy-start.11 = (s32[1,192]{1,0:T(1,128)}, s32[1,192]{1,0:T(1,128)S(1)}, u32[]{:S(2)}) copy-start(s32[1,192]{1,0:T(1,128)S(1)} %get-tuple-element.19) | copy-start | bytes 2308
  3.4 21.0 %copy-start.12 = (s32[1,192]{1,0:T(1,128)}, s32[1,192]{1,0:T(1,128)S(1)}, u32[]{:S(2)}) copy-start(s32[1,192]{1,0:T(1,128)S(1)} %get-tuple-element.20) | copy-start | bytes 2308
  3.4 21.0 %copy-start.13 = (s32[1,192]{1,0:T(1,128)}, s32[1,192]{1,0:T(1,128)S(1)}, u32[]{:S(2)}) copy-start(s32[1,192]{1,0:T(1,128)S(1)} %get-tuple-element.21) | copy-start | bytes 2308
  3.4 21.0 %copy-start.14 = (s32[1,192]{1,0:T(1,128)}, s32[1,192]{1,0:T(1,128)S(1)}, u32[]{:S(2)}) copy-start(s32[1,192]{1,0:T(1,128)S(1)} %get-tuple-element.22) | copy-start | bytes 2308
  3.4 21.0 %copy-start.15 = (s32[1,192]{1,0:T(1,128)}, s32[1,192]{1,0:T(1,128)S(1)}, u32[]{:S(2)}) copy-start(s32[1,192]{1,0:T(1,128)S(1)} %get-tuple-element.23) | copy-start | bytes 2308
  3.4 21.0 %copy-start.16 = (s32[1,192]{1,0:T(1,128)}, s32[1,192]{1,0:T(1,128)S(1)}, u32[]{:S(2)}) copy-start(s32[1,192]{1,0:T(1,128)S(1)} %get-tuple-element.24) | copy-start | bytes 2308
  3.4 21.0 %copy-start.17 = (s32[1,192]{1,0:T(1,128)}, s32[1,192]{1,0:T(1,128)S(1)}, u32[]{:S(2)}) copy-start(s32[1,192]{1,0:T(1,128)S(1)} %get-tuple-element.25) | copy-start | bytes 2308
  29.9 108.7 %all-to-all-start = ((bf16[32,12,4096]{2,1,0:T(8,128)(2,1)}), bf16[32,12,4096]{2,1,0:T(8,128)(2,1)}, u32[]{:S(2)}, u32[]{:S(2)}) async-start(bf16[32,12,4096]{2,1,0:T(8,128)(2,1)} %reshape.355), calls=%async_computation | async-start | bytes 8388608 | tf_op jit(solution)/shard_map/all_to_all | solution.py:91
  138.7 103.6 %all-to-all-start.2 = ((bf16[32,12,4096]{2,1,0:T(8,128)(2,1)}), bf16[32,12,4096]{2,1,0:T(8,128)(2,1)}, u32[]{:S(2)}, u32[]{:S(2)}) async-start(bf16[32,12,4096]{2,1,0:T(8,128)(2,1)} %reshape.359), calls=%async_computation.2 | async-start | bytes 8388608 | tf_op jit(solution)/shard_map/all_to_all | solution.py:91
  149.8 5.0 %copy-start.3 = (bf16[384,4096]{1,0:T(8,128)(2,1)S(1)}, bf16[384,4096]{1,0:T(8,128)(2,1)}, u32[]{:S(2)}) copy-start(bf16[384,4096]{1,0:T(8,128)(2,1)} %reshape.356) | copy-start | bytes 9437188
  149.8 5.0 %copy-start.19 = (bf16[1,1,2048,768]{3,2,1,0:T(8,128)(2,1)S(1)}, bf16[1,1,2048,768]{3,2,1,0:T(8,128)(2,1)}, u32[]{:S(2)}) copy-start(bf16[1,1,2048,768]{3,2,1,0:T(8,128)(2,1)} %param.12) | copy-start | bytes 9437188
  247.9 5.0 %copy-start.2 = (bf16[384,4096]{1,0:T(8,128)(2,1)S(1)}, bf16[384,4096]{1,0:T(8,128)(2,1)}, u32[]{:S(2)}) copy-start(bf16[384,4096]{1,0:T(8,128)(2,1)} %reshape.360) | copy-start | bytes 9437188
  247.9 5.0 %copy-start.20 = (bf16[1,1,2048,768]{3,2,1,0:T(8,128)(2,1)S(1)}, bf16[1,1,2048,768]{3,2,1,0:T(8,128)(2,1)}, u32[]{:S(2)}) copy-start(bf16[1,1,2048,768]{3,2,1,0:T(8,128)(2,1)} %param.12) | copy-start | bytes 9437188
  259.2 13.8 %all-to-all-start.4 = ((bf16[32,1,12]{2,1,0:T(2,128)(2,1)}), bf16[32,1,12]{2,1,0:T(2,128)(2,1)S(1)}, u32[]{:S(2)}, u32[]{:S(2)}) async-start(bf16[32,1,12]{2,1,0:T(2,128)(2,1)} %convert_element_type.195), calls=%async_computation.4 | async-start | bytes 32768 | tf_op jit(solution)/shard_map/all_to_all | solution.py:100
  263.6 4.7 %copy-start.21 = (bf16[1,1,2048,768]{3,2,1,0:T(8,128)(2,1)S(1)}, bf16[1,1,2048,768]{3,2,1,0:T(8,128)(2,1)}, u32[]{:S(2)}) copy-start(bf16[1,1,2048,768]{3,2,1,0:T(8,128)(2,1)} %param.12) | copy-start | bytes 9437188
  263.6 4.7 %copy-start.25 = (f32[384,768]{1,0:T(8,128)S(1)}, f32[384,768]{1,0:T(8,128)}, u32[]{:S(2)}) copy-start(f32[384,768]{1,0:T(8,128)} %fusion.18) | copy-start | bytes 3538948
  263.6 4.7 %copy-start.27 = (f32[384,768]{1,0:T(8,128)S(1)}, f32[384,768]{1,0:T(8,128)}, u32[]{:S(2)}) copy-start(f32[384,768]{1,0:T(8,128)} %fusion.6) | copy-start | bytes 3538948
  263.7 4.7 %copy-start.28 = (f32[384,768]{1,0:T(8,128)S(1)}, f32[384,768]{1,0:T(8,128)}, u32[]{:S(2)}) copy-start(f32[384,768]{1,0:T(8,128)} %get-tuple-element.29) | copy-start | bytes 3538948
  273.0 18.6 %all-to-all-start.5 = ((bf16[32,1,12]{2,1,0:T(2,128)(2,1)}), bf16[32,1,12]{2,1,0:T(2,128)(2,1)S(1)}, u32[]{:S(2)}, u32[]{:S(2)}) async-start(bf16[32,1,12]{2,1,0:T(2,128)(2,1)} %convert_element_type.196), calls=%async_computation.5 | async-start | bytes 32768 | tf_op jit(solution)/shard_map/all_to_all | solution.py:100
  291.1 10.1 %copy-start.8 = (s32[1,192,8]{1,2,0:T(8,128)S(1)}, s32[1,192,8]{1,2,0:T(8,128)}, u32[]{:S(2)}) copy-start(s32[1,192,8]{1,2,0:T(8,128)} %param.10) | copy-start | bytes 18436
  291.1 10.2 %copy-start.18 = (f32[1,192,8]{1,2,0:T(8,128)S(1)}, f32[1,192,8]{1,2,0:T(8,128)}, u32[]{:S(2)}) copy-start(f32[1,192,8]{1,2,0:T(8,128)} %param.11) | copy-start | bytes 18436
  291.6 61.2 %all-to-all-start.1 = ((bf16[32,12,2048]{2,1,0:T(8,128)(2,1)}), bf16[32,12,2048]{2,1,0:T(8,128)(2,1)}, u32[]{:S(2)}, u32[]{:S(2)}) async-start(bf16[32,12,2048]{2,1,0:T(8,128)(2,1)} %reshape.357), calls=%async_computation.1 | async-start | bytes 4194304 | tf_op jit(solution)/shard_map/all_to_all | solution.py:96
  301.6 4.8 %copy-start.22 = (f32[384,768]{1,0:T(8,128)S(1)}, f32[384,768]{1,0:T(8,128)}, u32[]{:S(2)}) copy-start(f32[384,768]{1,0:T(8,128)} %fusion.16) | copy-start | bytes 3538948
  301.6 4.8 %copy-start.23 = (f32[384,768]{1,0:T(8,128)S(1)}, f32[384,768]{1,0:T(8,128)}, u32[]{:S(2)}) copy-start(f32[384,768]{1,0:T(8,128)} %fusion.2) | copy-start | bytes 3538948
  352.8 54.8 %all-to-all-start.3 = ((bf16[32,12,2048]{2,1,0:T(8,128)(2,1)}), bf16[32,12,2048]{2,1,0:T(8,128)(2,1)}, u32[]{:S(2)}, u32[]{:S(2)}) async-start(bf16[32,12,2048]{2,1,0:T(8,128)(2,1)} %reshape.361), calls=%async_computation.3 | async-start | bytes 4194304 | tf_op jit(solution)/shard_map/all_to_all | solution.py:96
  362.2 3.7 copy-start.1
  365.9 5.1 %copy-start.6 = (f32[192,32,24]{0,1,2:T(8,128)}, f32[192,32,24]{0,1,2:T(8,128)S(1)}, u32[]{:S(2)}) copy-start(f32[192,32,24]{0,1,2:T(8,128)S(1)} %select_add_fusion) | copy-start | bytes 1769476
  407.6 3.5 copy-start.5
  407.6 3.5 copy-start.7
  (4 other events, 8.4 us)

commit v2 on v1

v2 whole, which is shorter than its diff:
```python
import jax
import jax.numpy as jnp
from jax import lax
from jax.sharding import PartitionSpec as P


def from_behind(shard, axis, by):
    size = lax.axis_size(axis)
    return lax.ppermute(shard, axis, [(i, (i + by) % size) for i in range(size)])


def split_bf16(values, parts):
    pieces = []
    rest = values
    for _ in range(parts):
        piece = rest.astype(jnp.bfloat16)
        pieces.append(piece)
        rest = rest - piece.astype(jnp.float32)
    return pieces


def per_device(
    grad_out, layer_input, routes, route_logits, gate_weight, up_weight, down_weight, router_weight
):
    incoming = from_behind(grad_out, "section", -1)[0]
    x_in = layer_input[0]
    token_count, width_model = x_in.shape
    top_count = routes.shape[2]
    expert_count = lax.axis_size("expert")
    every_expert = router_weight.shape[2]
    capacity = 2 * token_count * top_count // every_expert
    slots_all = expert_count * capacity
    w_gate = gate_weight[0, 0]
    w_up = up_weight[0, 0]
    w_down = down_weight[0, 0]
    w_router = router_weight[0]
    picks = routes[0]

    experts = jnp.arange(expert_count, dtype=jnp.int32)
    hit = picks[:, :, None] == experts[None, None, :]
    per_token = jnp.sum(hit.astype(jnp.float32), axis=1).astype(jnp.bfloat16)
    token_ids = jnp.arange(token_count, dtype=jnp.int32)
    before = (token_ids[None, :] < token_ids[:, None]).astype(jnp.bfloat16)
    earlier = jnp.dot(before, per_token, preferred_element_type=jnp.float32).astype(jnp.int32)
    rank_inside = jnp.sum(jnp.where(hit, earlier[:, None, :], 0), axis=2)
    slot_index = jnp.where(picks < expert_count, picks * capacity + rank_inside, slots_all)

    exponent = jnp.exp(route_logits[0])
    route_weight = exponent / jnp.sum(exponent, axis=1, keepdims=True)

    slot_ids = jnp.arange(slots_all, dtype=jnp.int32).reshape(expert_count, capacity)
    pack = jnp.zeros((expert_count, capacity, token_count), jnp.float32)
    combine = jnp.zeros((token_count, expert_count, capacity), jnp.float32)
    for k in range(top_count):
        chosen = slot_index[:, k]
        pack = pack + (slot_ids[:, :, None] == chosen[None, None, :]).astype(jnp.float32)
        combine = combine + jnp.where(
            chosen[:, None, None] == slot_ids[None, :, :], route_weight[:, k][:, None, None], 0.0
        )
    pack = pack.astype(jnp.bfloat16)

    def pack_rows(rows):
        sent = jnp.einsum("est,td->esd", pack, rows, preferred_element_type=jnp.float32)
        return sent.astype(jnp.bfloat16)

    def exchange(block):
        return lax.all_to_all(block, "expert", split_axis=0, concat_axis=0, tiled=True)

    inputs = exchange(pack_rows(x_in))
    grad_rows = exchange(pack_rows(incoming))
    pre_gate = jnp.einsum("esd,df->esf", inputs, w_gate, preferred_element_type=jnp.float32)
    pre_up = jnp.einsum("esd,df->esf", inputs, w_up, preferred_element_type=jnp.float32)
    hidden_grad = jnp.einsum("esd,fd->esf", grad_rows, w_down, preferred_element_type=jnp.float32)
    sigmoid_gate = jax.nn.sigmoid(pre_gate)
    activation = pre_gate * sigmoid_gate
    pair_dots = jnp.sum(hidden_grad * activation * pre_up, axis=-1).astype(jnp.bfloat16)
    gate_grad = (
        hidden_grad * pre_up * sigmoid_gate * (1.0 + pre_gate * (1.0 - sigmoid_gate))
    ).astype(jnp.bfloat16)
    up_grad = (hidden_grad * activation).astype(jnp.bfloat16)
    returned_dots = exchange(pair_dots)
    pair_rows = jnp.einsum(
        "esf,df->esd", gate_grad, w_gate, preferred_element_type=jnp.float32
    ) + jnp.einsum("esf,df->esd", up_grad, w_up, preferred_element_type=jnp.float32)
    returned_rows = exchange(pair_rows.astype(jnp.bfloat16))

    slot_dots = returned_dots.astype(jnp.float32)
    weight_grad = jnp.sum(
        jnp.where(
            slot_index[:, :, None, None] == slot_ids[None, None, :, :],
            slot_dots[None, None, :, :],
            0.0,
        ),
        axis=(2, 3),
    )
    center = jnp.sum(route_weight * weight_grad, axis=1, keepdims=True)
    logit_grad = route_weight * (weight_grad - center)
    matches = picks[:, :, None] == jnp.arange(every_expert, dtype=jnp.int32)[None, None, :]
    dense_grad = jnp.sum(jnp.where(matches, logit_grad[:, :, None], 0.0), axis=1)
    router_grad = jnp.zeros((token_count, width_model), jnp.float32)
    for part in split_bf16(dense_grad, 3):
        router_grad = router_grad + lax.dot_general(
            part, w_router, (((1,), (1,)), ((), ())), preferred_element_type=jnp.float32
        )
    expert_sum = jnp.zeros((token_count, width_model), jnp.float32)
    for part in split_bf16(combine, 2):
        expert_sum = expert_sum + jnp.einsum(
            "tes,esd->td", part, returned_rows, preferred_element_type=jnp.float32
        )
    grad_in = (incoming.astype(jnp.float32) + expert_sum + router_grad).astype(jnp.bfloat16)
    return (grad_in[None], logit_grad[None])


def solution(mesh):
    in_specs = (
        P("section", "expert", None),
        P("section", "expert", None),
        P("section", "expert", None),
        P("section", "expert", None),
        P("section", "expert", None, None),
        P("section", "expert", None, None),
        P("section", "expert", None, None),
        P("section", None, None),
    )
    out_specs = (P("section", "expert", None), P("section", "expert", None))
    return jax.shard_map(
        per_device, mesh=mesh, in_specs=in_specs, out_specs=out_specs, check_vma=False
    )
```

time: 419 us -> 320 us (0.76)
  local copies, waits for them, and re-layouts: 38.5 us -> 2.02 us
  waiting for transfers between devices: 258 us -> 225 us
  starting transfers between devices: 45.6 us -> 33.9 us
  matrix products: 62.7 us -> 52.9 us
    all_to_all x6 -> x4, waiting for transfers between devices: 244 us -> 139 us  [exchange(): lax.all_to_all(block, 'expert', split_axis=0, concat_axis=0, tiled=True)]
    ppermute x1, waiting for transfers between devices: 14.3 us -> 86.3 us  [from_behind(): lax.ppermute(shard, axis, [(i, (i + by) % size) for i in range(size)])]
    reshape x8 -> x0, local copies, waits for them, and re-layouts: 31.5 us -> none  [the longest x2 11.2 us: per_device(): got = got.reshape(-1, 2 * width_model)]
    all_to_all x6 -> x4, starting transfers between devices: 45.5 us -> 33.1 us  [exchange(): lax.all_to_all(block, 'expert', split_axis=0, concat_axis=0, tiled=True)]
    dot_general x16 -> x9, matrix products: 60.3 us -> 48.5 us  [the longest x2 9.36 us: per_device(): jnp.einsum('tes,esd->td', part, returned_rows, preferred_element_type=jnp...]
  transfers between devices with their start and end apart: 7 -> 5, of which waited for: 7 -> 4; matrix products, arithmetic and copies ran while one was open for 18% -> 7% of each run, Pallas kernels for 0% -> 0%
where the time goes in v2:
time: 320 us
  waiting for transfers between devices  225 us (70%)
  matrix products  52.9 us (17%)
  starting transfers between devices  33.9 us (11%)
  other arithmetic  4.84 us (2%)
    all_to_all x4, waiting for transfers between devices, exchange(): lax.all_to_all(block, 'expert', split_axis=0, concat_axis=0, tiled=True)  139 us
    ppermute x1, waiting for transfers between devices, from_behind(): lax.ppermute(shard, axis, [(i, (i + by) % size) for i in range(size)])  86.3 us
    all_to_all x4, starting transfers between devices, exchange(): lax.all_to_all(block, 'expert', split_axis=0, concat_axis=0, tiled=True)  33.1 us
    dot_general x2, matrix products, per_device(): jnp.einsum('tes,esd->td', part, returned_rows, preferred_element_type=jnp...  9.36 us
    dot_general x1, matrix products, per_device(): jnp.einsum('esf,df->esd', up_grad, w_up, preferred_element_type=jnp.float32)  7.67 us
    dot_general x2, matrix products, pack_rows(): jnp.einsum('est,td->esd', pack, rows, preferred_element_type=jnp.float32)  7.56 us
    dot_general x1, matrix products, per_device(): jnp.einsum('esd,df->esf', inputs, w_gate, preferred_element_type=jnp.floa...  6.88 us
  transfers between devices with their start and end apart: 5, of which 4 were waited for; matrix products, arithmetic and copies ran while one was open for 7% of the time, Pallas kernels for 0%

profile of v2, /device:TPU:33, one launch (start us, length us, event | category | flops | bytes accessed | tf_op | source)
XLA Modules:
  0.0 319.6 jit_solution(6902646969691046068)
XLA Ops:
  0.7 0.9 convert_reduce_fusion
  1.5 0.1 convolution_convert_fusion.2
  1.7 0.8 select_reduce_fusion.2
  2.5 0.7 add_select_fusion
  3.2 4.4 %convolution_convert_fusion = bf16[32,24,2048]{2,1,0:T(8,128)(2,1)} fusion(bf16[1,192,2048]{2,1,0:T(8,128)(2,1)} %param.9, s32[192]{0:T(256)S(1)} %bitcast.89, s32[192]{0:T(256)S(1)} %bitcast.93, s32[192]{0:T(256)S(1)} %bitcast.97, s32[192]{0:T(256)S(1)} %bitcast.101, s32[192]{0:T(256)S(1)} %bitcast.105, s32[192]{0:T(256)S(1)} %bitcast.109, ...), kind=kOutput, calls=%fused_computation.2 | convolution fusion | flops 609091584 | bytes 3941376 | tf_op jit(solution)/shard_map/est,td->esd/dot_general | solution.py:63
  7.6 11.1 %all-to-all-start.1 = ((bf16[32,24,2048]{2,1,0:T(8,128)(2,1)}), bf16[32,24,2048]{2,1,0:T(8,128)(2,1)}, u32[]{:S(2)}, u32[]{:S(2)}) async-start(bf16[32,24,2048]{2,1,0:T(8,128)(2,1)} %convolution_convert_fusion), calls=%async_computation.1 | async-start | bytes 6291456 | tf_op jit(solution)/shard_map/all_to_all | solution.py:67
  18.6 0.8 collective-permute-start
  19.4 86.3 %collective-permute-done = bf16[1,192,2048]{2,1,0:T(8,128)(2,1)S(1)} collective-permute-done((bf16[1,192,2048]{2,1,0:T(8,128)(2,1)}, bf16[1,192,2048]{2,1,0:T(8,128)(2,1)S(1)}, u32[]{:S(2)}, u32[]{:S(2)}) %collective-permute-start) | collective-permute-done | bytes 786464 | tf_op jit(solution)/shard_map/ppermute | solution.py:9
  105.7 0.9 copy-done.4
  106.6 3.2 convolution_convert_fusion.1
  109.8 9.7 %all-to-all-start = ((bf16[32,24,2048]{2,1,0:T(8,128)(2,1)}), bf16[32,24,2048]{2,1,0:T(8,128)(2,1)}, u32[]{:S(2)}, u32[]{:S(2)}) async-start(bf16[32,24,2048]{2,1,0:T(8,128)(2,1)} %convolution_convert_fusion.1), calls=%async_computation | async-start | bytes 6291456 | tf_op jit(solution)/shard_map/all_to_all | solution.py:67
  119.5 6.9 %fusion.2 = f32[32,24,768]{2,1,0:T(8,128)} fusion(bf16[32,24,2048]{2,1,0:T(8,128)(2,1)} %all-to-all-done.1, bf16[1,1,2048,768]{3,2,1,0:T(8,128)(2,1)} %param.12), kind=kOutput, calls=%fused_computation.6 | convolution fusion | flops 2415919104 | bytes 8650752 | tf_op jit(solution)/shard_map/esd,df->esf/dot_general | solution.py:71
  126.3 68.7 %all-to-all-done = bf16[32,24,2048]{2,1,0:T(8,128)(2,1)} async-done(((bf16[32,24,2048]{2,1,0:T(8,128)(2,1)}), bf16[32,24,2048]{2,1,0:T(8,128)(2,1)}, u32[]{:S(2)}, u32[]{:S(2)}) %all-to-all-start) | async-done | bytes 3145760 | tf_op jit(solution)/shard_map/all_to_all | solution.py:67
  195.1 5.6 %fusion.4 = f32[32,24,768]{2,1,0:T(8,128)S(1)} fusion(bf16[32,24,2048]{2,1,0:T(8,128)(2,1)} %all-to-all-done, bf16[1,1,768,2048]{3,2,1,0:T(8,128)(2,1)} %param.14), kind=kOutput, calls=%fused_computation.8 | convolution fusion | flops 2415919104 | bytes 8650752 | tf_op jit(solution)/shard_map/esd,fd->esf/dot_general | solution.py:73
  200.8 5.8 %multiply_reduce_fusion = (bf16[32,24]{1,0:T(8,128)(2,1)S(1)}, f32[32,24,768]{2,1,0:T(8,128)S(1)}) fusion(f32[32,24,768]{2,1,0:T(8,128)S(1)} %fusion.4, f32[32,24,768]{2,1,0:T(8,128)S(1)} %copy-done.9, bf16[32,24,2048]{2,1,0:T(8,128)(2,1)} %all-to-all-done.1, bf16[1,1,2048,768]{3,2,1,0:T(8,128)(2,1)S(1)} %copy-done), kind=kOutput, calls=%fused_computation.22 | convolution fusion | flops 2420047104 | bytes 13370880 | tf_op jit(solution)/shard_map/esd,df->esf/dot_general | solution.py:72
  206.6 5.6 %fusion = f32[32,24,2048]{2,1,0:T(8,128)} fusion(bf16[1,1,2048,768]{3,2,1,0:T(8,128)(2,1)S(1)} %copy-done.8, f32[32,24,768]{2,1,0:T(8,128)S(1)} %copy-done.9, f32[32,24,768]{2,1,0:T(8,128)S(1)} %fusion.4, f32[32,24,768]{2,1,0:T(8,128)S(1)} %get-tuple-element.21), kind=kOutput, calls=%fused_computation.4 | convolution fusion | flops 2421817344 | bytes 16515072 | tf_op jit(solution)/shard_map/esf,df->esd/dot_general | solution.py:82
  212.3 0.7 copy.61
  213.0 4.1 %all-to-all-start.3 = ((bf16[32,1,24]{2,1,0:T(2,128)(2,1)}), bf16[32,1,24]{2,1,0:T(2,128)(2,1)S(1)}, u32[]{:S(2)}, u32[]{:S(2)}) async-start(bf16[32,1,24]{2,1,0:T(2,128)(2,1)} %copy.61), calls=%async_computation.3 | async-start | bytes 32768 | tf_op jit(solution)/shard_map/all_to_all | solution.py:67
  217.1 7.7 %add_convert_fusion = bf16[32,24,2048]{2,1,0:T(8,128)(2,1)} fusion(f32[32,24,2048]{2,1,0:T(8,128)} %fusion, bf16[1,1,2048,768]{3,2,1,0:T(8,128)(2,1)S(1)} %copy-done, f32[32,24,768]{2,1,0:T(8,128)} %copy-done.10, f32[32,24,768]{2,1,0:T(8,128)} %fusion.2), kind=kOutput, calls=%fused_computation.1 | convolution fusion | flops 2422603776 | bytes 17301504 | tf_op jit(solution)/shard_map/esf,df->esd/dot_general | solution.py:84
  224.8 1.7 all-to-all-done.3
  226.4 8.3 %all-to-all-start.2 = ((bf16[32,24,2048]{2,1,0:T(8,128)(2,1)}), bf16[32,24,2048]{2,1,0:T(8,128)(2,1)}, u32[]{:S(2)}, u32[]{:S(2)}) async-start(bf16[32,24,2048]{2,1,0:T(8,128)(2,1)} %add_convert_fusion), calls=%async_computation.2 | async-start | bytes 6291456 | tf_op jit(solution)/shard_map/all_to_all | solution.py:67
  234.8 0.1 copy.59
  235.0 0.8 select_reduce_fusion
  235.8 0.1 copy.62
  235.9 1.0 select_reduce_fusion.1
  237.0 0.6 fusion.38
  237.6 1.4 fusion.29
  239.0 1.5 convolution_add_fusion.1
  240.5 68.4 %all-to-all-done.2 = bf16[32,24,2048]{2,1,0:T(8,128)(2,1)} async-done(((bf16[32,24,2048]{2,1,0:T(8,128)(2,1)}), bf16[32,24,2048]{2,1,0:T(8,128)(2,1)}, u32[]{:S(2)}, u32[]{:S(2)}) %all-to-all-start.2) | async-done | bytes 3145760 | tf_op jit(solution)/shard_map/all_to_all | solution.py:67
  308.9 4.6 %fusion.13 = f32[192,2048]{1,0:T(8,128)S(1)} fusion(bf16[32,24,2048]{2,1,0:T(8,128)(2,1)} %all-to-all-done.2, f32[192]{0:T(256)S(1)} %bitcast.119, s32[192]{0:T(256)S(1)} %bitcast.91, f32[192]{0:T(256)S(1)} %bitcast.121, s32[192]{0:T(256)S(1)} %bitcast.95, f32[192]{0:T(256)S(1)} %bitcast.123, s32[192]{0:T(256)S(1)} %bitcast.99, f32[192]{0:T(256)S(1)} %bitcast.125, ...), kind=kOutput, calls=%fused_computation.17 | convolution fusion | flops 607518720 | bytes 4733952 | tf_op jit(solution)/shard_map/tes,esd->td/dot_general | solution.py:107
  313.5 4.8 %fusion.19 = f32[192,2048]{1,0:T(8,128)S(1)} fusion(f32[192,2048]{1,0:T(8,128)S(1)} %fusion.13, bf16[32,24,2048]{2,1,0:T(8,128)(2,1)} %all-to-all-done.2, f32[192]{0:T(256)S(1)} %bitcast.120, s32[192]{0:T(256)S(1)} %bitcast.92, f32[192]{0:T(256)S(1)} %bitcast.122, s32[192]{0:T(256)S(1)} %bitcast.96, f32[192]{0:T(256)S(1)} %bitcast.124, ...), kind=kOutput, calls=%fused_computation.21 | convolution fusion | flops 608354304 | bytes 6306816 | tf_op jit(solution)/shard_map/tes,esd->td/dot_general | solution.py:107
  318.3 1.3 fusion.24
  (31 shorter events, 0.3 us)
Async XLA Ops:
  0.6 200.1 %copy-start = (bf16[1,1,2048,768]{3,2,1,0:T(8,128)(2,1)S(1)}, bf16[1,1,2048,768]{3,2,1,0:T(8,128)(2,1)}, u32[]{:S(2)}) copy-start(bf16[1,1,2048,768]{3,2,1,0:T(8,128)(2,1)} %param.13) | copy-start | bytes 9437188
  7.6 102.2 %all-to-all-start.1 = ((bf16[32,24,2048]{2,1,0:T(8,128)(2,1)}), bf16[32,24,2048]{2,1,0:T(8,128)(2,1)}, u32[]{:S(2)}, u32[]{:S(2)}) async-start(bf16[32,24,2048]{2,1,0:T(8,128)(2,1)} %convolution_convert_fusion), calls=%async_computation.1 | async-start | bytes 6291456 | tf_op jit(solution)/shard_map/all_to_all | solution.py:67
  18.6 87.1 %collective-permute-start = (bf16[1,192,2048]{2,1,0:T(8,128)(2,1)}, bf16[1,192,2048]{2,1,0:T(8,128)(2,1)S(1)}, u32[]{:S(2)}, u32[]{:S(2)}) collective-permute-start(bf16[1,192,2048]{2,1,0:T(8,128)(2,1)} %param.8), channel_id=1, source_target_pairs={{0,224},{32,0},{64,32},{96,64},{128,96},{160,128},{192,160},{224,1... | collective-permute-start | bytes 2359304 | tf_op jit(solution)/shard_map/ppermute | solution.py:9
  105.7 0.9 copy-start.4
  109.8 85.3 %all-to-all-start = ((bf16[32,24,2048]{2,1,0:T(8,128)(2,1)}), bf16[32,24,2048]{2,1,0:T(8,128)(2,1)}, u32[]{:S(2)}, u32[]{:S(2)}) async-start(bf16[32,24,2048]{2,1,0:T(8,128)(2,1)} %convolution_convert_fusion.1), calls=%async_computation | async-start | bytes 6291456 | tf_op jit(solution)/shard_map/all_to_all | solution.py:67
  195.1 5.6 %copy-start.9 = (f32[32,24,768]{2,1,0:T(8,128)S(1)}, f32[32,24,768]{2,1,0:T(8,128)}, u32[]{:S(2)}) copy-start(f32[32,24,768]{2,1,0:T(8,128)} %fusion.2) | copy-start | bytes 7077892
  200.7 5.8 %copy-start.10 = (f32[32,24,768]{2,1,0:T(8,128)}, f32[32,24,768]{2,1,0:T(8,128)S(1)}, u32[]{:S(2)}) copy-start(f32[32,24,768]{2,1,0:T(8,128)S(1)} %fusion.4) | copy-start | bytes 7077892
  200.7 5.8 %copy-start.8 = (bf16[1,1,2048,768]{3,2,1,0:T(8,128)(2,1)S(1)}, bf16[1,1,2048,768]{3,2,1,0:T(8,128)(2,1)}, u32[]{:S(2)}) copy-start(bf16[1,1,2048,768]{3,2,1,0:T(8,128)(2,1)} %param.12) | copy-start | bytes 9437188
  213.0 13.4 %all-to-all-start.3 = ((bf16[32,1,24]{2,1,0:T(2,128)(2,1)}), bf16[32,1,24]{2,1,0:T(2,128)(2,1)S(1)}, u32[]{:S(2)}, u32[]{:S(2)}) async-start(bf16[32,1,24]{2,1,0:T(2,128)(2,1)} %copy.61), calls=%async_computation.3 | async-start | bytes 32768 | tf_op jit(solution)/shard_map/all_to_all | solution.py:67
  224.8 10.0 %copy-start.6 = (s32[1,192,8]{1,2,0:T(8,128)S(1)}, s32[1,192,8]{1,2,0:T(8,128)}, u32[]{:S(2)}) copy-start(s32[1,192,8]{1,2,0:T(8,128)} %param.10) | copy-start | bytes 18436
  224.8 10.2 %copy-start.7 = (f32[1,192,8]{1,2,0:T(8,128)S(1)}, f32[1,192,8]{1,2,0:T(8,128)}, u32[]{:S(2)}) copy-start(f32[1,192,8]{1,2,0:T(8,128)} %param.11) | copy-start | bytes 18436
  226.4 82.4 %all-to-all-start.2 = ((bf16[32,24,2048]{2,1,0:T(8,128)(2,1)}), bf16[32,24,2048]{2,1,0:T(8,128)(2,1)}, u32[]{:S(2)}, u32[]{:S(2)}) async-start(bf16[32,24,2048]{2,1,0:T(8,128)(2,1)} %add_convert_fusion), calls=%async_computation.2 | async-start | bytes 6291456 | tf_op jit(solution)/shard_map/all_to_all | solution.py:67
  235.9 3.0 copy-start.2
  313.5 4.8 %copy-start.1 = (f32[192,2048]{1,0:T(8,128)S(1)}, f32[192,2048]{1,0:T(8,128)}, u32[]{:S(2)}) copy-start(f32[192,2048]{1,0:T(8,128)} %convolution_add_fusion.1) | copy-start | bytes 4718596
  313.5 4.8 %copy-start.3 = (bf16[1,2048,128]{2,1,0:T(8,128)(2,1)S(1)}, bf16[1,2048,128]{2,1,0:T(8,128)(2,1)}, u32[]{:S(2)}) copy-start(bf16[1,2048,128]{2,1,0:T(8,128)(2,1)} %param.15) | copy-start | bytes 1572868
  313.5 4.8 %copy-start.5 = (bf16[1,192,2048]{2,1,0:T(8,128)(2,1)S(1)}, bf16[1,192,2048]{2,1,0:T(8,128)(2,1)}, u32[]{:S(2)}) copy-start(bf16[1,192,2048]{2,1,0:T(8,128)(2,1)} %copy-done.4) | copy-start | bytes 2359300

commit v3 on v2

--- a/solution.py
+++ b/solution.py
@@ -78,11 +78,16 @@
         hidden_grad * pre_up * sigmoid_gate * (1.0 + pre_gate * (1.0 - sigmoid_gate))
     ).astype(jnp.bfloat16)
     up_grad = (hidden_grad * activation).astype(jnp.bfloat16)
-    returned_dots = exchange(pair_dots)
     pair_rows = jnp.einsum(
         "esf,df->esd", gate_grad, w_gate, preferred_element_type=jnp.float32
     ) + jnp.einsum("esf,df->esd", up_grad, w_up, preferred_element_type=jnp.float32)
-    returned_rows = exchange(pair_rows.astype(jnp.bfloat16))
+    lanes = 128
+    dot_lanes = jnp.where(
+        jnp.arange(lanes, dtype=jnp.int32)[None, None, :] == 0, pair_dots[:, :, None], 0.0
+    ).astype(jnp.bfloat16)
+    returned = exchange(jnp.concatenate([pair_rows.astype(jnp.bfloat16), dot_lanes], axis=2))
+    returned_rows = returned[:, :, :width_model]
+    returned_dots = returned[:, :, width_model]
 
     slot_dots = returned_dots.astype(jnp.float32)
     weight_grad = jnp.sum(
@@ -102,11 +107,11 @@
         router_grad = router_grad + lax.dot_general(
             part, w_router, (((1,), (1,)), ((), ())), preferred_element_type=jnp.float32
         )
-    expert_sum = jnp.zeros((token_count, width_model), jnp.float32)
-    for part in split_bf16(combine, 2):
-        expert_sum = expert_sum + jnp.einsum(
-            "tes,esd->td", part, returned_rows, preferred_element_type=jnp.float32
-        )
+    combine_parts = jnp.stack(split_bf16(combine, 2))
+    expert_sum = jnp.sum(
+        jnp.einsum("ptes,esd->ptd", combine_parts, returned_rows, preferred_element_type=jnp.float32),
+        axis=0,
+    )
     grad_in = (incoming.astype(jnp.float32) + expert_sum + router_grad).astype(jnp.bfloat16)
     return (grad_in[None], logit_grad[None])
 

time: 320 us -> 310 us (0.969)
  matrix products: 52.9 us -> 37.3 us
  waiting for transfers between devices: 225 us -> 233 us
  starting transfers between devices: 33.9 us -> 26.5 us
    all_to_all x4 -> x3, waiting for transfers between devices: 139 us -> 146 us  [exchange(): lax.all_to_all(block, 'expert', split_axis=0, concat_axis=0, tiled=True)]
    all_to_all x4 -> x3, starting transfers between devices: 33.1 us -> 25.7 us  [exchange(): lax.all_to_all(block, 'expert', split_axis=0, concat_axis=0, tiled=True)]
    dot_general x2 -> x1, matrix products: 9.36 us -> 2.49 us  [per_device(): jnp.einsum('ptes,esd->ptd', combine_parts, returned_rows, preferred_eleme...]
    dot_general x1, matrix products: 7.67 us -> 3.02 us  [per_device(): jnp.einsum('esf,df->esd', up_grad, w_up, preferred_element_type=jnp.float32)]
    slice x0 -> x2, local copies, waits for them, and re-layouts: none -> 3.24 us  [the longest x1 2.29 us: per_device(): returned_rows = returned[:, :, :width_model]]
  transfers between devices with their start and end apart: 5 -> 4, of which waited for: 4 -> 3; matrix products, arithmetic and copies ran while one was open for 7% -> 3% of each run, Pallas kernels for 0% -> 0%
where the time goes in v3:
time: 310 us
  waiting for transfers between devices  233 us (75%)
  matrix products  37.3 us (12%)
  starting transfers between devices  26.5 us (9%)
  other arithmetic  7.74 us (2%)
  local copies, waits for them, and re-layouts  4.78 us (2%)
    all_to_all x3, waiting for transfers between devices, exchange(): lax.all_to_all(block, 'expert', split_axis=0, concat_axis=0, tiled=True)  146 us
    ppermute x1, waiting for transfers between devices, from_behind(): lax.ppermute(shard, axis, [(i, (i + by) % size) for i in range(size)])  86.3 us
    all_to_all x3, starting transfers between devices, exchange(): lax.all_to_all(block, 'expert', split_axis=0, concat_axis=0, tiled=True)  25.7 us
    dot_general x2, matrix products, pack_rows(): jnp.einsum('est,td->esd', pack, rows, preferred_element_type=jnp.float32)  7.6 us
    dot_general x1, matrix products, per_device(): jnp.einsum('esd,df->esf', inputs, w_gate, preferred_element_type=jnp.floa...  6.86 us
  transfers between devices with their start and end apart: 4, of which 3 were waited for; matrix products, arithmetic and copies ran while one was open for 3% of the time, Pallas kernels for 0%

profile of v3, /device:TPU:33, one launch (start us, length us, event | category | flops | bytes accessed | tf_op | source)
XLA Modules:
  0.0 309.8 jit_solution(12758974458772379764)
XLA Ops:
  0.7 0.9 convert_reduce_fusion
  1.5 0.1 convolution_convert_fusion.2
  1.7 0.8 select_reduce_fusion.2
  2.5 0.7 add_select_fusion
  3.3 4.4 %convolution_convert_fusion = bf16[32,24,2048]{2,1,0:T(8,128)(2,1)} fusion(bf16[1,192,2048]{2,1,0:T(8,128)(2,1)} %param.9, s32[192]{0:T(256)S(1)} %bitcast.87, s32[192]{0:T(256)S(1)} %bitcast.90, s32[192]{0:T(256)S(1)} %bitcast.93, s32[192]{0:T(256)S(1)} %bitcast.96, s32[192]{0:T(256)S(1)} %bitcast.99, s32[192]{0:T(256)S(1)} %bitcast.102, ...), kind=kOutput, calls=%fused_computation.2 | convolution fusion | flops 609091584 | bytes 3941376 | tf_op jit(solution)/shard_map/est,td->esd/dot_general | solution.py:63
  7.6 11.1 %all-to-all-start.1 = ((bf16[32,24,2048]{2,1,0:T(8,128)(2,1)}), bf16[32,24,2048]{2,1,0:T(8,128)(2,1)}, u32[]{:S(2)}, u32[]{:S(2)}) async-start(bf16[32,24,2048]{2,1,0:T(8,128)(2,1)} %convolution_convert_fusion), calls=%async_computation.1 | async-start | bytes 6291456 | tf_op jit(solution)/shard_map/all_to_all | solution.py:67
  18.7 0.8 collective-permute-start
  19.5 86.3 %collective-permute-done = bf16[1,192,2048]{2,1,0:T(8,128)(2,1)S(1)} collective-permute-done((bf16[1,192,2048]{2,1,0:T(8,128)(2,1)}, bf16[1,192,2048]{2,1,0:T(8,128)(2,1)S(1)}, u32[]{:S(2)}, u32[]{:S(2)}) %collective-permute-start) | collective-permute-done | bytes 786464 | tf_op jit(solution)/shard_map/ppermute | solution.py:9
  105.8 0.9 copy-done.2
  106.7 3.2 %convolution_convert_fusion.1 = bf16[32,24,2048]{2,1,0:T(8,128)(2,1)} fusion(bf16[1,192,2048]{2,1,0:T(8,128)(2,1)S(1)} %collective-permute-done, s32[192]{0:T(256)S(1)} %bitcast.88, s32[192]{0:T(256)S(1)} %bitcast.91, s32[192]{0:T(256)S(1)} %bitcast.94, s32[192]{0:T(256)S(1)} %bitcast.97, s32[192]{0:T(256)S(1)} %bitcast.100, s32[192]{0:T(256)S(1)} %bitcast.103, ...), kind=kOutput, calls=%fused_computation.3 | convolution fusion | flops 609091584 | bytes 3941376 | tf_op jit(solution)/shard_map/est,td->esd/dot_general | solution.py:63
  109.9 9.7 %all-to-all-start = ((bf16[32,24,2048]{2,1,0:T(8,128)(2,1)}), bf16[32,24,2048]{2,1,0:T(8,128)(2,1)}, u32[]{:S(2)}, u32[]{:S(2)}) async-start(bf16[32,24,2048]{2,1,0:T(8,128)(2,1)} %convolution_convert_fusion.1), calls=%async_computation | async-start | bytes 6291456 | tf_op jit(solution)/shard_map/all_to_all | solution.py:67
  119.6 6.9 %fusion.3 = f32[32,24,768]{2,1,0:T(8,128)} fusion(bf16[32,24,2048]{2,1,0:T(8,128)(2,1)} %all-to-all-done.1, bf16[1,1,2048,768]{3,2,1,0:T(8,128)(2,1)} %param.12), kind=kOutput, calls=%fused_computation.9 | convolution fusion | flops 2415919104 | bytes 8650752 | tf_op jit(solution)/shard_map/esd,df->esf/dot_general | solution.py:71
  126.4 68.7 %all-to-all-done = bf16[32,24,2048]{2,1,0:T(8,128)(2,1)} async-done(((bf16[32,24,2048]{2,1,0:T(8,128)(2,1)}), bf16[32,24,2048]{2,1,0:T(8,128)(2,1)}, u32[]{:S(2)}, u32[]{:S(2)}) %all-to-all-start) | async-done | bytes 3145760 | tf_op jit(solution)/shard_map/all_to_all | solution.py:67
  195.2 5.6 %fusion.5 = f32[32,24,768]{2,1,0:T(8,128)S(1)} fusion(bf16[32,24,2048]{2,1,0:T(8,128)(2,1)} %all-to-all-done, bf16[1,1,768,2048]{3,2,1,0:T(8,128)(2,1)} %param.14), kind=kOutput, calls=%fused_computation.11 | convolution fusion | flops 2415919104 | bytes 8650752 | tf_op jit(solution)/shard_map/esd,fd->esf/dot_general | solution.py:73
  200.9 5.0 %multiply_reduce_fusion = (bf16[32,24]{1,0:T(8,128)(2,1)S(1)}, f32[32,24,768]{2,1,0:T(8,128)S(1)}) fusion(f32[32,24,768]{2,1,0:T(8,128)S(1)} %fusion.5, f32[32,24,768]{2,1,0:T(8,128)S(1)} %copy-done.7, bf16[32,24,2048]{2,1,0:T(8,128)(2,1)} %all-to-all-done.1, bf16[1,1,2048,768]{3,2,1,0:T(8,128)(2,1)S(1)} %copy-done), kind=kOutput, calls=%fused_computation.19 | convolution fusion | flops 2420047104 | bytes 13370880 | tf_op jit(solution)/shard_map/esd,df->esf/dot_general | solution.py:72
  205.9 3.4 %fusion.1 = f32[32,24,2048]{2,1,0:T(8,128)S(1)} fusion(bf16[1,1,2048,768]{3,2,1,0:T(8,128)(2,1)S(1)} %copy-done.6, f32[32,24,768]{2,1,0:T(8,128)S(1)} %copy-done.7, f32[32,24,768]{2,1,0:T(8,128)S(1)} %fusion.5, f32[32,24,768]{2,1,0:T(8,128)S(1)} %get-tuple-element.23), kind=kOutput, calls=%fused_computation.7 | convolution fusion | flops 2421817344 | bytes 16515072 | tf_op jit(solution)/shard_map/esf,df->esd/dot_general | solution.py:81
  209.3 3.0 add_convert_fusion
  212.3 0.2 broadcast_select_fusion
  212.5 2.0 pad_maximum_fusion
  214.6 5.0 %all-to-all-start.2 = ((bf16[32,24,2176]{2,1,0:T(8,128)(2,1)}), bf16[32,24,2176]{2,1,0:T(8,128)(2,1)}, u32[]{:S(2)}, u32[]{:S(2)}) async-start(bf16[32,24,2176]{2,1,0:T(8,128)(2,1)} %pad_maximum_fusion), calls=%async_computation.2 | async-start | bytes 6684672 | tf_op jit(solution)/shard_map/all_to_all | solution.py:67
  219.7 77.6 %all-to-all-done.2 = bf16[32,24,2176]{2,1,0:T(8,128)(2,1)} async-done(((bf16[32,24,2176]{2,1,0:T(8,128)(2,1)}), bf16[32,24,2176]{2,1,0:T(8,128)(2,1)}, u32[]{:S(2)}, u32[]{:S(2)}) %all-to-all-start.2) | async-done | bytes 3342368 | tf_op jit(solution)/shard_map/all_to_all | solution.py:67
  297.3 0.9 slice.89
  298.3 0.2 copy.52
  298.6 0.8 select_reduce_fusion
  299.4 0.6 fusion.29
  300.2 1.0 select_reduce_fusion.1
  301.2 1.4 fusion.20
  302.6 0.4 convolution_add_fusion.1
  303.0 0.7 subtract_convert_fusion
  303.7 2.3 slice.88
  306.0 2.5 bitcast_reduce_fusion
  308.5 1.3 fusion.12
  (28 shorter events, 0.5 us)
Async XLA Ops:
  0.6 200.2 %copy-start = (bf16[1,1,2048,768]{3,2,1,0:T(8,128)(2,1)S(1)}, bf16[1,1,2048,768]{3,2,1,0:T(8,128)(2,1)}, u32[]{:S(2)}) copy-start(bf16[1,1,2048,768]{3,2,1,0:T(8,128)(2,1)} %param.13) | copy-start | bytes 9437188
  7.6 102.3 %all-to-all-start.1 = ((bf16[32,24,2048]{2,1,0:T(8,128)(2,1)}), bf16[32,24,2048]{2,1,0:T(8,128)(2,1)}, u32[]{:S(2)}, u32[]{:S(2)}) async-start(bf16[32,24,2048]{2,1,0:T(8,128)(2,1)} %convolution_convert_fusion), calls=%async_computation.1 | async-start | bytes 6291456 | tf_op jit(solution)/shard_map/all_to_all | solution.py:67
  18.7 87.1 %collective-permute-start = (bf16[1,192,2048]{2,1,0:T(8,128)(2,1)}, bf16[1,192,2048]{2,1,0:T(8,128)(2,1)S(1)}, u32[]{:S(2)}, u32[]{:S(2)}) collective-permute-start(bf16[1,192,2048]{2,1,0:T(8,128)(2,1)} %param.8), channel_id=1, source_target_pairs={{0,224},{32,0},{64,32},{96,64},{128,96},{160,128},{192,160},{224,1... | collective-permute-start | bytes 2359304 | tf_op jit(solution)/shard_map/ppermute | solution.py:9
  105.8 0.9 copy-start.2
  109.9 85.3 %all-to-all-start = ((bf16[32,24,2048]{2,1,0:T(8,128)(2,1)}), bf16[32,24,2048]{2,1,0:T(8,128)(2,1)}, u32[]{:S(2)}, u32[]{:S(2)}) async-start(bf16[32,24,2048]{2,1,0:T(8,128)(2,1)} %convolution_convert_fusion.1), calls=%async_computation | async-start | bytes 6291456 | tf_op jit(solution)/shard_map/all_to_all | solution.py:67
  195.2 5.6 %copy-start.7 = (f32[32,24,768]{2,1,0:T(8,128)S(1)}, f32[32,24,768]{2,1,0:T(8,128)}, u32[]{:S(2)}) copy-start(f32[32,24,768]{2,1,0:T(8,128)} %fusion.3) | copy-start | bytes 7077892
  200.8 5.0 %copy-start.6 = (bf16[1,1,2048,768]{3,2,1,0:T(8,128)(2,1)S(1)}, bf16[1,1,2048,768]{3,2,1,0:T(8,128)(2,1)}, u32[]{:S(2)}) copy-start(bf16[1,1,2048,768]{3,2,1,0:T(8,128)(2,1)} %param.12) | copy-start | bytes 9437188
  214.5 5.0 %copy-start.4 = (s32[1,192,8]{1,2,0:T(8,128)S(1)}, s32[1,192,8]{1,2,0:T(8,128)}, u32[]{:S(2)}) copy-start(s32[1,192,8]{1,2,0:T(8,128)} %param.10) | copy-start | bytes 18436
  214.6 5.1 %copy-start.5 = (f32[1,192,8]{1,2,0:T(8,128)S(1)}, f32[1,192,8]{1,2,0:T(8,128)}, u32[]{:S(2)}) copy-start(f32[1,192,8]{1,2,0:T(8,128)} %param.11) | copy-start | bytes 18436
  214.6 82.8 %all-to-all-start.2 = ((bf16[32,24,2176]{2,1,0:T(8,128)(2,1)}), bf16[32,24,2176]{2,1,0:T(8,128)(2,1)}, u32[]{:S(2)}, u32[]{:S(2)}) async-start(bf16[32,24,2176]{2,1,0:T(8,128)(2,1)} %pad_maximum_fusion), calls=%async_computation.2 | async-start | bytes 6684672 | tf_op jit(solution)/shard_map/all_to_all | solution.py:67
  300.2 2.4 copy-start.1
  306.0 2.5 copy-start.3

commit v4 on v2

--- a/solution.py
+++ b/solution.py
@@ -66,8 +66,14 @@
     def exchange(block):
         return lax.all_to_all(block, "expert", split_axis=0, concat_axis=0, tiled=True)
 
-    inputs = exchange(pack_rows(x_in))
-    grad_rows = exchange(pack_rows(incoming))
+    got = exchange(pack_rows(jnp.concatenate([x_in, incoming], axis=1)))
+    inputs = got[:, :, :width_model]
+    grad_rows = got[:, :, width_model:]
+    lanes = 128
+    wide = width_model + lanes
+    pad_cols = jnp.zeros((lanes, w_gate.shape[1]), w_gate.dtype)
+    w_gate_wide = jnp.concatenate([w_gate, pad_cols], axis=0)
+    w_up_wide = jnp.concatenate([w_up, pad_cols], axis=0)
     pre_gate = jnp.einsum("esd,df->esf", inputs, w_gate, preferred_element_type=jnp.float32)
     pre_up = jnp.einsum("esd,df->esf", inputs, w_up, preferred_element_type=jnp.float32)
     hidden_grad = jnp.einsum("esd,fd->esf", grad_rows, w_down, preferred_element_type=jnp.float32)
@@ -78,11 +84,15 @@
         hidden_grad * pre_up * sigmoid_gate * (1.0 + pre_gate * (1.0 - sigmoid_gate))
     ).astype(jnp.bfloat16)
     up_grad = (hidden_grad * activation).astype(jnp.bfloat16)
-    returned_dots = exchange(pair_dots)
     pair_rows = jnp.einsum(
-        "esf,df->esd", gate_grad, w_gate, preferred_element_type=jnp.float32
-    ) + jnp.einsum("esf,df->esd", up_grad, w_up, preferred_element_type=jnp.float32)
-    returned_rows = exchange(pair_rows.astype(jnp.bfloat16))
+        "esf,df->esd", gate_grad, w_gate_wide, preferred_element_type=jnp.float32
+    ) + jnp.einsum("esf,df->esd", up_grad, w_up_wide, preferred_element_type=jnp.float32)
+    lane_ids = jnp.arange(wide, dtype=jnp.int32)[None, None, :]
+    pair_rows = jnp.where(
+        lane_ids == width_model, pair_dots.astype(jnp.float32)[:, :, None], pair_rows
+    )
+    returned = exchange(pair_rows.astype(jnp.bfloat16))
+    returned_dots = returned[:, :, width_model]
 
     slot_dots = returned_dots.astype(jnp.float32)
     weight_grad = jnp.sum(
@@ -102,11 +112,11 @@
         router_grad = router_grad + lax.dot_general(
             part, w_router, (((1,), (1,)), ((), ())), preferred_element_type=jnp.float32
         )
-    expert_sum = jnp.zeros((token_count, width_model), jnp.float32)
-    for part in split_bf16(combine, 2):
-        expert_sum = expert_sum + jnp.einsum(
-            "tes,esd->td", part, returned_rows, preferred_element_type=jnp.float32
-        )
+    combine_hi, combine_lo = split_bf16(combine, 2)
+    expert_sum = jnp.einsum(
+        "tes,esd->td", combine_hi, returned, preferred_element_type=jnp.float32
+    ) + jnp.einsum("tes,esd->td", combine_lo, returned, preferred_element_type=jnp.float32)
+    expert_sum = expert_sum[:, :width_model]
     grad_in = (incoming.astype(jnp.float32) + expert_sum + router_grad).astype(jnp.bfloat16)
     return (grad_in[None], logit_grad[None])
 

time: 320 us -> 303 us (0.947)
  starting transfers between devices: 33.9 us -> 18.3 us
  matrix products: 52.9 us -> 39 us
  waiting for transfers between devices: 225 us -> 237 us
    all_to_all x4 -> x2, waiting for transfers between devices: 139 us -> 220 us  [exchange(): lax.all_to_all(block, 'expert', split_axis=0, concat_axis=0, tiled=True)]
    ppermute x1, waiting for transfers between devices: 86.3 us -> 17 us  [from_behind(): lax.ppermute(shard, axis, [(i, (i + by) % size) for i in range(size)])]
    all_to_all x4 -> x2, starting transfers between devices: 33.1 us -> 18.2 us  [exchange(): lax.all_to_all(block, 'expert', split_axis=0, concat_axis=0, tiled=True)]
    dot_general x4, matrix products: 22.7 us -> 15.2 us  [the longest x1 4.65 us: per_device(): jnp.einsum('esf,df->esd', up_grad, w_up_wide, preferred_element_type=jnp....]
    dot_general x2 -> x1, matrix products: 7.56 us -> 6.19 us  [pack_rows(): jnp.einsum('est,td->esd', pack, rows, preferred_element_type=jnp.float32)]
  transfers between devices with their start and end apart: 5 -> 3, of which waited for: 4 -> 3; matrix products, arithmetic and copies ran while one was open for 7% -> 1% of each run, Pallas kernels for 0% -> 0%
where the time goes in v4:
time: 303 us
  waiting for transfers between devices  237 us (78%)
  matrix products  39 us (13%)
  starting transfers between devices  18.3 us (6%)
  other arithmetic  4.85 us (2%)
    all_to_all x2, waiting for transfers between devices, exchange(): lax.all_to_all(block, 'expert', split_axis=0, concat_axis=0, tiled=True)  220 us
    all_to_all x2, starting transfers between devices, exchange(): lax.all_to_all(block, 'expert', split_axis=0, concat_axis=0, tiled=True)  18.2 us
    ppermute x1, waiting for transfers between devices, from_behind(): lax.ppermute(shard, axis, [(i, (i + by) % size) for i in range(size)])  17 us
    dot_general x1, matrix products, pack_rows(): jnp.einsum('est,td->esd', pack, rows, preferred_element_type=jnp.float32)  6.19 us
  transfers between devices with their start and end apart: 3, of which 3 were waited for; matrix products, arithmetic and copies ran while one was open for 1% of the time, Pallas kernels for 0%

profile of v4, /device:TPU:33, one launch (start us, length us, event | category | flops | bytes accessed | tf_op | source)
XLA Modules:
  0.0 302.6 jit_solution(16297934571393677309)
XLA Ops:
  0.6 0.0 copy-start
  0.6 0.1 collective-permute-start
  0.7 0.9 convert_reduce_fusion
  1.6 0.1 convolution_convert_fusion.1
  1.8 0.8 select_reduce_fusion.2
  2.6 0.7 add_select_fusion
  3.3 17.0 %collective-permute-done = bf16[1,192,2048]{2,1,0:T(8,128)(2,1)S(1)} collective-permute-done((bf16[1,192,2048]{2,1,0:T(8,128)(2,1)}, bf16[1,192,2048]{2,1,0:T(8,128)(2,1)S(1)}, u32[]{:S(2)}, u32[]{:S(2)}) %collective-permute-start) | collective-permute-done | bytes 786464 | tf_op jit(solution)/shard_map/ppermute | solution.py:9
  20.2 0.9 copy-done.2
  21.1 6.2 %convolution_convert_fusion = bf16[32,24,4096]{2,1,0:T(8,128)(2,1)} fusion(bf16[192,2048]{1,0:T(8,128)(2,1)S(1)} %bitcast.73, bf16[192,2048]{1,0:T(8,128)(2,1)} %bitcast.119, s32[192]{0:T(256)S(1)} %bitcast.80, s32[192]{0:T(256)S(1)} %bitcast.83, s32[192]{0:T(256)S(1)} %bitcast.86, s32[192]{0:T(256)S(1)} %bitcast.89, s32[192]{0:T(256)S(1)} %bitcast.92, ...), kind=kOutput, calls=%fused_computation | convolution fusion | flops 1217789952 | bytes 7873536 | tf_op jit(solution)/shard_map/est,td->esd/dot_general | solution.py:63
  27.3 12.0 %all-to-all-start = ((bf16[32,24,4096]{2,1,0:T(8,128)(2,1)}), bf16[32,24,4096]{2,1,0:T(8,128)(2,1)}, u32[]{:S(2)}, u32[]{:S(2)}) async-start(bf16[32,24,4096]{2,1,0:T(8,128)(2,1)} %convolution_convert_fusion), calls=%async_computation | async-start | bytes 12582912 | tf_op jit(solution)/shard_map/all_to_all | solution.py:67
  39.3 141.4 %all-to-all-done = bf16[32,24,4096]{2,1,0:T(8,128)(2,1)} async-done(((bf16[32,24,4096]{2,1,0:T(8,128)(2,1)}), bf16[32,24,4096]{2,1,0:T(8,128)(2,1)}, u32[]{:S(2)}, u32[]{:S(2)}) %all-to-all-start) | async-done | bytes 6291488 | tf_op jit(solution)/shard_map/all_to_all | solution.py:67
  180.7 4.7 %fusion.5 = f32[32,24,768]{2,1,0:T(8,128)S(1)} fusion(bf16[32,24,4096]{2,1,0:T(8,128)(2,1)} %all-to-all-done, bf16[1,1,768,2048]{3,2,1,0:T(8,128)(2,1)S(1)} %copy-done), kind=kOutput, calls=%fused_computation.10 | convolution fusion | flops 2415919104 | bytes 8650752 | tf_op jit(solution)/shard_map/esd,fd->esf/dot_general | solution.py:79
  185.4 4.7 %fusion.9 = f32[32,24,768]{2,1,0:T(8,128)S(1)} fusion(bf16[1,1,2048,768]{3,2,1,0:T(8,128)(2,1)S(1)} %copy-done.6, bf16[32,24,4096]{2,1,0:T(8,128)(2,1)} %all-to-all-done), kind=kOutput, calls=%fused_computation.14 | convolution fusion | flops 2415919104 | bytes 8650752 | tf_op jit(solution)/shard_map/esd,df->esf/dot_general | solution.py:77
  190.1 5.0 %multiply_reduce_fusion = (bf16[32,24]{1,0:T(8,128)(2,1)S(1)}, f32[32,24,768]{2,1,0:T(8,128)S(1)}) fusion(f32[32,24,768]{2,1,0:T(8,128)S(1)} %fusion.5, f32[32,24,768]{2,1,0:T(8,128)S(1)} %fusion.9, bf16[1,1,2048,768]{3,2,1,0:T(8,128)(2,1)S(1)} %copy-done.7, bf16[32,24,4096]{2,1,0:T(8,128)(2,1)} %all-to-all-done), kind=kOutput, calls=%fused_computation.24 | convolution fusion | flops 2420047104 | bytes 13370880 | tf_op jit(solution)/shard_map/esd,df->esf/dot_general | solution.py:78
  195.1 3.8 %fusion.1 = f32[32,24,2176]{2,1,0:T(8,128)S(1)} fusion(bf16[2048,768]{1,0:T(8,128)(2,1)S(1)} %bitcast.117, f32[32,24,768]{2,1,0:T(8,128)S(1)} %fusion.9, f32[32,24,768]{2,1,0:T(8,128)S(1)} %fusion.5, f32[32,24,768]{2,1,0:T(8,128)S(1)} %get-tuple-element.21), kind=kOutput, calls=%fused_computation.6 | convolution fusion | flops 2572812288 | bytes 16908288 | tf_op jit(solution)/shard_map/esf,df->esd/dot_general | solution.py:87
  198.9 4.7 %select_convert_fusion = bf16[32,24,2176]{2,1,0:T(8,128)(2,1)} fusion(f32[32,24,2176]{2,1,0:T(8,128)S(1)} %fusion.1, bf16[2048,768]{1,0:T(8,128)(2,1)S(1)} %bitcast.118, bf16[32,24]{1,0:T(8,128)(2,1)S(1)} %get-tuple-element.20, pred[2176]{0:T(1024)(128)(4,1)S(1)} %iota_compare_fusion.4, f32[32,24,768]{2,1,0:T(8,128)S(1)} %fusion.5, f32[32,24,768]{2,1,0:T(8,128)S(1)} %fusion.9), kind=kOutput, calls=%fused_computation.1 | convolution fusion | flops 2573795328 | bytes 17895040 | tf_op jit(solution)/shard_map/esf,df->esd/dot_general | solution.py:89
  203.5 6.2 %all-to-all-start.1 = ((bf16[32,24,2176]{2,1,0:T(8,128)(2,1)}), bf16[32,24,2176]{2,1,0:T(8,128)(2,1)}, u32[]{:S(2)}, u32[]{:S(2)}) async-start(bf16[32,24,2176]{2,1,0:T(8,128)(2,1)} %select_convert_fusion), calls=%async_computation.1 | async-start | bytes 6684672 | tf_op jit(solution)/shard_map/all_to_all | solution.py:67
  209.8 0.1 copy.48
  209.9 0.1 copy.45
  210.0 78.8 %all-to-all-done.1 = bf16[32,24,2176]{2,1,0:T(8,128)(2,1)} async-done(((bf16[32,24,2176]{2,1,0:T(8,128)(2,1)}), bf16[32,24,2176]{2,1,0:T(8,128)(2,1)}, u32[]{:S(2)}, u32[]{:S(2)}) %all-to-all-start.1) | async-done | bytes 3342368 | tf_op jit(solution)/shard_map/all_to_all | solution.py:67
  288.8 0.9 slice.100
  289.8 0.2 copy.52
  290.0 0.1 copy.50
  290.1 0.8 select_reduce_fusion
  290.9 0.6 fusion.44
  291.6 0.1 copy.51
  291.7 1.0 select_reduce_fusion.1
  292.7 1.4 fusion.26
  294.1 0.4 convolution_add_fusion.1
  294.5 3.3 %convolution_bitcast_fusion.1 = f32[192,2176]{1,0:T(8,128)S(1)} fusion(bf16[32,24,2176]{2,1,0:T(8,128)(2,1)} %all-to-all-done.1, f32[192]{0:T(256)S(1)} %bitcast.103, s32[192]{0:T(256)S(1)} %bitcast.81, f32[192]{0:T(256)S(1)} %bitcast.105, s32[192]{0:T(256)S(1)} %bitcast.84, f32[192]{0:T(256)S(1)} %bitcast.107, s32[192]{0:T(256)S(1)} %bitcast.87, ...), kind=kOutput, calls=%fused_computation.4 | convolution fusion | flops 645267456 | bytes 5028864 | tf_op jit(solution)/shard_map/tes,esd->td/dot_general | solution.py:116
  297.8 3.4 %convolution_bitcast_fusion = f32[192,2176]{1,0:T(8,128)S(1)} fusion(bf16[32,24,2176]{2,1,0:T(8,128)(2,1)} %all-to-all-done.1, f32[192]{0:T(256)S(1)} %bitcast.104, s32[192]{0:T(256)S(1)} %bitcast.82, f32[192]{0:T(256)S(1)} %bitcast.106, s32[192]{0:T(256)S(1)} %bitcast.85, f32[192]{0:T(256)S(1)} %bitcast.108, s32[192]{0:T(256)S(1)} %bitcast.88, ...), kind=kOutput, calls=%fused_computation.3 | convolution fusion | flops 645709824 | bytes 5028864 | tf_op jit(solution)/shard_map/tes,esd->td/dot_general | solution.py:118
  301.3 1.3 fusion.23
  (22 shorter events, 0.1 us)
Async XLA Ops:
  0.6 180.0 %copy-start = (bf16[1,1,768,2048]{3,2,1,0:T(8,128)(2,1)S(1)}, bf16[1,1,768,2048]{3,2,1,0:T(8,128)(2,1)}, u32[]{:S(2)}) copy-start(bf16[1,1,768,2048]{3,2,1,0:T(8,128)(2,1)} %param.14) | copy-start | bytes 9437188
  0.6 19.6 %collective-permute-start = (bf16[1,192,2048]{2,1,0:T(8,128)(2,1)}, bf16[1,192,2048]{2,1,0:T(8,128)(2,1)S(1)}, u32[]{:S(2)}, u32[]{:S(2)}) collective-permute-start(bf16[1,192,2048]{2,1,0:T(8,128)(2,1)} %param.8), channel_id=1, source_target_pairs={{0,224},{32,0},{64,32},{96,64},{128,96},{160,128},{192,160},{224,1... | collective-permute-start | bytes 2359304 | tf_op jit(solution)/shard_map/ppermute | solution.py:9
  20.2 0.9 copy-start.2
  27.3 153.3 %all-to-all-start = ((bf16[32,24,4096]{2,1,0:T(8,128)(2,1)}), bf16[32,24,4096]{2,1,0:T(8,128)(2,1)}, u32[]{:S(2)}, u32[]{:S(2)}) async-start(bf16[32,24,4096]{2,1,0:T(8,128)(2,1)} %convolution_convert_fusion), calls=%async_computation | async-start | bytes 12582912 | tf_op jit(solution)/shard_map/all_to_all | solution.py:67
  180.7 4.7 %copy-start.6 = (bf16[1,1,2048,768]{3,2,1,0:T(8,128)(2,1)S(1)}, bf16[1,1,2048,768]{3,2,1,0:T(8,128)(2,1)}, u32[]{:S(2)}) copy-start(bf16[1,1,2048,768]{3,2,1,0:T(8,128)(2,1)} %param.12) | copy-start | bytes 9437188
  185.4 4.7 %copy-start.7 = (bf16[1,1,2048,768]{3,2,1,0:T(8,128)(2,1)S(1)}, bf16[1,1,2048,768]{3,2,1,0:T(8,128)(2,1)}, u32[]{:S(2)}) copy-start(bf16[1,1,2048,768]{3,2,1,0:T(8,128)(2,1)} %param.13) | copy-start | bytes 9437188
  203.5 6.2 %copy-start.4 = (s32[1,192,8]{1,2,0:T(8,128)S(1)}, s32[1,192,8]{1,2,0:T(8,128)}, u32[]{:S(2)}) copy-start(s32[1,192,8]{1,2,0:T(8,128)} %param.10) | copy-start | bytes 18436
  203.5 6.4 %copy-start.5 = (f32[1,192,8]{1,2,0:T(8,128)S(1)}, f32[1,192,8]{1,2,0:T(8,128)}, u32[]{:S(2)}) copy-start(f32[1,192,8]{1,2,0:T(8,128)} %param.11) | copy-start | bytes 18436
  203.5 85.3 %all-to-all-start.1 = ((bf16[32,24,2176]{2,1,0:T(8,128)(2,1)}), bf16[32,24,2176]{2,1,0:T(8,128)(2,1)}, u32[]{:S(2)}, u32[]{:S(2)}) async-start(bf16[32,24,2176]{2,1,0:T(8,128)(2,1)} %select_convert_fusion), calls=%async_computation.1 | async-start | bytes 6684672 | tf_op jit(solution)/shard_map/all_to_all | solution.py:67
  291.7 2.4 copy-start.1
  297.8 3.5 %copy-start.3 = (bf16[1,192,2048]{2,1,0:T(8,128)(2,1)S(1)}, bf16[1,192,2048]{2,1,0:T(8,128)(2,1)}, u32[]{:S(2)}) copy-start(bf16[1,192,2048]{2,1,0:T(8,128)(2,1)} %copy-done.2) | copy-start | bytes 2359300

commit v5 on v4

--- a/solution.py
+++ b/solution.py
@@ -22,7 +22,15 @@
 def per_device(
     grad_out, layer_input, routes, route_logits, gate_weight, up_weight, down_weight, router_weight
 ):
-    incoming = from_behind(grad_out, "section", -1)[0]
+    row_blocks = 4 if grad_out.shape[1] % 64 == 0 else 1
+    block_rows = grad_out.shape[1] // row_blocks
+    incoming = jnp.concatenate(
+        [
+            from_behind(grad_out[0, b * block_rows : (b + 1) * block_rows], "section", -1)
+            for b in range(row_blocks)
+        ],
+        axis=0,
+    )
     x_in = layer_input[0]
     token_count, width_model = x_in.shape
     top_count = routes.shape[2]
@@ -74,8 +82,13 @@
     pad_cols = jnp.zeros((lanes, w_gate.shape[1]), w_gate.dtype)
     w_gate_wide = jnp.concatenate([w_gate, pad_cols], axis=0)
     w_up_wide = jnp.concatenate([w_up, pad_cols], axis=0)
-    pre_gate = jnp.einsum("esd,df->esf", inputs, w_gate, preferred_element_type=jnp.float32)
-    pre_up = jnp.einsum("esd,df->esf", inputs, w_up, preferred_element_type=jnp.float32)
+    hidden_count = w_gate.shape[1]
+    pre_both = jnp.einsum(
+        "esd,df->esf", inputs, jnp.concatenate([w_gate, w_up], axis=1),
+        preferred_element_type=jnp.float32,
+    )
+    pre_gate = pre_both[:, :, :hidden_count]
+    pre_up = pre_both[:, :, hidden_count:]
     hidden_grad = jnp.einsum("esd,fd->esf", grad_rows, w_down, preferred_element_type=jnp.float32)
     sigmoid_gate = jax.nn.sigmoid(pre_gate)
     activation = pre_gate * sigmoid_gate
@@ -112,11 +125,11 @@
         router_grad = router_grad + lax.dot_general(
             part, w_router, (((1,), (1,)), ((), ())), preferred_element_type=jnp.float32
         )
-    combine_hi, combine_lo = split_bf16(combine, 2)
-    expert_sum = jnp.einsum(
-        "tes,esd->td", combine_hi, returned, preferred_element_type=jnp.float32
-    ) + jnp.einsum("tes,esd->td", combine_lo, returned, preferred_element_type=jnp.float32)
-    expert_sum = expert_sum[:, :width_model]
+    combine_parts = jnp.stack(split_bf16(combine, 2))
+    expert_both = jnp.einsum(
+        "ptes,esd->ptd", combine_parts, returned, preferred_element_type=jnp.float32
+    )
+    expert_sum = expert_both[0, :, :width_model] + expert_both[1, :, :width_model]
     grad_in = (incoming.astype(jnp.float32) + expert_sum + router_grad).astype(jnp.bfloat16)
     return (grad_in[None], logit_grad[None])
 

time: 303 us -> 304 us (level)
  waiting for transfers between devices: 237 us -> 227 us
  local copies, waits for them, and re-layouts: 2.48 us -> 9.99 us
  starting transfers between devices: 18.3 us -> 22.9 us
    ppermute x1 -> x4, waiting for transfers between devices: 17 us -> 6.68 us  [from_behind(): lax.ppermute(shard, axis, [(i, (i + by) % size) for i in range(size)])]
    ppermute x1 -> x4, starting transfers between devices: 0.08 us -> 5.39 us  [from_behind(): lax.ppermute(shard, axis, [(i, (i + by) % size) for i in range(size)])]
    dot_general x4 -> x2, matrix products: 16.5 us -> 12 us  [the longest x1 8.31 us: per_device(): jnp.einsum('esd,df->esf', inputs, jnp.concatenate([w_gate, w_up], axis=1)...]
  transfers between devices with their start and end apart: 3 -> 6, of which waited for: 3 -> 5; matrix products, arithmetic and copies ran while one was open for 1% -> 3% of each run, Pallas kernels for 0% -> 0%
where the time goes in v5:
time: 304 us; the launch traced here: 303 us
  waiting for transfers between devices  227 us (75%)
  matrix products  36 us (12%)
  starting transfers between devices  22.9 us (8%)
  local copies, waits for them, and re-layouts  9.99 us (3%)
  other arithmetic  5.99 us (2%)
    all_to_all x2, waiting for transfers between devices, exchange(): lax.all_to_all(block, 'expert', split_axis=0, concat_axis=0, tiled=True)  220 us
    all_to_all x2, starting transfers between devices, exchange(): lax.all_to_all(block, 'expert', split_axis=0, concat_axis=0, tiled=True)  17.6 us
    dot_general x1, matrix products, per_device(): jnp.einsum('esd,df->esf', inputs, jnp.concatenate([w_gate, w_up], axis=1)...  8.31 us
    ppermute x4, waiting for transfers between devices, from_behind(): lax.ppermute(shard, axis, [(i, (i + by) % size) for i in range(size)])  6.68 us
    dot_general x1, matrix products, pack_rows(): jnp.einsum('est,td->esd', pack, rows, preferred_element_type=jnp.float32)  6.19 us
  transfers between devices with their start and end apart: 6, of which 5 were waited for; matrix products, arithmetic and copies ran while one was open for 3% of the time, Pallas kernels for 0%

profile of v5, /device:TPU:33, one launch (start us, length us, event | category | flops | bytes accessed | tf_op | source)
XLA Modules:
  0.0 302.8 jit_solution(13029921770467326878)
XLA Ops:
  0.6 2.2 slice_bitcast_fusion
  2.8 3.7 %collective-permute-start.1 = (bf16[48,2048]{1,0:T(8,128)(2,1)}, bf16[48,2048]{1,0:T(8,128)(2,1)}, u32[]{:S(2)}, u32[]{:S(2)}) collective-permute-start(bf16[48,2048]{1,0:T(8,128)(2,1)} %get-tuple-element.7), channel_id=1, source_target_pairs={{0,224},{32,0},{64,32},{96,64},{128,96},{160,128},{192,160},{224,1... | collective-permute-start | bytes 589832 | tf_op jit(solution)/shard_map/ppermute | solution.py:9
  6.5 1.7 collective-permute-start.3
  8.2 0.7 convert_reduce_fusion
  9.1 0.8 select_reduce_fusion.2
  9.9 1.3 add_select_fusion
  11.2 0.7 copy.43
  11.8 1.0 fusion.55
  12.9 0.9 constant_dynamic-update-slice_fusion.3
  14.0 0.9 constant_dynamic-update-slice_fusion.2
  14.9 3.3 %collective-permute-done.2 = bf16[48,2048]{1,0:T(8,128)(2,1)} collective-permute-done((bf16[48,2048]{1,0:T(8,128)(2,1)S(1)}, bf16[48,2048]{1,0:T(8,128)(2,1)}, u32[]{:S(2)}, u32[]{:S(2)}) %collective-permute-start.2) | collective-permute-done | bytes 196640 | tf_op jit(solution)/shard_map/ppermute | solution.py:9
  18.2 0.9 constant_dynamic-update-slice_fusion.1
  19.2 3.3 %collective-permute-done.3 = bf16[48,2048]{1,0:T(8,128)(2,1)} collective-permute-done((bf16[48,2048]{1,0:T(8,128)(2,1)S(1)}, bf16[48,2048]{1,0:T(8,128)(2,1)}, u32[]{:S(2)}, u32[]{:S(2)}) %collective-permute-start.3) | collective-permute-done | bytes 196640 | tf_op jit(solution)/shard_map/ppermute | solution.py:9
  22.4 0.9 constant_dynamic-update-slice_fusion
  23.5 0.8 copy-done.2
  24.3 6.2 %convolution_convert_fusion = bf16[32,24,4096]{2,1,0:T(8,128)(2,1)} fusion(bf16[192,2048]{1,0:T(8,128)(2,1)S(1)} %constant_dynamic-update-slice_fusion, bf16[192,2048]{1,0:T(8,128)(2,1)} %bitcast.117, s32[192]{0:T(256)S(1)} %bitcast.91, s32[192]{0:T(256)S(1)} %bitcast.93, s32[192]{0:T(256)S(1)} %bitcast.95, s32[192]{0:T(256)S(1)} %bitcast.97, ...), kind=kOutput, calls=%fused_computation | convolution fusion | flops 1217789952 | bytes 7873536 | tf_op jit(solution)/shard_map/est,td->esd/dot_general | solution.py:71
  30.4 12.0 %all-to-all-start = ((bf16[32,24,4096]{2,1,0:T(8,128)(2,1)}), bf16[32,24,4096]{2,1,0:T(8,128)(2,1)}, u32[]{:S(2)}, u32[]{:S(2)}) async-start(bf16[32,24,4096]{2,1,0:T(8,128)(2,1)} %convolution_convert_fusion), calls=%async_computation | async-start | bytes 12582912 | tf_op jit(solution)/shard_map/all_to_all | solution.py:75
  42.4 141.6 %all-to-all-done = bf16[32,24,4096]{2,1,0:T(8,128)(2,1)} async-done(((bf16[32,24,4096]{2,1,0:T(8,128)(2,1)}), bf16[32,24,4096]{2,1,0:T(8,128)(2,1)}, u32[]{:S(2)}, u32[]{:S(2)}) %all-to-all-start) | async-done | bytes 6291488 | tf_op jit(solution)/shard_map/all_to_all | solution.py:75
  184.0 8.3 %fusion = f32[32,24,1536]{2,1,0:T(8,128)S(1)} fusion(bf16[2048,768]{1,0:T(8,128)(2,1)} %bitcast.115, bf16[2048,768]{1,0:T(8,128)(2,1)} %bitcast.113, bf16[32,24,4096]{2,1,0:T(8,128)(2,1)} %all-to-all-done), kind=kOutput, calls=%fused_computation.3 | convolution fusion | flops 4844421120 | bytes 14155776 | tf_op jit(solution)/shard_map/esd,df->esf/dot_general | solution.py:86
  192.3 5.1 %multiply_reduce_fusion = (bf16[32,24]{1,0:T(8,128)(2,1)S(1)}, f32[32,24,768]{2,1,0:T(8,128)S(1)}) fusion(f32[32,24,1536]{2,1,0:T(8,128)S(1)} %fusion, bf16[1,1,768,2048]{3,2,1,0:T(8,128)(2,1)S(1)} %copy-done, bf16[32,24,4096]{2,1,0:T(8,128)(2,1)} %all-to-all-done), kind=kOutput, calls=%fused_computation.22 | convolution fusion | flops 2420047104 | bytes 13370880 | tf_op jit(solution)/shard_map/esd,fd->esf/dot_general | solution.py:92
  197.4 3.7 %fusion.5 = f32[32,24,2176]{2,1,0:T(8,128)S(1)} fusion(bf16[2048,768]{1,0:T(8,128)(2,1)S(1)} %bitcast.114, f32[32,24,768]{2,1,0:T(8,128)S(1)} %get-tuple-element.27, f32[32,24,1536]{2,1,0:T(8,128)S(1)} %fusion), kind=kOutput, calls=%fused_computation.10 | convolution fusion | flops 2572812288 | bytes 16908288 | tf_op jit(solution)/shard_map/esf,df->esd/dot_general | solution.py:100
  201.2 4.7 %select_convert_fusion = bf16[32,24,2176]{2,1,0:T(8,128)(2,1)} fusion(f32[32,24,2176]{2,1,0:T(8,128)S(1)} %fusion.5, bf16[2048,768]{1,0:T(8,128)(2,1)S(1)} %bitcast.116, bf16[32,24]{1,0:T(8,128)(2,1)S(1)} %get-tuple-element.26, pred[2176]{0:T(1024)(128)(4,1)S(1)} %iota_compare_fusion.4, f32[32,24,768]{2,1,0:T(8,128)S(1)} %get-tuple-element.27, ...), kind=kOutput, calls=%fused_computation.1 | convolution fusion | flops 2573795328 | bytes 17902592 | tf_op jit(solution)/shard_map/esf,df->esd/dot_general | solution.py:102
  205.9 5.6 %all-to-all-start.1 = ((bf16[32,24,2176]{2,1,0:T(8,128)(2,1)}), bf16[32,24,2176]{2,1,0:T(8,128)(2,1)}, u32[]{:S(2)}, u32[]{:S(2)}) async-start(bf16[32,24,2176]{2,1,0:T(8,128)(2,1)} %select_convert_fusion), calls=%async_computation.1 | async-start | bytes 6684672 | tf_op jit(solution)/shard_map/all_to_all | solution.py:75
  211.7 78.5 %all-to-all-done.1 = bf16[32,24,2176]{2,1,0:T(8,128)(2,1)} async-done(((bf16[32,24,2176]{2,1,0:T(8,128)(2,1)}), bf16[32,24,2176]{2,1,0:T(8,128)(2,1)}, u32[]{:S(2)}, u32[]{:S(2)}) %all-to-all-start.1) | async-done | bytes 3342368 | tf_op jit(solution)/shard_map/all_to_all | solution.py:75
  290.1 0.9 slice.130
  291.4 0.8 select_reduce_fusion
  293.1 1.0 select_reduce_fusion.1
  294.1 1.4 fusion.28
  295.5 1.4 convolution_add_fusion.1
  297.0 0.7 subtract_convert_fusion
  297.7 3.7 %convolution_bitcast_fusion = f32[2,192,2176]{2,1,0:T(8,128)S(1)} fusion(bf16[32,24,2176]{2,1,0:T(8,128)(2,1)} %all-to-all-done.1, bf16[1,192,32,24]{1,2,3,0:T(8,128)(2,1)S(1)} %get-tuple-element.4, bf16[1,192,32,24]{1,2,3,0:T(8,128)(2,1)S(1)} %get-tuple-element.5), kind=kOutput, calls=%fused_computation.7 | convolution fusion | flops 1283751936 | bytes 7274496 | tf_op jit(solution)/shard_map/ptes,esd->ptd/dot_general | solution.py:129
  301.4 1.3 fusion.22
  (64 shorter events, 1.7 us)
Async XLA Ops:
  0.6 191.7 %copy-start = (bf16[1,1,768,2048]{3,2,1,0:T(8,128)(2,1)S(1)}, bf16[1,1,768,2048]{3,2,1,0:T(8,128)(2,1)}, u32[]{:S(2)}) copy-start(bf16[1,1,768,2048]{3,2,1,0:T(8,128)(2,1)} %param.14) | copy-start | bytes 9437188
  2.8 10.1 %collective-permute-start = (bf16[48,2048]{1,0:T(8,128)(2,1)}, bf16[48,2048]{1,0:T(8,128)(2,1)}, u32[]{:S(2)}, u32[]{:S(2)}) collective-permute-start(bf16[48,2048]{1,0:T(8,128)(2,1)} %get-tuple-element.8), channel_id=1, source_target_pairs={{0,224},{32,0},{64,32},{96,64},{128,96},{160,128},{192,160},{224,1... | collective-permute-start | bytes 589832 | tf_op jit(solution)/shard_map/ppermute | solution.py:9
  2.8 11.2 %collective-permute-start.1 = (bf16[48,2048]{1,0:T(8,128)(2,1)}, bf16[48,2048]{1,0:T(8,128)(2,1)}, u32[]{:S(2)}, u32[]{:S(2)}) collective-permute-start(bf16[48,2048]{1,0:T(8,128)(2,1)} %get-tuple-element.7), channel_id=1, source_target_pairs={{0,224},{32,0},{64,32},{96,64},{128,96},{160,128},{192,160},{224,1... | collective-permute-start | bytes 589832 | tf_op jit(solution)/shard_map/ppermute | solution.py:9
  6.5 11.7 %collective-permute-start.2 = (bf16[48,2048]{1,0:T(8,128)(2,1)S(1)}, bf16[48,2048]{1,0:T(8,128)(2,1)}, u32[]{:S(2)}, u32[]{:S(2)}) collective-permute-start(bf16[48,2048]{1,0:T(8,128)(2,1)S(1)} %get-tuple-element.9), channel_id=1, source_target_pairs={{0,224},{32,0},{64,32},{96,64},{128,96},{160,128},{192,160},{224,1... | collective-permute-start | bytes 589832 | tf_op jit(solution)/shard_map/ppermute | solution.py:9
  6.5 15.9 %collective-permute-start.3 = (bf16[48,2048]{1,0:T(8,128)(2,1)S(1)}, bf16[48,2048]{1,0:T(8,128)(2,1)}, u32[]{:S(2)}, u32[]{:S(2)}) collective-permute-start(bf16[48,2048]{1,0:T(8,128)(2,1)S(1)} %get-tuple-element.6), channel_id=1, source_target_pairs={{0,224},{32,0},{64,32},{96,64},{128,96},{160,128},{192,160},{224,1... | collective-permute-start | bytes 589832 | tf_op jit(solution)/shard_map/ppermute | solution.py:9
  12.8 10.5 %copy-start.8 = (s32[192,1]{0,1:T(1,128)}, s32[192,1]{0,1:T(1,128)S(1)}, u32[]{:S(2)}) copy-start(s32[192,1]{0,1:T(1,128)S(1)} %get-tuple-element.19) | copy-start | bytes 2308
  12.8 10.5 %copy-start.10 = (s32[192,1]{0,1:T(1,128)}, s32[192,1]{0,1:T(1,128)S(1)}, u32[]{:S(2)}) copy-start(s32[192,1]{0,1:T(1,128)S(1)} %get-tuple-element.20) | copy-start | bytes 2308
  12.9 10.5 %copy-start.12 = (s32[192,1]{0,1:T(1,128)}, s32[192,1]{0,1:T(1,128)S(1)}, u32[]{:S(2)}) copy-start(s32[192,1]{0,1:T(1,128)S(1)} %get-tuple-element.21) | copy-start | bytes 2308
  12.9 10.5 %copy-start.14 = (s32[192,1]{0,1:T(1,128)}, s32[192,1]{0,1:T(1,128)S(1)}, u32[]{:S(2)}) copy-start(s32[192,1]{0,1:T(1,128)S(1)} %get-tuple-element.22) | copy-start | bytes 2308
  12.9 10.5 %copy-start.16 = (s32[192,1]{0,1:T(1,128)}, s32[192,1]{0,1:T(1,128)S(1)}, u32[]{:S(2)}) copy-start(s32[192,1]{0,1:T(1,128)S(1)} %get-tuple-element.23) | copy-start | bytes 2308
  12.9 10.5 %copy-start.18 = (s32[192,1]{0,1:T(1,128)}, s32[192,1]{0,1:T(1,128)S(1)}, u32[]{:S(2)}) copy-start(s32[192,1]{0,1:T(1,128)S(1)} %get-tuple-element.24) | copy-start | bytes 2308
  12.9 10.5 %copy-start.20 = (s32[192,1]{0,1:T(1,128)}, s32[192,1]{0,1:T(1,128)S(1)}, u32[]{:S(2)}) copy-start(s32[192,1]{0,1:T(1,128)S(1)} %get-tuple-element.25) | copy-start | bytes 2308
  23.4 0.9 copy-start.2
  30.4 153.5 %all-to-all-start = ((bf16[32,24,4096]{2,1,0:T(8,128)(2,1)}), bf16[32,24,4096]{2,1,0:T(8,128)(2,1)}, u32[]{:S(2)}, u32[]{:S(2)}) async-start(bf16[32,24,4096]{2,1,0:T(8,128)(2,1)} %convolution_convert_fusion), calls=%async_computation | async-start | bytes 12582912 | tf_op jit(solution)/shard_map/all_to_all | solution.py:75
  192.3 5.1 %copy-start.22 = (bf16[1,1,2048,768]{3,2,1,0:T(8,128)(2,1)S(1)}, bf16[1,1,2048,768]{3,2,1,0:T(8,128)(2,1)}, u32[]{:S(2)}) copy-start(bf16[1,1,2048,768]{3,2,1,0:T(8,128)(2,1)} %param.12) | copy-start | bytes 9437188
  197.4 3.7 %copy-start.23 = (bf16[1,1,2048,768]{3,2,1,0:T(8,128)(2,1)S(1)}, bf16[1,1,2048,768]{3,2,1,0:T(8,128)(2,1)}, u32[]{:S(2)}) copy-start(bf16[1,1,2048,768]{3,2,1,0:T(8,128)(2,1)} %param.13) | copy-start | bytes 9437188
  205.9 5.6 %copy-start.4 = (s32[1,192,8]{1,2,0:T(8,128)S(1)}, s32[1,192,8]{1,2,0:T(8,128)}, u32[]{:S(2)}) copy-start(s32[1,192,8]{1,2,0:T(8,128)} %param.10) | copy-start | bytes 18436
  205.9 5.7 %copy-start.5 = (f32[1,192,8]{1,2,0:T(8,128)S(1)}, f32[1,192,8]{1,2,0:T(8,128)}, u32[]{:S(2)}) copy-start(f32[1,192,8]{1,2,0:T(8,128)} %param.11) | copy-start | bytes 18436
  205.9 85.5 %copy-start.6 = (s32[192,8]{0,1:T(8,128)S(1)}, s32[192,8]{0,1:T(8,128)}, u32[]{:S(2)}) copy-start(s32[192,8]{0,1:T(8,128)} %add_select_fusion) | copy-start | bytes 18436
  205.9 85.5 %copy-start.7 = (s32[32,24]{1,0:T(8,128)S(1)}, s32[32,24]{1,0:T(8,128)}, u32[]{:S(2)}) copy-start(s32[32,24]{1,0:T(8,128)} %copy.43) | copy-start | bytes 9220
  205.9 84.2 %all-to-all-start.1 = ((bf16[32,24,2176]{2,1,0:T(8,128)(2,1)}), bf16[32,24,2176]{2,1,0:T(8,128)(2,1)}, u32[]{:S(2)}, u32[]{:S(2)}) async-start(bf16[32,24,2176]{2,1,0:T(8,128)(2,1)} %select_convert_fusion), calls=%async_computation.1 | async-start | bytes 6684672 | tf_op jit(solution)/shard_map/all_to_all | solution.py:75
  293.0 3.9 %copy-start.9 = (s32[192,1]{0,1:T(1,128)S(1)}, s32[192,1]{0,1:T(1,128)}, u32[]{:S(2)}) copy-start(s32[192,1]{0,1:T(1,128)} %copy-done.8) | copy-start | bytes 2308
  293.0 3.9 %copy-start.11 = (s32[192,1]{0,1:T(1,128)S(1)}, s32[192,1]{0,1:T(1,128)}, u32[]{:S(2)}) copy-start(s32[192,1]{0,1:T(1,128)} %copy-done.10) | copy-start | bytes 2308
  293.0 3.9 %copy-start.13 = (s32[192,1]{0,1:T(1,128)S(1)}, s32[192,1]{0,1:T(1,128)}, u32[]{:S(2)}) copy-start(s32[192,1]{0,1:T(1,128)} %copy-done.12) | copy-start | bytes 2308
  293.0 3.9 %copy-start.15 = (s32[192,1]{0,1:T(1,128)S(1)}, s32[192,1]{0,1:T(1,128)}, u32[]{:S(2)}) copy-start(s32[192,1]{0,1:T(1,128)} %copy-done.14) | copy-start | bytes 2308
  293.0 3.9 %copy-start.17 = (s32[192,1]{0,1:T(1,128)S(1)}, s32[192,1]{0,1:T(1,128)}, u32[]{:S(2)}) copy-start(s32[192,1]{0,1:T(1,128)} %copy-done.16) | copy-start | bytes 2308
  293.0 3.9 %copy-start.19 = (s32[192,1]{0,1:T(1,128)S(1)}, s32[192,1]{0,1:T(1,128)}, u32[]{:S(2)}) copy-start(s32[192,1]{0,1:T(1,128)} %copy-done.18) | copy-start | bytes 2308
  293.1 3.9 %copy-start.21 = (s32[192,1]{0,1:T(1,128)S(1)}, s32[192,1]{0,1:T(1,128)}, u32[]{:S(2)}) copy-start(s32[192,1]{0,1:T(1,128)} %copy-done.20) | copy-start | bytes 2308
  297.7 3.7 %copy-start.1 = (bf16[1,2048,128]{2,1,0:T(8,128)(2,1)S(1)}, bf16[1,2048,128]{2,1,0:T(8,128)(2,1)}, u32[]{:S(2)}) copy-start(bf16[1,2048,128]{2,1,0:T(8,128)(2,1)} %param.15) | copy-start | bytes 1572868
  297.7 3.7 %copy-start.3 = (bf16[192,2048]{1,0:T(8,128)(2,1)S(1)}, bf16[192,2048]{1,0:T(8,128)(2,1)}, u32[]{:S(2)}) copy-start(bf16[192,2048]{1,0:T(8,128)(2,1)} %copy-done.2) | copy-start | bytes 2359300

commit v6 on v5

--- a/solution.py
+++ b/solution.py
@@ -22,15 +22,7 @@
 def per_device(
     grad_out, layer_input, routes, route_logits, gate_weight, up_weight, down_weight, router_weight
 ):
-    row_blocks = 4 if grad_out.shape[1] % 64 == 0 else 1
-    block_rows = grad_out.shape[1] // row_blocks
-    incoming = jnp.concatenate(
-        [
-            from_behind(grad_out[0, b * block_rows : (b + 1) * block_rows], "section", -1)
-            for b in range(row_blocks)
-        ],
-        axis=0,
-    )
+    incoming = from_behind(grad_out, "section", -1)[0]
     x_in = layer_input[0]
     token_count, width_model = x_in.shape
     top_count = routes.shape[2]

time: 304 us -> 301 us (level)
  waiting for transfers between devices: 227 us -> 238 us
  local copies, waits for them, and re-layouts: 9.99 us -> 1.61 us
  starting transfers between devices: 22.9 us -> 17.6 us
    ppermute x4 -> x1, waiting for transfers between devices: 6.68 us -> 17 us  [from_behind(): lax.ppermute(shard, axis, [(i, (i + by) % size) for i in range(size)])]
    ppermute x4 -> x1, starting transfers between devices: 5.39 us -> 0.08 us  [from_behind(): lax.ppermute(shard, axis, [(i, (i + by) % size) for i in range(size)])]
    unnamed x52 -> x13, local copies, waits for them, and re-layouts: 3.99 us -> 0.29 us
  transfers between devices with their start and end apart: 6 -> 3, of which waited for: 5 -> 3; matrix products, arithmetic and copies ran while one was open for 3% -> 1% of each run, Pallas kernels for 0% -> 0%
where the time goes in v6:
time: 301 us
  waiting for transfers between devices  238 us (79%)
  matrix products  37.3 us (12%)
  starting transfers between devices  17.6 us (6%)
  other arithmetic  5.55 us (2%)
    all_to_all x2, waiting for transfers between devices, exchange(): lax.all_to_all(block, 'expert', split_axis=0, concat_axis=0, tiled=True)  221 us
    all_to_all x2, starting transfers between devices, exchange(): lax.all_to_all(block, 'expert', split_axis=0, concat_axis=0, tiled=True)  17.5 us
    ppermute x1, waiting for transfers between devices, from_behind(): lax.ppermute(shard, axis, [(i, (i + by) % size) for i in range(size)])  17 us
    dot_general x1, matrix products, per_device(): jnp.einsum('esd,df->esf', inputs, jnp.concatenate([w_gate, w_up], axis=1)...  8.31 us
    dot_general x1, matrix products, pack_rows(): jnp.einsum('est,td->esd', pack, rows, preferred_element_type=jnp.float32)  6.42 us
  transfers between devices with their start and end apart: 3, of which 3 were waited for; matrix products, arithmetic and copies ran while one was open for 1% of the time, Pallas kernels for 0%

profile of v6, /device:TPU:33, one launch (start us, length us, event | category | flops | bytes accessed | tf_op | source)
XLA Modules:
  0.0 300.9 jit_solution(1295545480054096077)
XLA Ops:
  0.6 0.0 copy-start
  0.6 0.1 collective-permute-start
  0.7 0.9 convert_reduce_fusion
  1.6 0.1 copy.43
  1.7 0.1 convolution_convert_fusion.1
  1.9 0.8 select_reduce_fusion.2
  2.6 0.7 add_select_fusion
  3.3 17.0 %collective-permute-done = bf16[1,192,2048]{2,1,0:T(8,128)(2,1)} collective-permute-done((bf16[1,192,2048]{2,1,0:T(8,128)(2,1)}, bf16[1,192,2048]{2,1,0:T(8,128)(2,1)}, u32[]{:S(2)}, u32[]{:S(2)}) %collective-permute-start) | collective-permute-done | bytes 786464 | tf_op jit(solution)/shard_map/ppermute | solution.py:9
  20.3 6.4 %convolution_convert_fusion = bf16[32,24,4096]{2,1,0:T(8,128)(2,1)} fusion(bf16[192,2048]{1,0:T(8,128)(2,1)} %bitcast, bf16[192,2048]{1,0:T(8,128)(2,1)} %bitcast.111, s32[192]{0:T(256)S(1)} %bitcast.85, s32[192]{0:T(256)S(1)} %bitcast.87, s32[192]{0:T(256)S(1)} %bitcast.89, s32[192]{0:T(256)S(1)} %bitcast.91, s32[192]{0:T(256)S(1)} %bitcast.93, ...), kind=kOutput, calls=%fused_computation | convolution fusion | flops 1217789952 | bytes 7873536 | tf_op jit(solution)/shard_map/est,td->esd/dot_general | solution.py:63
  26.8 12.0 %all-to-all-start = ((bf16[32,24,4096]{2,1,0:T(8,128)(2,1)}), bf16[32,24,4096]{2,1,0:T(8,128)(2,1)}, u32[]{:S(2)}, u32[]{:S(2)}) async-start(bf16[32,24,4096]{2,1,0:T(8,128)(2,1)} %convolution_convert_fusion), calls=%async_computation | async-start | bytes 12582912 | tf_op jit(solution)/shard_map/all_to_all | solution.py:67
  38.7 141.2 %all-to-all-done = bf16[32,24,4096]{2,1,0:T(8,128)(2,1)} async-done(((bf16[32,24,4096]{2,1,0:T(8,128)(2,1)}), bf16[32,24,4096]{2,1,0:T(8,128)(2,1)}, u32[]{:S(2)}, u32[]{:S(2)}) %all-to-all-start) | async-done | bytes 6291488 | tf_op jit(solution)/shard_map/all_to_all | solution.py:67
  180.0 8.3 %fusion = f32[32,24,1536]{2,1,0:T(8,128)S(1)} fusion(bf16[2048,768]{1,0:T(8,128)(2,1)} %bitcast.109, bf16[2048,768]{1,0:T(8,128)(2,1)} %bitcast.107, bf16[32,24,4096]{2,1,0:T(8,128)(2,1)} %all-to-all-done), kind=kOutput, calls=%fused_computation.3 | convolution fusion | flops 4844421120 | bytes 14155776 | tf_op jit(solution)/shard_map/esd,df->esf/dot_general | solution.py:78
  188.3 5.1 %multiply_reduce_fusion = (bf16[32,24]{1,0:T(8,128)(2,1)S(1)}, f32[32,24,768]{2,1,0:T(8,128)S(1)}) fusion(f32[32,24,1536]{2,1,0:T(8,128)S(1)} %fusion, bf16[1,1,768,2048]{3,2,1,0:T(8,128)(2,1)S(1)} %copy-done, bf16[32,24,4096]{2,1,0:T(8,128)(2,1)} %all-to-all-done), kind=kOutput, calls=%fused_computation.22 | convolution fusion | flops 2420047104 | bytes 13370880 | tf_op jit(solution)/shard_map/esd,fd->esf/dot_general | solution.py:84
  193.4 0.0 copy-done.4
  193.4 0.0 copy-start.5
  193.4 3.7 %fusion.5 = f32[32,24,2176]{2,1,0:T(8,128)S(1)} fusion(bf16[2048,768]{1,0:T(8,128)(2,1)S(1)} %bitcast.108, f32[32,24,768]{2,1,0:T(8,128)S(1)} %get-tuple-element.23, f32[32,24,1536]{2,1,0:T(8,128)S(1)} %fusion), kind=kOutput, calls=%fused_computation.10 | convolution fusion | flops 2572812288 | bytes 16908288 | tf_op jit(solution)/shard_map/esf,df->esd/dot_general | solution.py:92
  197.2 4.7 %select_convert_fusion = bf16[32,24,2176]{2,1,0:T(8,128)(2,1)} fusion(f32[32,24,2176]{2,1,0:T(8,128)S(1)} %fusion.5, bf16[2048,768]{1,0:T(8,128)(2,1)S(1)} %bitcast.110, bf16[32,24]{1,0:T(8,128)(2,1)S(1)} %get-tuple-element.22, pred[2176]{0:T(1024)(128)(4,1)S(1)} %iota_compare_fusion.4, f32[32,24,768]{2,1,0:T(8,128)S(1)} %get-tuple-element.23, ...), kind=kOutput, calls=%fused_computation.1 | convolution fusion | flops 2573795328 | bytes 17902592 | tf_op jit(solution)/shard_map/esf,df->esd/dot_general | solution.py:94
  201.8 5.5 %all-to-all-start.1 = ((bf16[32,24,2176]{2,1,0:T(8,128)(2,1)}), bf16[32,24,2176]{2,1,0:T(8,128)(2,1)}, u32[]{:S(2)}, u32[]{:S(2)}) async-start(bf16[32,24,2176]{2,1,0:T(8,128)(2,1)} %select_convert_fusion), calls=%async_computation.1 | async-start | bytes 6684672 | tf_op jit(solution)/shard_map/all_to_all | solution.py:67
  207.4 0.1 copy.45
  207.5 79.8 %all-to-all-done.1 = bf16[32,24,2176]{2,1,0:T(8,128)(2,1)} async-done(((bf16[32,24,2176]{2,1,0:T(8,128)(2,1)}), bf16[32,24,2176]{2,1,0:T(8,128)(2,1)}, u32[]{:S(2)}, u32[]{:S(2)}) %all-to-all-start.1) | async-done | bytes 3342368 | tf_op jit(solution)/shard_map/all_to_all | solution.py:67
  287.4 0.9 slice.114
  288.3 0.2 copy.51
  288.6 0.1 copy.48
  288.6 0.8 select_reduce_fusion
  289.5 0.6 fusion.46
  290.1 0.1 copy.49
  290.2 1.0 select_reduce_fusion.1
  291.2 1.4 fusion.28
  292.6 1.4 convolution_add_fusion.1
  294.1 0.7 subtract_convert_fusion
  294.8 3.6 %convolution_bitcast_fusion = f32[2,192,2176]{2,1,0:T(8,128)S(1)} fusion(bf16[32,24,2176]{2,1,0:T(8,128)(2,1)} %all-to-all-done.1, bf16[1,192,32,24]{1,2,3,0:T(8,128)(2,1)S(1)} %get-tuple-element.4, bf16[1,192,32,24]{1,2,3,0:T(8,128)(2,1)S(1)} %get-tuple-element.5), kind=kOutput, calls=%fused_computation.7 | convolution fusion | flops 1283751936 | bytes 7274496 | tf_op jit(solution)/shard_map/ptes,esd->ptd/dot_general | solution.py:121
  298.4 2.5 fusion.22
  (17 shorter events, 0.1 us)
Async XLA Ops:
  0.6 187.7 %copy-start = (bf16[1,1,768,2048]{3,2,1,0:T(8,128)(2,1)S(1)}, bf16[1,1,768,2048]{3,2,1,0:T(8,128)(2,1)}, u32[]{:S(2)}) copy-start(bf16[1,1,768,2048]{3,2,1,0:T(8,128)(2,1)} %param.14) | copy-start | bytes 9437188
  0.6 19.7 %collective-permute-start = (bf16[1,192,2048]{2,1,0:T(8,128)(2,1)}, bf16[1,192,2048]{2,1,0:T(8,128)(2,1)}, u32[]{:S(2)}, u32[]{:S(2)}) collective-permute-start(bf16[1,192,2048]{2,1,0:T(8,128)(2,1)} %param.8), channel_id=1, source_target_pairs={{0,224},{32,0},{64,32},{96,64},{128,96},{160,128},{192,160},{224,1... | collective-permute-start | bytes 2359304 | tf_op jit(solution)/shard_map/ppermute | solution.py:9
  26.8 153.2 %all-to-all-start = ((bf16[32,24,4096]{2,1,0:T(8,128)(2,1)}), bf16[32,24,4096]{2,1,0:T(8,128)(2,1)}, u32[]{:S(2)}, u32[]{:S(2)}) async-start(bf16[32,24,4096]{2,1,0:T(8,128)(2,1)} %convolution_convert_fusion), calls=%async_computation | async-start | bytes 12582912 | tf_op jit(solution)/shard_map/all_to_all | solution.py:67
  188.3 5.1 %copy-start.4 = (bf16[1,1,2048,768]{3,2,1,0:T(8,128)(2,1)S(1)}, bf16[1,1,2048,768]{3,2,1,0:T(8,128)(2,1)}, u32[]{:S(2)}) copy-start(bf16[1,1,2048,768]{3,2,1,0:T(8,128)(2,1)} %param.12) | copy-start | bytes 9437188
  193.4 3.7 %copy-start.5 = (bf16[1,1,2048,768]{3,2,1,0:T(8,128)(2,1)S(1)}, bf16[1,1,2048,768]{3,2,1,0:T(8,128)(2,1)}, u32[]{:S(2)}) copy-start(bf16[1,1,2048,768]{3,2,1,0:T(8,128)(2,1)} %param.13) | copy-start | bytes 9437188
  201.8 5.5 %copy-start.2 = (s32[1,192,8]{1,2,0:T(8,128)S(1)}, s32[1,192,8]{1,2,0:T(8,128)}, u32[]{:S(2)}) copy-start(s32[1,192,8]{1,2,0:T(8,128)} %param.10) | copy-start | bytes 18436
  201.8 5.7 %copy-start.3 = (f32[1,192,8]{1,2,0:T(8,128)S(1)}, f32[1,192,8]{1,2,0:T(8,128)}, u32[]{:S(2)}) copy-start(f32[1,192,8]{1,2,0:T(8,128)} %param.11) | copy-start | bytes 18436
  201.8 85.5 %all-to-all-start.1 = ((bf16[32,24,2176]{2,1,0:T(8,128)(2,1)}), bf16[32,24,2176]{2,1,0:T(8,128)(2,1)}, u32[]{:S(2)}, u32[]{:S(2)}) async-start(bf16[32,24,2176]{2,1,0:T(8,128)(2,1)} %select_convert_fusion), calls=%async_computation.1 | async-start | bytes 6684672 | tf_op jit(solution)/shard_map/all_to_all | solution.py:67
  294.8 3.7 %copy-start.1 = (bf16[1,2048,128]{2,1,0:T(8,128)(2,1)S(1)}, bf16[1,2048,128]{2,1,0:T(8,128)(2,1)}, u32[]{:S(2)}) copy-start(bf16[1,2048,128]{2,1,0:T(8,128)(2,1)} %param.15) | copy-start | bytes 1572868

commit v7 on v6

--- a/solution.py
+++ b/solution.py
@@ -58,6 +58,8 @@
             chosen[:, None, None] == slot_ids[None, :, :], route_weight[:, k][:, None, None], 0.0
         )
     pack = pack.astype(jnp.bfloat16)
+    combine_parts = jnp.stack(split_bf16(combine, 2))
+    pack, combine_parts = lax.optimization_barrier((pack, combine_parts))
 
     def pack_rows(rows):
         sent = jnp.einsum("est,td->esd", pack, rows, preferred_element_type=jnp.float32)
@@ -117,7 +119,6 @@
         router_grad = router_grad + lax.dot_general(
             part, w_router, (((1,), (1,)), ((), ())), preferred_element_type=jnp.float32
         )
-    combine_parts = jnp.stack(split_bf16(combine, 2))
     expert_both = jnp.einsum(
         "ptes,esd->ptd", combine_parts, returned, preferred_element_type=jnp.float32
     )

time: 301 us -> 300 us (level)
  waiting for transfers between devices: 238 us -> 234 us
  other arithmetic: 5.55 us -> 8.65 us
    ppermute x1, waiting for transfers between devices: 17 us -> 13.1 us  [from_behind(): lax.ppermute(shard, axis, [(i, (i + by) % size) for i in range(size)])]
  transfers between devices with their start and end apart: 3 -> 3, of which waited for: 3 -> 3; matrix products, arithmetic and copies ran while one was open for 1% -> 2% of each run, Pallas kernels for 0% -> 0%
where the time goes in v7:
time: 300 us
  waiting for transfers between devices  234 us (78%)
  matrix products  36.5 us (12%)
  starting transfers between devices  18.3 us (6%)
  other arithmetic  8.65 us (3%)
    all_to_all x2, waiting for transfers between devices, exchange(): lax.all_to_all(block, 'expert', split_axis=0, concat_axis=0, tiled=True)  221 us
    all_to_all x2, starting transfers between devices, exchange(): lax.all_to_all(block, 'expert', split_axis=0, concat_axis=0, tiled=True)  18.2 us
    ppermute x1, waiting for transfers between devices, from_behind(): lax.ppermute(shard, axis, [(i, (i + by) % size) for i in range(size)])  13.1 us
    dot_general x1, matrix products, per_device(): jnp.einsum('esd,df->esf', inputs, jnp.concatenate([w_gate, w_up], axis=1)...  8.31 us
  transfers between devices with their start and end apart: 3, of which 3 were waited for; matrix products, arithmetic and copies ran while one was open for 2% of the time, Pallas kernels for 0%

profile of v7, /device:TPU:33, one launch (start us, length us, event | category | flops | bytes accessed | tf_op | source)
XLA Modules:
  0.0 299.6 jit_solution(16836311428309767752)
XLA Ops:
  0.6 0.1 collective-permute-start
  0.7 0.9 convert_reduce_fusion
  1.6 0.1 convolution_convert_fusion.1
  1.8 0.8 select_reduce_fusion.2
  2.6 0.7 add_select_fusion
  3.3 0.7 exponential_reduce_fusion
  4.0 0.7 bitcast_divide_fusion
  4.8 0.7 subtract_convert_fusion
  5.5 1.0 pad_maximum_fusion
  6.5 0.7 add_convert_fusion
  7.2 13.1 %collective-permute-done = bf16[1,192,2048]{2,1,0:T(8,128)(2,1)} collective-permute-done((bf16[1,192,2048]{2,1,0:T(8,128)(2,1)}, bf16[1,192,2048]{2,1,0:T(8,128)(2,1)}, u32[]{:S(2)}, u32[]{:S(2)}) %collective-permute-start) | collective-permute-done | bytes 786464 | tf_op jit(solution)/shard_map/ppermute | solution.py:9
  20.3 5.6 %convolution_convert_fusion = bf16[32,24,4096]{2,1,0:T(8,128)(2,1)} fusion(bf16[32,24,192]{2,1,0:T(8,128)(2,1)S(1)} %add_convert_fusion, bf16[192,2048]{1,0:T(8,128)(2,1)} %bitcast, bf16[192,2048]{1,0:T(8,128)(2,1)S(1)} %bitcast.85), kind=kOutput, calls=%fused_computation | convolution fusion | flops 1214251008 | bytes 8159232 | tf_op jit(solution)/shard_map/est,td->esd/dot_general | solution.py:65
  25.9 12.0 %all-to-all-start = ((bf16[32,24,4096]{2,1,0:T(8,128)(2,1)}), bf16[32,24,4096]{2,1,0:T(8,128)(2,1)}, u32[]{:S(2)}, u32[]{:S(2)}) async-start(bf16[32,24,4096]{2,1,0:T(8,128)(2,1)} %convolution_convert_fusion), calls=%async_computation | async-start | bytes 12582912 | tf_op jit(solution)/shard_map/all_to_all | solution.py:69
  37.9 141.1 %all-to-all-done = bf16[32,24,4096]{2,1,0:T(8,128)(2,1)} async-done(((bf16[32,24,4096]{2,1,0:T(8,128)(2,1)}), bf16[32,24,4096]{2,1,0:T(8,128)(2,1)}, u32[]{:S(2)}, u32[]{:S(2)}) %all-to-all-start) | async-done | bytes 6291488 | tf_op jit(solution)/shard_map/all_to_all | solution.py:69
  179.0 8.3 %fusion = f32[32,24,1536]{2,1,0:T(8,128)S(1)} fusion(bf16[2048,768]{1,0:T(8,128)(2,1)} %bitcast.115, bf16[2048,768]{1,0:T(8,128)(2,1)} %bitcast.113, bf16[32,24,4096]{2,1,0:T(8,128)(2,1)} %all-to-all-done), kind=kOutput, calls=%fused_computation.3 | convolution fusion | flops 4844421120 | bytes 14155776 | tf_op jit(solution)/shard_map/esd,df->esf/dot_general | solution.py:80
  187.4 5.1 %multiply_reduce_fusion = (bf16[32,24]{1,0:T(8,128)(2,1)S(1)}, f32[32,24,768]{2,1,0:T(8,128)S(1)}) fusion(f32[32,24,1536]{2,1,0:T(8,128)S(1)} %fusion, bf16[1,1,768,2048]{3,2,1,0:T(8,128)(2,1)S(1)} %copy-done, bf16[32,24,4096]{2,1,0:T(8,128)(2,1)} %all-to-all-done), kind=kOutput, calls=%fused_computation.22 | convolution fusion | flops 2420047104 | bytes 13370880 | tf_op jit(solution)/shard_map/esd,fd->esf/dot_general | solution.py:86
  192.5 3.7 %fusion.5 = f32[32,24,2176]{2,1,0:T(8,128)S(1)} fusion(bf16[2048,768]{1,0:T(8,128)(2,1)S(1)} %bitcast.114, f32[32,24,768]{2,1,0:T(8,128)S(1)} %get-tuple-element.25, f32[32,24,1536]{2,1,0:T(8,128)S(1)} %fusion), kind=kOutput, calls=%fused_computation.10 | convolution fusion | flops 2572812288 | bytes 16908288 | tf_op jit(solution)/shard_map/esf,df->esd/dot_general | solution.py:94
  196.2 4.7 %select_convert_fusion = bf16[32,24,2176]{2,1,0:T(8,128)(2,1)} fusion(f32[32,24,2176]{2,1,0:T(8,128)S(1)} %fusion.5, bf16[2048,768]{1,0:T(8,128)(2,1)S(1)} %bitcast.116, bf16[32,24]{1,0:T(8,128)(2,1)S(1)} %get-tuple-element.24, pred[2176]{0:T(1024)(128)(4,1)S(1)} %iota_compare_fusion.4, f32[32,24,768]{2,1,0:T(8,128)S(1)} %get-tuple-element.25, ...), kind=kOutput, calls=%fused_computation.1 | convolution fusion | flops 2573795328 | bytes 17902592 | tf_op jit(solution)/shard_map/esf,df->esd/dot_general | solution.py:96
  200.9 6.3 %all-to-all-start.1 = ((bf16[32,24,2176]{2,1,0:T(8,128)(2,1)}), bf16[32,24,2176]{2,1,0:T(8,128)(2,1)}, u32[]{:S(2)}, u32[]{:S(2)}) async-start(bf16[32,24,2176]{2,1,0:T(8,128)(2,1)} %select_convert_fusion), calls=%async_computation.1 | async-start | bytes 6684672 | tf_op jit(solution)/shard_map/all_to_all | solution.py:69
  207.2 0.1 copy.43
  207.3 79.4 %all-to-all-done.1 = bf16[32,24,2176]{2,1,0:T(8,128)(2,1)} async-done(((bf16[32,24,2176]{2,1,0:T(8,128)(2,1)}), bf16[32,24,2176]{2,1,0:T(8,128)(2,1)}, u32[]{:S(2)}, u32[]{:S(2)}) %all-to-all-start.1) | async-done | bytes 3342368 | tf_op jit(solution)/shard_map/all_to_all | solution.py:69
  286.7 0.9 slice.114
  287.7 0.2 copy.48
  287.9 0.1 copy.45
  288.0 0.8 select_reduce_fusion
  288.8 0.6 fusion.34
  289.5 0.1 copy.46
  289.6 1.0 select_reduce_fusion.1
  290.6 1.4 fusion.25
  292.0 1.4 convolution_add_fusion.1
  293.4 3.6 %convolution_bitcast_fusion = f32[2,192,2176]{2,1,0:T(8,128)S(1)} fusion(bf16[2,192,32,24]{1,2,3,0:T(8,128)(2,1)S(1)} %copy-done.2, bf16[32,24,2176]{2,1,0:T(8,128)(2,1)} %all-to-all-done.1), kind=kOutput, calls=%fused_computation.7 | convolution fusion | flops 1283457024 | bytes 7274496 | tf_op jit(solution)/shard_map/ptes,esd->ptd/dot_general | solution.py:122
  297.1 2.5 fusion.22
  (24 shorter events, 0.2 us)
Async XLA Ops:
  0.6 186.7 %copy-start = (bf16[1,1,768,2048]{3,2,1,0:T(8,128)(2,1)S(1)}, bf16[1,1,768,2048]{3,2,1,0:T(8,128)(2,1)}, u32[]{:S(2)}) copy-start(bf16[1,1,768,2048]{3,2,1,0:T(8,128)(2,1)} %param.14) | copy-start | bytes 9437188
  0.6 19.7 %collective-permute-start = (bf16[1,192,2048]{2,1,0:T(8,128)(2,1)}, bf16[1,192,2048]{2,1,0:T(8,128)(2,1)}, u32[]{:S(2)}, u32[]{:S(2)}) collective-permute-start(bf16[1,192,2048]{2,1,0:T(8,128)(2,1)} %param.8), channel_id=1, source_target_pairs={{0,224},{32,0},{64,32},{96,64},{128,96},{160,128},{192,160},{224,1... | collective-permute-start | bytes 2359304 | tf_op jit(solution)/shard_map/ppermute | solution.py:9
  4.8 15.6 %copy-start.3 = (bf16[1,192,2048]{2,1,0:T(8,128)(2,1)S(1)}, bf16[1,192,2048]{2,1,0:T(8,128)(2,1)}, u32[]{:S(2)}) copy-start(bf16[1,192,2048]{2,1,0:T(8,128)(2,1)} %param.9) | copy-start | bytes 2359300
  25.9 153.1 %all-to-all-start = ((bf16[32,24,4096]{2,1,0:T(8,128)(2,1)}), bf16[32,24,4096]{2,1,0:T(8,128)(2,1)}, u32[]{:S(2)}, u32[]{:S(2)}) async-start(bf16[32,24,4096]{2,1,0:T(8,128)(2,1)} %convolution_convert_fusion), calls=%async_computation | async-start | bytes 12582912 | tf_op jit(solution)/shard_map/all_to_all | solution.py:69
  187.4 5.1 %copy-start.6 = (bf16[1,1,2048,768]{3,2,1,0:T(8,128)(2,1)S(1)}, bf16[1,1,2048,768]{3,2,1,0:T(8,128)(2,1)}, u32[]{:S(2)}) copy-start(bf16[1,1,2048,768]{3,2,1,0:T(8,128)(2,1)} %param.12) | copy-start | bytes 9437188
  192.5 3.7 %copy-start.7 = (bf16[1,1,2048,768]{3,2,1,0:T(8,128)(2,1)S(1)}, bf16[1,1,2048,768]{3,2,1,0:T(8,128)(2,1)}, u32[]{:S(2)}) copy-start(bf16[1,1,2048,768]{3,2,1,0:T(8,128)(2,1)} %param.13) | copy-start | bytes 9437188
  200.9 6.3 %copy-start.5 = (s32[1,192,8]{1,2,0:T(8,128)S(1)}, s32[1,192,8]{1,2,0:T(8,128)}, u32[]{:S(2)}) copy-start(s32[1,192,8]{1,2,0:T(8,128)} %param.10) | copy-start | bytes 18436
  200.9 87.9 %copy-start.4 = (f32[1,192,8]{1,2,0:T(8,128)S(1)}, f32[1,192,8]{1,2,0:T(8,128)}, u32[]{:S(2)}) copy-start(f32[1,192,8]{1,2,0:T(8,128)} %param.11) | copy-start | bytes 18436
  200.9 85.8 %all-to-all-start.1 = ((bf16[32,24,2176]{2,1,0:T(8,128)(2,1)}), bf16[32,24,2176]{2,1,0:T(8,128)(2,1)}, u32[]{:S(2)}, u32[]{:S(2)}) async-start(bf16[32,24,2176]{2,1,0:T(8,128)(2,1)} %select_convert_fusion), calls=%async_computation.1 | async-start | bytes 6684672 | tf_op jit(solution)/shard_map/all_to_all | solution.py:69
  289.6 3.9 %copy-start.2 = (bf16[2,192,32,24]{1,2,3,0:T(8,128)(2,1)S(1)}, bf16[2,192,32,24]{1,2,3,0:T(8,128)(2,1)}, u32[]{:S(2)}) copy-start(bf16[2,192,32,24]{1,2,3,0:T(8,128)(2,1)} %pad_maximum_fusion) | copy-start | bytes 1769476
  293.4 3.6 %copy-start.1 = (bf16[1,2048,128]{2,1,0:T(8,128)(2,1)S(1)}, bf16[1,2048,128]{2,1,0:T(8,128)(2,1)}, u32[]{:S(2)}) copy-start(bf16[1,2048,128]{2,1,0:T(8,128)(2,1)} %param.15) | copy-start | bytes 1572868

commit v8 on v7

--- a/solution.py
+++ b/solution.py
@@ -92,8 +92,11 @@
     ).astype(jnp.bfloat16)
     up_grad = (hidden_grad * activation).astype(jnp.bfloat16)
     pair_rows = jnp.einsum(
-        "esf,df->esd", gate_grad, w_gate_wide, preferred_element_type=jnp.float32
-    ) + jnp.einsum("esf,df->esd", up_grad, w_up_wide, preferred_element_type=jnp.float32)
+        "esf,df->esd",
+        jnp.concatenate([gate_grad, up_grad], axis=2),
+        jnp.concatenate([w_gate_wide, w_up_wide], axis=1),
+        preferred_element_type=jnp.float32,
+    )
     lane_ids = jnp.arange(wide, dtype=jnp.int32)[None, None, :]
     pair_rows = jnp.where(
         lane_ids == width_model, pair_dots.astype(jnp.float32)[:, :, None], pair_rows

time: 300 us -> 302 us (level)
    dot_general x2 -> x1, matrix products: 8.37 us -> 8.69 us  [per_device(): jnp.einsum('esf,df->esd', jnp.concatenate([gate_grad, up_grad], axis=2),...]
where the time goes in v8:
time: 302 us; the launch traced here: 301 us
  waiting for transfers between devices  234 us (77%)
  matrix products  38.1 us (13%)
  starting transfers between devices  18.3 us (6%)
  other arithmetic  8.65 us (3%)
    all_to_all x2, waiting for transfers between devices, exchange(): lax.all_to_all(block, 'expert', split_axis=0, concat_axis=0, tiled=True)  221 us
    all_to_all x2, starting transfers between devices, exchange(): lax.all_to_all(block, 'expert', split_axis=0, concat_axis=0, tiled=True)  18.2 us
    ppermute x1, waiting for transfers between devices, from_behind(): lax.ppermute(shard, axis, [(i, (i + by) % size) for i in range(size)])  13.1 us
    dot_general x1, matrix products, per_device(): jnp.einsum('esf,df->esd', jnp.concatenate([gate_grad, up_grad], axis=2),...  8.69 us
    dot_general x1, matrix products, per_device(): jnp.einsum('esd,df->esf', inputs, jnp.concatenate([w_gate, w_up], axis=1)...  8.31 us
    dot_general x1, matrix products, per_device(): jnp.einsum('esd,fd->esf', grad_rows, w_down, preferred_element_type=jnp.f...  6.45 us
  transfers between devices with their start and end apart: 3, of which 3 were waited for; matrix products, arithmetic and copies ran while one was open for 2% of the time, Pallas kernels for 0%

profile of v8, /device:TPU:33, one launch (start us, length us, event | category | flops | bytes accessed | tf_op | source)
XLA Modules:
  0.0 301.3 jit_solution(9601133518185000137)
XLA Ops:
  0.6 0.1 collective-permute-start
  0.7 0.9 convert_reduce_fusion
  1.6 0.1 convolution_convert_fusion.1
  1.8 0.8 select_reduce_fusion.2
  2.6 0.7 add_select_fusion
  3.3 0.7 exponential_reduce_fusion
  4.0 0.7 bitcast_divide_fusion
  4.7 0.1 copy.40
  4.8 0.7 subtract_convert_fusion
  5.5 1.0 pad_maximum_fusion
  6.5 0.7 add_convert_fusion
  7.2 13.1 %collective-permute-done = bf16[1,192,2048]{2,1,0:T(8,128)(2,1)} collective-permute-done((bf16[1,192,2048]{2,1,0:T(8,128)(2,1)}, bf16[1,192,2048]{2,1,0:T(8,128)(2,1)}, u32[]{:S(2)}, u32[]{:S(2)}) %collective-permute-start) | collective-permute-done | bytes 786464 | tf_op jit(solution)/shard_map/ppermute | solution.py:9
  20.3 5.6 %convolution_convert_fusion = bf16[32,24,4096]{2,1,0:T(8,128)(2,1)} fusion(bf16[32,24,192]{2,1,0:T(8,128)(2,1)S(1)} %add_convert_fusion, bf16[192,2048]{1,0:T(8,128)(2,1)} %bitcast, bf16[192,2048]{1,0:T(8,128)(2,1)S(1)} %bitcast.84), kind=kOutput, calls=%fused_computation.4 | convolution fusion | flops 1214251008 | bytes 8159232 | tf_op jit(solution)/shard_map/est,td->esd/dot_general | solution.py:65
  25.9 12.0 %all-to-all-start = ((bf16[32,24,4096]{2,1,0:T(8,128)(2,1)}), bf16[32,24,4096]{2,1,0:T(8,128)(2,1)}, u32[]{:S(2)}, u32[]{:S(2)}) async-start(bf16[32,24,4096]{2,1,0:T(8,128)(2,1)} %convolution_convert_fusion), calls=%async_computation | async-start | bytes 12582912 | tf_op jit(solution)/shard_map/all_to_all | solution.py:69
  37.9 141.1 %all-to-all-done = bf16[32,24,4096]{2,1,0:T(8,128)(2,1)} async-done(((bf16[32,24,4096]{2,1,0:T(8,128)(2,1)}), bf16[32,24,4096]{2,1,0:T(8,128)(2,1)}, u32[]{:S(2)}, u32[]{:S(2)}) %all-to-all-start) | async-done | bytes 6291488 | tf_op jit(solution)/shard_map/all_to_all | solution.py:69
  179.0 8.3 %fusion.10 = f32[32,24,1536]{2,1,0:T(8,128)S(1)} fusion(bf16[2048,768]{1,0:T(8,128)(2,1)} %bitcast.112, bf16[2048,768]{1,0:T(8,128)(2,1)} %bitcast.114, bf16[32,24,4096]{2,1,0:T(8,128)(2,1)} %all-to-all-done), kind=kOutput, calls=%fused_computation.13 | convolution fusion | flops 4844421120 | bytes 14155776 | tf_op jit(solution)/shard_map/esd,df->esf/dot_general | solution.py:80
  187.4 6.4 %multiply_convert_fusion = (bf16[32,24,768]{2,1,0:T(8,128)(2,1)S(1)}, bf16[32,24,768]{2,1,0:T(8,128)(2,1)}, bf16[32,24]{1,0:T(8,128)(2,1)S(1)}) fusion(f32[32,24,1536]{2,1,0:T(8,128)S(1)} %fusion.10, bf16[1,1,768,2048]{3,2,1,0:T(8,128)(2,1)S(1)} %copy-done, bf16[32,24,4096]{2,1,0:T(8,128)(2,1)} %all-to-all-done), kind=kOutput, calls=%fused_computation.30 | convolution fusion | flops 2424765696 | bytes 13370880 | tf_op jit(solution)/shard_map/esd,fd->esf/dot_general | solution.py:86
  193.8 8.7 %select_convert_fusion = bf16[32,24,2176]{2,1,0:T(8,128)(2,1)} fusion(bf16[2048,768]{1,0:T(8,128)(2,1)S(1)} %bitcast.113, bf16[2048,768]{1,0:T(8,128)(2,1)S(1)} %bitcast.115, bf16[32,24]{1,0:T(8,128)(2,1)S(1)} %get-tuple-element.10, pred[2176]{0:T(1024)(128)(4,1)S(1)} %iota_compare_fusion.6, bf16[32,24,768]{2,1,0:T(8,128)(2,1)} %get-tuple-element.9, ...), kind=kOutput, calls=%fused_computation.11 | convolution fusion | flops 5166956544 | bytes 11996800 | tf_op jit(solution)/shard_map/esf,df->esd/dot_general | solution.py:94
  202.5 6.3 %all-to-all-start.1 = ((bf16[32,24,2176]{2,1,0:T(8,128)(2,1)}), bf16[32,24,2176]{2,1,0:T(8,128)(2,1)}, u32[]{:S(2)}, u32[]{:S(2)}) async-start(bf16[32,24,2176]{2,1,0:T(8,128)(2,1)} %select_convert_fusion), calls=%async_computation.1 | async-start | bytes 6684672 | tf_op jit(solution)/shard_map/all_to_all | solution.py:69
  208.8 0.1 copy.42
  208.9 79.5 %all-to-all-done.1 = bf16[32,24,2176]{2,1,0:T(8,128)(2,1)} async-done(((bf16[32,24,2176]{2,1,0:T(8,128)(2,1)}), bf16[32,24,2176]{2,1,0:T(8,128)(2,1)}, u32[]{:S(2)}, u32[]{:S(2)}) %all-to-all-start.1) | async-done | bytes 3342368 | tf_op jit(solution)/shard_map/all_to_all | solution.py:69
  288.4 0.9 slice.114
  289.4 0.2 copy.47
  289.6 0.1 copy.44
  289.7 0.8 select_reduce_fusion
  290.6 0.6 fusion.43
  291.2 0.1 copy.45
  291.3 1.0 select_reduce_fusion.1
  292.3 1.4 fusion.34
  293.7 1.4 convolution_add_fusion.1
  295.2 3.6 %convolution_bitcast_fusion = f32[2,192,2176]{2,1,0:T(8,128)S(1)} fusion(bf16[2,192,32,24]{1,2,3,0:T(8,128)(2,1)S(1)} %copy-done.2, bf16[32,24,2176]{2,1,0:T(8,128)(2,1)} %all-to-all-done.1), kind=kOutput, calls=%fused_computation.17 | convolution fusion | flops 1283457024 | bytes 7274496 | tf_op jit(solution)/shard_map/ptes,esd->ptd/dot_general | solution.py:125
  298.8 2.5 fusion.31
  (23 shorter events, 0.1 us)
Async XLA Ops:
  0.6 186.7 %copy-start = (bf16[1,1,768,2048]{3,2,1,0:T(8,128)(2,1)S(1)}, bf16[1,1,768,2048]{3,2,1,0:T(8,128)(2,1)}, u32[]{:S(2)}) copy-start(bf16[1,1,768,2048]{3,2,1,0:T(8,128)(2,1)} %param.14) | copy-start | bytes 9437188
  0.6 19.7 %collective-permute-start = (bf16[1,192,2048]{2,1,0:T(8,128)(2,1)}, bf16[1,192,2048]{2,1,0:T(8,128)(2,1)}, u32[]{:S(2)}, u32[]{:S(2)}) collective-permute-start(bf16[1,192,2048]{2,1,0:T(8,128)(2,1)} %param.8), channel_id=1, source_target_pairs={{0,224},{32,0},{64,32},{96,64},{128,96},{160,128},{192,160},{224,1... | collective-permute-start | bytes 2359304 | tf_op jit(solution)/shard_map/ppermute | solution.py:9
  4.8 15.6 %copy-start.3 = (bf16[1,192,2048]{2,1,0:T(8,128)(2,1)S(1)}, bf16[1,192,2048]{2,1,0:T(8,128)(2,1)}, u32[]{:S(2)}) copy-start(bf16[1,192,2048]{2,1,0:T(8,128)(2,1)} %param.9) | copy-start | bytes 2359300
  25.9 153.1 %all-to-all-start = ((bf16[32,24,4096]{2,1,0:T(8,128)(2,1)}), bf16[32,24,4096]{2,1,0:T(8,128)(2,1)}, u32[]{:S(2)}, u32[]{:S(2)}) async-start(bf16[32,24,4096]{2,1,0:T(8,128)(2,1)} %convolution_convert_fusion), calls=%async_computation | async-start | bytes 12582912 | tf_op jit(solution)/shard_map/all_to_all | solution.py:69
  187.4 6.5 %copy-start.6 = (bf16[1,1,2048,768]{3,2,1,0:T(8,128)(2,1)S(1)}, bf16[1,1,2048,768]{3,2,1,0:T(8,128)(2,1)}, u32[]{:S(2)}) copy-start(bf16[1,1,2048,768]{3,2,1,0:T(8,128)(2,1)} %param.13) | copy-start | bytes 9437188
  187.4 6.5 %copy-start.7 = (bf16[1,1,2048,768]{3,2,1,0:T(8,128)(2,1)S(1)}, bf16[1,1,2048,768]{3,2,1,0:T(8,128)(2,1)}, u32[]{:S(2)}) copy-start(bf16[1,1,2048,768]{3,2,1,0:T(8,128)(2,1)} %param.12) | copy-start | bytes 9437188
  202.5 6.3 %copy-start.5 = (s32[1,192,8]{1,2,0:T(8,128)S(1)}, s32[1,192,8]{1,2,0:T(8,128)}, u32[]{:S(2)}) copy-start(s32[1,192,8]{1,2,0:T(8,128)} %param.10) | copy-start | bytes 18436
  202.5 88.0 %copy-start.4 = (f32[1,192,8]{1,2,0:T(8,128)S(1)}, f32[1,192,8]{1,2,0:T(8,128)}, u32[]{:S(2)}) copy-start(f32[1,192,8]{1,2,0:T(8,128)} %param.11) | copy-start | bytes 18436
  202.5 85.9 %all-to-all-start.1 = ((bf16[32,24,2176]{2,1,0:T(8,128)(2,1)}), bf16[32,24,2176]{2,1,0:T(8,128)(2,1)}, u32[]{:S(2)}, u32[]{:S(2)}) async-start(bf16[32,24,2176]{2,1,0:T(8,128)(2,1)} %select_convert_fusion), calls=%async_computation.1 | async-start | bytes 6684672 | tf_op jit(solution)/shard_map/all_to_all | solution.py:69
  291.3 3.9 %copy-start.2 = (bf16[2,192,32,24]{1,2,3,0:T(8,128)(2,1)S(1)}, bf16[2,192,32,24]{1,2,3,0:T(8,128)(2,1)}, u32[]{:S(2)}) copy-start(bf16[2,192,32,24]{1,2,3,0:T(8,128)(2,1)} %pad_maximum_fusion) | copy-start | bytes 1769476
  295.1 3.6 %copy-start.1 = (bf16[1,2048,128]{2,1,0:T(8,128)(2,1)S(1)}, bf16[1,2048,128]{2,1,0:T(8,128)(2,1)}, u32[]{:S(2)}) copy-start(bf16[1,2048,128]{2,1,0:T(8,128)(2,1)} %param.15) | copy-start | bytes 1572868

commit v9 on v7

--- a/solution.py
+++ b/solution.py
@@ -68,7 +68,9 @@
     def exchange(block):
         return lax.all_to_all(block, "expert", split_axis=0, concat_axis=0, tiled=True)
 
-    got = exchange(pack_rows(jnp.concatenate([x_in, incoming], axis=1)))
+    sent = jnp.concatenate([pack_rows(x_in), jnp.zeros_like(pack_rows(x_in))], axis=2)
+    sent = lax.optimization_barrier(sent)
+    got = exchange(lax.dynamic_update_slice(sent, pack_rows(incoming), (0, 0, width_model)))
     inputs = got[:, :, :width_model]
     grad_rows = got[:, :, width_model:]
     lanes = 128

time: 300 us -> 298 us (level)
  waiting for transfers between devices: 234 us -> 230 us
  local copies, waits for them, and re-layouts: 1.62 us -> 4.91 us
    ppermute x1, waiting for transfers between devices: 13.1 us -> 8.86 us  [from_behind(): lax.ppermute(shard, axis, [(i, (i + by) % size) for i in range(size)])]
    concatenate x0 -> x1, local copies, waits for them, and re-layouts: none -> 3.29 us  [per_device(): jnp.concatenate([pack_rows(x_in), jnp.zeros_like(pack_rows(x_in))], axis=2)]
  transfers between devices with their start and end apart: 3 -> 3, of which waited for: 3 -> 3; matrix products, arithmetic and copies ran while one was open for 2% -> 4% of each run, Pallas kernels for 0% -> 0%
where the time goes in v9:
time: 298 us
  waiting for transfers between devices  230 us (77%)
  matrix products  35.8 us (12%)
  starting transfers between devices  17.7 us (6%)
  other arithmetic  8.65 us (3%)
  local copies, waits for them, and re-layouts  4.91 us (2%)
    all_to_all x2, waiting for transfers between devices, exchange(): lax.all_to_all(block, 'expert', split_axis=0, concat_axis=0, tiled=True)  221 us
    all_to_all x2, starting transfers between devices, exchange(): lax.all_to_all(block, 'expert', split_axis=0, concat_axis=0, tiled=True)  17.6 us
    ppermute x1, waiting for transfers between devices, from_behind(): lax.ppermute(shard, axis, [(i, (i + by) % size) for i in range(size)])  8.86 us
    dot_general x1, matrix products, per_device(): jnp.einsum('esd,df->esf', inputs, jnp.concatenate([w_gate, w_up], axis=1)...  8.31 us
  transfers between devices with their start and end apart: 3, of which 3 were waited for; matrix products, arithmetic and copies ran while one was open for 4% of the time, Pallas kernels for 0%

profile of v9, /device:TPU:33, one launch (start us, length us, event | category | flops | bytes accessed | tf_op | source)
XLA Modules:
  0.0 297.6 jit_solution(11209685657618091576)
XLA Ops:
  0.7 0.9 convert_reduce_fusion
  1.6 0.1 convolution_convert_fusion.2
  1.8 0.8 select_reduce_fusion.2
  2.6 0.7 add_select_fusion
  3.3 0.7 exponential_reduce_fusion
  4.0 0.7 bitcast_divide_fusion
  4.8 0.7 subtract_convert_fusion
  5.5 1.0 pad_maximum_fusion
  6.5 0.7 add_convert_fusion
  7.2 1.0 convolution_convert_fusion.1
  8.2 3.3 %concatenate.12 = bf16[32,24,4096]{2,1,0:T(8,128)(2,1)} pad(bf16[32,24,2048]{2,1,0:T(8,128)(2,1)S(1)} %convolution_convert_fusion.1, bf16[]{:T(256)} %constant.7.clone.1), padding=0_0x0_0x0_2048 | pad | bytes 9437186 | tf_op jit(solution)/shard_map/concatenate | solution.py:71
  11.5 8.9 %collective-permute-done = bf16[1,192,2048]{2,1,0:T(8,128)(2,1)} collective-permute-done((bf16[1,192,2048]{2,1,0:T(8,128)(2,1)}, bf16[1,192,2048]{2,1,0:T(8,128)(2,1)}, u32[]{:S(2)}, u32[]{:S(2)}) %collective-permute-start) | collective-permute-done | bytes 786464 | tf_op jit(solution)/shard_map/ppermute | solution.py:9
  20.3 3.9 %fusion.3 = bf16[32,24,4096]{2,1,0:T(8,128)(2,1)} fusion(bf16[32,24,4096]{2,1,0:T(8,128)(2,1)} %concatenate.12, bf16[32,24,192]{2,1,0:T(8,128)(2,1)S(1)} %add_convert_fusion, bf16[1,192,2048]{2,1,0:T(8,128)(2,1)} %collective-permute-done), kind=kOutput, calls=%fused_computation.8 | convolution fusion | flops 605552640 | bytes 4227072 | tf_op jit(solution)/shard_map/est,td->esd/dot_general | solution.py:65
  24.2 12.0 %all-to-all-start = ((bf16[32,24,4096]{2,1,0:T(8,128)(2,1)}), bf16[32,24,4096]{2,1,0:T(8,128)(2,1)}, u32[]{:S(2)}, u32[]{:S(2)}) async-start(bf16[32,24,4096]{2,1,0:T(8,128)(2,1)} %fusion.3), calls=%async_computation | async-start | bytes 12582912 | tf_op jit(solution)/shard_map/all_to_all | solution.py:69
  36.2 141.2 %all-to-all-done = bf16[32,24,4096]{2,1,0:T(8,128)(2,1)} async-done(((bf16[32,24,4096]{2,1,0:T(8,128)(2,1)}), bf16[32,24,4096]{2,1,0:T(8,128)(2,1)}, u32[]{:S(2)}, u32[]{:S(2)}) %all-to-all-start) | async-done | bytes 6291488 | tf_op jit(solution)/shard_map/all_to_all | solution.py:69
  177.4 8.3 %fusion = f32[32,24,1536]{2,1,0:T(8,128)S(1)} fusion(bf16[2048,768]{1,0:T(8,128)(2,1)} %bitcast.118, bf16[2048,768]{1,0:T(8,128)(2,1)} %bitcast.116, bf16[32,24,4096]{2,1,0:T(8,128)(2,1)} %all-to-all-done), kind=kOutput, calls=%fused_computation.2 | convolution fusion | flops 4844421120 | bytes 14155776 | tf_op jit(solution)/shard_map/esd,df->esf/dot_general | solution.py:82
  185.8 5.1 %multiply_reduce_fusion = (bf16[32,24]{1,0:T(8,128)(2,1)S(1)}, f32[32,24,768]{2,1,0:T(8,128)S(1)}) fusion(f32[32,24,1536]{2,1,0:T(8,128)S(1)} %fusion, bf16[1,1,768,2048]{3,2,1,0:T(8,128)(2,1)S(1)} %copy-done, bf16[32,24,4096]{2,1,0:T(8,128)(2,1)} %all-to-all-done), kind=kOutput, calls=%fused_computation.24 | convolution fusion | flops 2420047104 | bytes 13370880 | tf_op jit(solution)/shard_map/esd,fd->esf/dot_general | solution.py:88
  190.9 3.7 %fusion.6 = f32[32,24,2176]{2,1,0:T(8,128)S(1)} fusion(bf16[2048,768]{1,0:T(8,128)(2,1)S(1)} %bitcast.117, f32[32,24,768]{2,1,0:T(8,128)S(1)} %get-tuple-element.25, f32[32,24,1536]{2,1,0:T(8,128)S(1)} %fusion), kind=kOutput, calls=%fused_computation.12 | convolution fusion | flops 2572812288 | bytes 16908288 | tf_op jit(solution)/shard_map/esf,df->esd/dot_general | solution.py:96
  194.6 4.7 %select_convert_fusion = bf16[32,24,2176]{2,1,0:T(8,128)(2,1)} fusion(f32[32,24,2176]{2,1,0:T(8,128)S(1)} %fusion.6, bf16[2048,768]{1,0:T(8,128)(2,1)S(1)} %bitcast.119, bf16[32,24]{1,0:T(8,128)(2,1)S(1)} %get-tuple-element.24, pred[2176]{0:T(1024)(128)(4,1)S(1)} %iota_compare_fusion.4, f32[32,24,768]{2,1,0:T(8,128)S(1)} %get-tuple-element.25, ...), kind=kOutput, calls=%fused_computation | convolution fusion | flops 2573795328 | bytes 17902592 | tf_op jit(solution)/shard_map/esf,df->esd/dot_general | solution.py:98
  199.3 5.7 %all-to-all-start.1 = ((bf16[32,24,2176]{2,1,0:T(8,128)(2,1)}), bf16[32,24,2176]{2,1,0:T(8,128)(2,1)}, u32[]{:S(2)}, u32[]{:S(2)}) async-start(bf16[32,24,2176]{2,1,0:T(8,128)(2,1)} %select_convert_fusion), calls=%async_computation.1 | async-start | bytes 6684672 | tf_op jit(solution)/shard_map/all_to_all | solution.py:69
  205.0 0.1 copy.43
  205.1 79.6 %all-to-all-done.1 = bf16[32,24,2176]{2,1,0:T(8,128)(2,1)} async-done(((bf16[32,24,2176]{2,1,0:T(8,128)(2,1)}), bf16[32,24,2176]{2,1,0:T(8,128)(2,1)}, u32[]{:S(2)}, u32[]{:S(2)}) %all-to-all-start.1) | async-done | bytes 3342368 | tf_op jit(solution)/shard_map/all_to_all | solution.py:69
  284.7 0.9 slice.114
  285.7 0.2 copy.48
  286.0 0.8 select_reduce_fusion
  286.9 0.6 fusion.35
  287.5 0.1 copy.46
  287.6 1.0 select_reduce_fusion.1
  288.6 1.4 fusion.26
  290.0 1.4 convolution_add_fusion.1
  291.4 3.6 %convolution_bitcast_fusion = f32[2,192,2176]{2,1,0:T(8,128)S(1)} fusion(bf16[2,192,32,24]{1,2,3,0:T(8,128)(2,1)S(1)} %copy-done.2, bf16[32,24,2176]{2,1,0:T(8,128)(2,1)} %all-to-all-done.1), kind=kOutput, calls=%fused_computation.6 | convolution fusion | flops 1283457024 | bytes 7274496 | tf_op jit(solution)/shard_map/ptes,esd->ptd/dot_general | solution.py:124
  295.1 2.5 fusion.21
  (26 shorter events, 0.4 us)
Async XLA Ops:
  0.6 185.1 %copy-start = (bf16[1,1,768,2048]{3,2,1,0:T(8,128)(2,1)S(1)}, bf16[1,1,768,2048]{3,2,1,0:T(8,128)(2,1)}, u32[]{:S(2)}) copy-start(bf16[1,1,768,2048]{3,2,1,0:T(8,128)(2,1)} %param.14) | copy-start | bytes 9437188
  0.6 19.7 %collective-permute-start = (bf16[1,192,2048]{2,1,0:T(8,128)(2,1)}, bf16[1,192,2048]{2,1,0:T(8,128)(2,1)}, u32[]{:S(2)}, u32[]{:S(2)}) collective-permute-start(bf16[1,192,2048]{2,1,0:T(8,128)(2,1)} %param.8), channel_id=1, source_target_pairs={{0,224},{32,0},{64,32},{96,64},{128,96},{160,128},{192,160},{224,1... | collective-permute-start | bytes 2359304 | tf_op jit(solution)/shard_map/ppermute | solution.py:9
  4.8 2.4 copy-start.3
  24.2 153.2 %all-to-all-start = ((bf16[32,24,4096]{2,1,0:T(8,128)(2,1)}), bf16[32,24,4096]{2,1,0:T(8,128)(2,1)}, u32[]{:S(2)}, u32[]{:S(2)}) async-start(bf16[32,24,4096]{2,1,0:T(8,128)(2,1)} %fusion.3), calls=%async_computation | async-start | bytes 12582912 | tf_op jit(solution)/shard_map/all_to_all | solution.py:69
  185.8 5.1 %copy-start.6 = (bf16[1,1,2048,768]{3,2,1,0:T(8,128)(2,1)S(1)}, bf16[1,1,2048,768]{3,2,1,0:T(8,128)(2,1)}, u32[]{:S(2)}) copy-start(bf16[1,1,2048,768]{3,2,1,0:T(8,128)(2,1)} %param.12) | copy-start | bytes 9437188
  190.9 3.7 %copy-start.7 = (bf16[1,1,2048,768]{3,2,1,0:T(8,128)(2,1)S(1)}, bf16[1,1,2048,768]{3,2,1,0:T(8,128)(2,1)}, u32[]{:S(2)}) copy-start(bf16[1,1,2048,768]{3,2,1,0:T(8,128)(2,1)} %param.13) | copy-start | bytes 9437188
  199.3 5.7 %copy-start.5 = (s32[1,192,8]{1,2,0:T(8,128)S(1)}, s32[1,192,8]{1,2,0:T(8,128)}, u32[]{:S(2)}) copy-start(s32[1,192,8]{1,2,0:T(8,128)} %param.10) | copy-start | bytes 18436
  199.3 87.5 %copy-start.4 = (f32[1,192,8]{1,2,0:T(8,128)S(1)}, f32[1,192,8]{1,2,0:T(8,128)}, u32[]{:S(2)}) copy-start(f32[1,192,8]{1,2,0:T(8,128)} %param.11) | copy-start | bytes 18436
  199.3 85.4 %all-to-all-start.1 = ((bf16[32,24,2176]{2,1,0:T(8,128)(2,1)}), bf16[32,24,2176]{2,1,0:T(8,128)(2,1)}, u32[]{:S(2)}, u32[]{:S(2)}) async-start(bf16[32,24,2176]{2,1,0:T(8,128)(2,1)} %select_convert_fusion), calls=%async_computation.1 | async-start | bytes 6684672 | tf_op jit(solution)/shard_map/all_to_all | solution.py:69
  287.6 3.9 %copy-start.2 = (bf16[2,192,32,24]{1,2,3,0:T(8,128)(2,1)S(1)}, bf16[2,192,32,24]{1,2,3,0:T(8,128)(2,1)}, u32[]{:S(2)}) copy-start(bf16[2,192,32,24]{1,2,3,0:T(8,128)(2,1)} %pad_maximum_fusion) | copy-start | bytes 1769476
  291.4 3.6 %copy-start.1 = (bf16[1,2048,128]{2,1,0:T(8,128)(2,1)S(1)}, bf16[1,2048,128]{2,1,0:T(8,128)(2,1)}, u32[]{:S(2)}) copy-start(bf16[1,2048,128]{2,1,0:T(8,128)(2,1)} %param.15) | copy-start | bytes 1572868

commit v10 on v9

--- a/solution.py
+++ b/solution.py
@@ -58,8 +58,8 @@
             chosen[:, None, None] == slot_ids[None, :, :], route_weight[:, k][:, None, None], 0.0
         )
     pack = pack.astype(jnp.bfloat16)
-    combine_parts = jnp.stack(split_bf16(combine, 2))
-    pack, combine_parts = lax.optimization_barrier((pack, combine_parts))
+    combine_bf16 = combine.astype(jnp.bfloat16)
+    pack, combine_bf16 = lax.optimization_barrier((pack, combine_bf16))
 
     def pack_rows(rows):
         sent = jnp.einsum("est,td->esd", pack, rows, preferred_element_type=jnp.float32)
@@ -121,10 +121,9 @@
         router_grad = router_grad + lax.dot_general(
             part, w_router, (((1,), (1,)), ((), ())), preferred_element_type=jnp.float32
         )
-    expert_both = jnp.einsum(
-        "ptes,esd->ptd", combine_parts, returned, preferred_element_type=jnp.float32
-    )
-    expert_sum = expert_both[0, :, :width_model] + expert_both[1, :, :width_model]
+    expert_sum = jnp.einsum(
+        "tes,esd->td", combine_bf16, returned, preferred_element_type=jnp.float32
+    )[:, :width_model]
     grad_in = (incoming.astype(jnp.float32) + expert_sum + router_grad).astype(jnp.bfloat16)
     return (grad_in[None], logit_grad[None])
 

time: 298 us -> 298 us (level)
  waiting for transfers between devices: 230 us -> 225 us
    ppermute x1, waiting for transfers between devices: 8.86 us -> 3.83 us  [from_behind(): lax.ppermute(shard, axis, [(i, (i + by) % size) for i in range(size)])]
  transfers between devices with their start and end apart: 3 -> 3, of which waited for: 3 -> 3; matrix products, arithmetic and copies ran while one was open for 4% -> 5% of each run, Pallas kernels for 0% -> 0%
where the time goes in v10:
time: 298 us; the launch traced here: 297 us
  waiting for transfers between devices  225 us (76%)
  matrix products  36.1 us (12%)
  starting transfers between devices  17.7 us (6%)
  other arithmetic  10.4 us (3%)
  local copies, waits for them, and re-layouts  7.12 us (2%)
    all_to_all x2, waiting for transfers between devices, exchange(): lax.all_to_all(block, 'expert', split_axis=0, concat_axis=0, tiled=True)  221 us
    all_to_all x2, starting transfers between devices, exchange(): lax.all_to_all(block, 'expert', split_axis=0, concat_axis=0, tiled=True)  17.6 us
    dot_general x1, matrix products, per_device(): jnp.einsum('esd,df->esf', inputs, jnp.concatenate([w_gate, w_up], axis=1)...  8.31 us
    dot_general x2, matrix products, pack_rows(): jnp.einsum('est,td->esd', pack, rows, preferred_element_type=jnp.float32)  6 us
  transfers between devices with their start and end apart: 3, of which 3 were waited for; matrix products, arithmetic and copies ran while one was open for 5% of the time, Pallas kernels for 0%

profile of v10, /device:TPU:33, one launch (start us, length us, event | category | flops | bytes accessed | tf_op | source)
XLA Modules:
  0.0 296.9 jit_solution(7795983962588730053)
XLA Ops:
  0.7 0.9 convert_reduce_fusion
  1.6 0.1 convolution_convert_fusion.2
  1.8 0.8 select_reduce_fusion.2
  2.6 0.7 add_select_fusion
  3.3 0.6 fusion.37
  3.9 0.7 exponential_reduce_fusion
  4.6 1.3 bitcast_divide_fusion
  5.9 0.7 copy.41
  6.6 1.4 add_convert_fusion.1
  8.0 1.0 fusion.36
  9.0 2.1 add_convert_fusion
  11.1 2.1 convolution_convert_fusion.1
  13.2 3.3 %concatenate.12 = bf16[32,24,4096]{2,1,0:T(8,128)(2,1)} pad(bf16[32,24,2048]{2,1,0:T(8,128)(2,1)S(1)} %convolution_convert_fusion.1, bf16[]{:T(256)} %constant.7.clone.1), padding=0_0x0_0x0_2048 | pad | bytes 9437186 | tf_op jit(solution)/shard_map/concatenate | solution.py:71
  16.5 3.8 %collective-permute-done = bf16[1,192,2048]{2,1,0:T(8,128)(2,1)} collective-permute-done((bf16[1,192,2048]{2,1,0:T(8,128)(2,1)}, bf16[1,192,2048]{2,1,0:T(8,128)(2,1)}, u32[]{:S(2)}, u32[]{:S(2)}) %collective-permute-start) | collective-permute-done | bytes 786464 | tf_op jit(solution)/shard_map/ppermute | solution.py:9
  20.3 3.9 %fusion.3 = bf16[32,24,4096]{2,1,0:T(8,128)(2,1)} fusion(bf16[32,24,4096]{2,1,0:T(8,128)(2,1)} %concatenate.12, bf16[32,24,192]{2,1,0:T(8,128)(2,1)S(1)} %add_convert_fusion.1, bf16[1,192,2048]{2,1,0:T(8,128)(2,1)} %collective-permute-done), kind=kOutput, calls=%fused_computation.8 | convolution fusion | flops 605552640 | bytes 4227072 | tf_op jit(solution)/shard_map/est,td->esd/dot_general | solution.py:65
  24.2 12.0 %all-to-all-start = ((bf16[32,24,4096]{2,1,0:T(8,128)(2,1)}), bf16[32,24,4096]{2,1,0:T(8,128)(2,1)}, u32[]{:S(2)}, u32[]{:S(2)}) async-start(bf16[32,24,4096]{2,1,0:T(8,128)(2,1)} %fusion.3), calls=%async_computation | async-start | bytes 12582912 | tf_op jit(solution)/shard_map/all_to_all | solution.py:69
  36.2 141.2 %all-to-all-done = bf16[32,24,4096]{2,1,0:T(8,128)(2,1)} async-done(((bf16[32,24,4096]{2,1,0:T(8,128)(2,1)}), bf16[32,24,4096]{2,1,0:T(8,128)(2,1)}, u32[]{:S(2)}, u32[]{:S(2)}) %all-to-all-start) | async-done | bytes 6291488 | tf_op jit(solution)/shard_map/all_to_all | solution.py:69
  177.4 8.3 %fusion = f32[32,24,1536]{2,1,0:T(8,128)S(1)} fusion(bf16[2048,768]{1,0:T(8,128)(2,1)} %bitcast.104, bf16[2048,768]{1,0:T(8,128)(2,1)} %bitcast.102, bf16[32,24,4096]{2,1,0:T(8,128)(2,1)} %all-to-all-done), kind=kOutput, calls=%fused_computation.2 | convolution fusion | flops 4844421120 | bytes 14155776 | tf_op jit(solution)/shard_map/esd,df->esf/dot_general | solution.py:82
  185.8 5.1 %multiply_reduce_fusion = (bf16[32,24]{1,0:T(8,128)(2,1)S(1)}, f32[32,24,768]{2,1,0:T(8,128)S(1)}) fusion(f32[32,24,1536]{2,1,0:T(8,128)S(1)} %fusion, bf16[1,1,768,2048]{3,2,1,0:T(8,128)(2,1)S(1)} %copy-done, bf16[32,24,4096]{2,1,0:T(8,128)(2,1)} %all-to-all-done), kind=kOutput, calls=%fused_computation.23 | convolution fusion | flops 2420047104 | bytes 13370880 | tf_op jit(solution)/shard_map/esd,fd->esf/dot_general | solution.py:88
  190.9 3.7 %fusion.5 = f32[32,24,2176]{2,1,0:T(8,128)S(1)} fusion(bf16[2048,768]{1,0:T(8,128)(2,1)S(1)} %bitcast.103, f32[32,24,768]{2,1,0:T(8,128)S(1)} %get-tuple-element.23, f32[32,24,1536]{2,1,0:T(8,128)S(1)} %fusion), kind=kOutput, calls=%fused_computation.11 | convolution fusion | flops 2572812288 | bytes 16908288 | tf_op jit(solution)/shard_map/esf,df->esd/dot_general | solution.py:96
  194.6 4.7 %select_convert_fusion = bf16[32,24,2176]{2,1,0:T(8,128)(2,1)} fusion(f32[32,24,2176]{2,1,0:T(8,128)S(1)} %fusion.5, bf16[2048,768]{1,0:T(8,128)(2,1)S(1)} %bitcast.105, bf16[32,24]{1,0:T(8,128)(2,1)S(1)} %get-tuple-element.22, pred[2176]{0:T(1024)(128)(4,1)S(1)} %iota_compare_fusion.4, f32[32,24,768]{2,1,0:T(8,128)S(1)} %get-tuple-element.23, ...), kind=kOutput, calls=%fused_computation | convolution fusion | flops 2573795328 | bytes 17902592 | tf_op jit(solution)/shard_map/esf,df->esd/dot_general | solution.py:98
  199.3 5.7 %all-to-all-start.1 = ((bf16[32,24,2176]{2,1,0:T(8,128)(2,1)}), bf16[32,24,2176]{2,1,0:T(8,128)(2,1)}, u32[]{:S(2)}, u32[]{:S(2)}) async-start(bf16[32,24,2176]{2,1,0:T(8,128)(2,1)} %select_convert_fusion), calls=%async_computation.1 | async-start | bytes 6684672 | tf_op jit(solution)/shard_map/all_to_all | solution.py:69
  205.1 79.7 %all-to-all-done.1 = bf16[32,24,2176]{2,1,0:T(8,128)(2,1)} async-done(((bf16[32,24,2176]{2,1,0:T(8,128)(2,1)}), bf16[32,24,2176]{2,1,0:T(8,128)(2,1)}, u32[]{:S(2)}, u32[]{:S(2)}) %all-to-all-start.1) | async-done | bytes 3342368 | tf_op jit(solution)/shard_map/all_to_all | solution.py:69
  284.8 0.9 slice.109
  285.7 0.2 copy.47
  286.1 0.8 select_reduce_fusion
  286.9 0.6 fusion.31
  287.7 1.0 select_reduce_fusion.1
  288.7 1.4 fusion.23
  290.1 1.4 convolution_add_fusion.1
  291.5 2.9 convolution_bitcast_fusion
  294.4 2.5 fusion.18
  (31 shorter events, 0.5 us)
Async XLA Ops:
  0.6 185.1 %copy-start = (bf16[1,1,768,2048]{3,2,1,0:T(8,128)(2,1)S(1)}, bf16[1,1,768,2048]{3,2,1,0:T(8,128)(2,1)}, u32[]{:S(2)}) copy-start(bf16[1,1,768,2048]{3,2,1,0:T(8,128)(2,1)} %param.14) | copy-start | bytes 9437188
  0.6 19.7 %collective-permute-start = (bf16[1,192,2048]{2,1,0:T(8,128)(2,1)}, bf16[1,192,2048]{2,1,0:T(8,128)(2,1)}, u32[]{:S(2)}, u32[]{:S(2)}) collective-permute-start(bf16[1,192,2048]{2,1,0:T(8,128)(2,1)} %param.8), channel_id=1, source_target_pairs={{0,224},{32,0},{64,32},{96,64},{128,96},{160,128},{192,160},{224,1... | collective-permute-start | bytes 2359304 | tf_op jit(solution)/shard_map/ppermute | solution.py:9
  3.3 3.3 %copy-start.5 = (s32[192,8]{0,1:T(8,128)}, s32[192,8]{0,1:T(8,128)S(1)}, u32[]{:S(2)}) copy-start(s32[192,8]{0,1:T(8,128)S(1)} %add_select_fusion) | copy-start | bytes 18436
  4.6 2.0 copy-start.7
  24.2 153.2 %all-to-all-start = ((bf16[32,24,4096]{2,1,0:T(8,128)(2,1)}), bf16[32,24,4096]{2,1,0:T(8,128)(2,1)}, u32[]{:S(2)}, u32[]{:S(2)}) async-start(bf16[32,24,4096]{2,1,0:T(8,128)(2,1)} %fusion.3), calls=%async_computation | async-start | bytes 12582912 | tf_op jit(solution)/shard_map/all_to_all | solution.py:69
  185.8 5.1 %copy-start.9 = (bf16[1,1,2048,768]{3,2,1,0:T(8,128)(2,1)S(1)}, bf16[1,1,2048,768]{3,2,1,0:T(8,128)(2,1)}, u32[]{:S(2)}) copy-start(bf16[1,1,2048,768]{3,2,1,0:T(8,128)(2,1)} %param.12) | copy-start | bytes 9437188
  190.9 3.7 %copy-start.10 = (bf16[1,1,2048,768]{3,2,1,0:T(8,128)(2,1)S(1)}, bf16[1,1,2048,768]{3,2,1,0:T(8,128)(2,1)}, u32[]{:S(2)}) copy-start(bf16[1,1,2048,768]{3,2,1,0:T(8,128)(2,1)} %param.13) | copy-start | bytes 9437188
  199.3 5.7 %copy-start.4 = (s32[1,192,8]{1,2,0:T(8,128)S(1)}, s32[1,192,8]{1,2,0:T(8,128)}, u32[]{:S(2)}) copy-start(s32[1,192,8]{1,2,0:T(8,128)} %param.10) | copy-start | bytes 18436
  199.3 86.8 %copy-start.6 = (s32[192,8]{0,1:T(8,128)S(1)}, s32[192,8]{0,1:T(8,128)}, u32[]{:S(2)}) copy-start(s32[192,8]{0,1:T(8,128)} %copy-done.5) | copy-start | bytes 18436
  199.3 87.6 %copy-start.3 = (f32[1,192,8]{1,2,0:T(8,128)S(1)}, f32[1,192,8]{1,2,0:T(8,128)}, u32[]{:S(2)}) copy-start(f32[1,192,8]{1,2,0:T(8,128)} %param.11) | copy-start | bytes 18436
  199.3 87.6 %copy-start.8 = (f32[192]{0:T(256)S(1)}, f32[192]{0:T(256)}, u32[]{:S(2)}) copy-start(f32[192]{0:T(256)} %copy-done.7) | copy-start | bytes 2308
  199.3 85.5 %all-to-all-start.1 = ((bf16[32,24,2176]{2,1,0:T(8,128)(2,1)}), bf16[32,24,2176]{2,1,0:T(8,128)(2,1)}, u32[]{:S(2)}, u32[]{:S(2)}) async-start(bf16[32,24,2176]{2,1,0:T(8,128)(2,1)} %select_convert_fusion), calls=%async_computation.1 | async-start | bytes 6684672 | tf_op jit(solution)/shard_map/all_to_all | solution.py:69
  287.7 3.9 %copy-start.2 = (bf16[192,32,24]{0,1,2:T(8,128)(2,1)S(1)}, bf16[192,32,24]{0,1,2:T(8,128)(2,1)}, u32[]{:S(2)}) copy-start(bf16[192,32,24]{0,1,2:T(8,128)(2,1)} %add_convert_fusion) | copy-start | bytes 884740
  291.5 2.9 copy-start.1

commit v11 on v9

--- a/solution.py
+++ b/solution.py
@@ -96,6 +96,11 @@
     pair_rows = jnp.einsum(
         "esf,df->esd", gate_grad, w_gate_wide, preferred_element_type=jnp.float32
     ) + jnp.einsum("esf,df->esd", up_grad, w_up_wide, preferred_element_type=jnp.float32)
+    own_column = lax.dynamic_index_in_dim(w_router, lax.axis_index("expert"), 1, False)
+    own_column = jnp.concatenate(
+        [own_column.astype(jnp.float32), jnp.zeros((lanes,), jnp.float32)]
+    )
+    pair_rows = pair_rows + pair_dots.astype(jnp.float32)[:, :, None] * own_column[None, None, :]
     lane_ids = jnp.arange(wide, dtype=jnp.int32)[None, None, :]
     pair_rows = jnp.where(
         lane_ids == width_model, pair_dots.astype(jnp.float32)[:, :, None], pair_rows
@@ -115,17 +120,18 @@
     center = jnp.sum(route_weight * weight_grad, axis=1, keepdims=True)
     logit_grad = route_weight * (weight_grad - center)
     matches = picks[:, :, None] == jnp.arange(every_expert, dtype=jnp.int32)[None, None, :]
-    dense_grad = jnp.sum(jnp.where(matches, logit_grad[:, :, None], 0.0), axis=1)
-    router_grad = jnp.zeros((token_count, width_model), jnp.float32)
-    for part in split_bf16(dense_grad, 3):
-        router_grad = router_grad + lax.dot_general(
+    dense_weight = jnp.sum(jnp.where(matches, route_weight[:, :, None], 0.0), axis=1)
+    mean_column = jnp.zeros((token_count, width_model), jnp.float32)
+    for part in split_bf16(dense_weight, 3):
+        mean_column = mean_column + lax.dot_general(
             part, w_router, (((1,), (1,)), ((), ())), preferred_element_type=jnp.float32
         )
     expert_both = jnp.einsum(
         "ptes,esd->ptd", combine_parts, returned, preferred_element_type=jnp.float32
     )
     expert_sum = expert_both[0, :, :width_model] + expert_both[1, :, :width_model]
-    grad_in = (incoming.astype(jnp.float32) + expert_sum + router_grad).astype(jnp.bfloat16)
+    router_rest = -center * mean_column
+    grad_in = (incoming.astype(jnp.float32) + expert_sum + router_rest).astype(jnp.bfloat16)
     return (grad_in[None], logit_grad[None])
 
 

time: 298 us -> 295 us (0.990)
  waiting for transfers between devices: 230 us -> 223 us
    all_to_all x2, waiting for transfers between devices: 221 us -> 215 us  [exchange(): lax.all_to_all(block, 'expert', split_axis=0, concat_axis=0, tiled=True)]
  transfers between devices with their start and end apart: 3 -> 3, of which waited for: 3 -> 3; matrix products, arithmetic and copies ran while one was open for 4% -> 6% of each run, Pallas kernels for 0% -> 0%
where the time goes in v11:
time: 295 us
  waiting for transfers between devices  223 us (76%)
  matrix products  37.6 us (13%)
  starting transfers between devices  17.7 us (6%)
  other arithmetic  8.65 us (3%)
  local copies, waits for them, and re-layouts  6.35 us (2%)
    all_to_all x2, waiting for transfers between devices, exchange(): lax.all_to_all(block, 'expert', split_axis=0, concat_axis=0, tiled=True)  215 us
    all_to_all x2, starting transfers between devices, exchange(): lax.all_to_all(block, 'expert', split_axis=0, concat_axis=0, tiled=True)  17.6 us
    ppermute x1, waiting for transfers between devices, from_behind(): lax.ppermute(shard, axis, [(i, (i + by) % size) for i in range(size)])  8.86 us
    dot_general x1, matrix products, per_device(): jnp.einsum('esd,df->esf', inputs, jnp.concatenate([w_gate, w_up], axis=1)...  8.31 us
    dot_general x3, matrix products, per_device(): lax.dot_general(part, w_router, (((1,), (1,)), ((), ())), preferred_eleme...  6.53 us
  transfers between devices with their start and end apart: 3, of which 3 were waited for; matrix products, arithmetic and copies ran while one was open for 6% of the time, Pallas kernels for 0%

profile of v11, /device:TPU:33, one launch (start us, length us, event | category | flops | bytes accessed | tf_op | source)
XLA Modules:
  0.0 294.6 jit_solution(16822899208766405672)
XLA Ops:
  0.7 0.9 convert_reduce_fusion
  1.6 0.1 convolution_convert_fusion.2
  1.8 0.8 select_reduce_fusion.2
  2.6 0.7 add_select_fusion
  3.3 0.7 exponential_reduce_fusion
  4.0 0.7 bitcast_divide_fusion
  4.8 0.7 subtract_convert_fusion
  5.5 1.0 pad_maximum_fusion
  6.5 0.7 add_convert_fusion
  7.2 1.0 convolution_convert_fusion.1
  8.2 3.3 %concatenate.17 = bf16[32,24,4096]{2,1,0:T(8,128)(2,1)} pad(bf16[32,24,2048]{2,1,0:T(8,128)(2,1)S(1)} %convolution_convert_fusion.1, bf16[]{:T(256)} %constant.9.clone.1), padding=0_0x0_0x0_2048 | pad | bytes 9437186 | tf_op jit(solution)/shard_map/concatenate | solution.py:71
  11.5 8.9 %collective-permute-done = bf16[1,192,2048]{2,1,0:T(8,128)(2,1)} collective-permute-done((bf16[1,192,2048]{2,1,0:T(8,128)(2,1)}, bf16[1,192,2048]{2,1,0:T(8,128)(2,1)}, u32[]{:S(2)}, u32[]{:S(2)}) %collective-permute-start) | collective-permute-done | bytes 786464 | tf_op jit(solution)/shard_map/ppermute | solution.py:9
  20.3 3.9 %fusion.3 = bf16[32,24,4096]{2,1,0:T(8,128)(2,1)} fusion(bf16[32,24,4096]{2,1,0:T(8,128)(2,1)} %concatenate.17, bf16[32,24,192]{2,1,0:T(8,128)(2,1)S(1)} %add_convert_fusion, bf16[1,192,2048]{2,1,0:T(8,128)(2,1)} %collective-permute-done), kind=kOutput, calls=%fused_computation.8 | convolution fusion | flops 605552640 | bytes 4227072 | tf_op jit(solution)/shard_map/est,td->esd/dot_general | solution.py:65
  24.2 12.0 %all-to-all-start = ((bf16[32,24,4096]{2,1,0:T(8,128)(2,1)}), bf16[32,24,4096]{2,1,0:T(8,128)(2,1)}, u32[]{:S(2)}, u32[]{:S(2)}) async-start(bf16[32,24,4096]{2,1,0:T(8,128)(2,1)} %fusion.3), calls=%async_computation | async-start | bytes 12582912 | tf_op jit(solution)/shard_map/all_to_all | solution.py:69
  36.2 1.4 dynamic-slice_reduce_fusion
  37.7 139.8 %all-to-all-done = bf16[32,24,4096]{2,1,0:T(8,128)(2,1)} async-done(((bf16[32,24,4096]{2,1,0:T(8,128)(2,1)}), bf16[32,24,4096]{2,1,0:T(8,128)(2,1)}, u32[]{:S(2)}, u32[]{:S(2)}) %all-to-all-start) | async-done | bytes 6291488 | tf_op jit(solution)/shard_map/all_to_all | solution.py:69
  177.4 8.3 %fusion = f32[32,24,1536]{2,1,0:T(8,128)S(1)} fusion(bf16[2048,768]{1,0:T(8,128)(2,1)} %bitcast.114, bf16[2048,768]{1,0:T(8,128)(2,1)} %bitcast.112, bf16[32,24,4096]{2,1,0:T(8,128)(2,1)} %all-to-all-done), kind=kOutput, calls=%fused_computation.2 | convolution fusion | flops 4844421120 | bytes 14155776 | tf_op jit(solution)/shard_map/esd,df->esf/dot_general | solution.py:82
  185.8 5.1 %multiply_reduce_fusion = (bf16[32,24]{1,0:T(8,128)(2,1)S(1)}, f32[32,24,768]{2,1,0:T(8,128)S(1)}) fusion(f32[32,24,1536]{2,1,0:T(8,128)S(1)} %fusion, bf16[1,1,768,2048]{3,2,1,0:T(8,128)(2,1)S(1)} %copy-done, bf16[32,24,4096]{2,1,0:T(8,128)(2,1)} %all-to-all-done), kind=kOutput, calls=%fused_computation.25 | convolution fusion | flops 2420047104 | bytes 13370880 | tf_op jit(solution)/shard_map/esd,fd->esf/dot_general | solution.py:88
  190.9 3.7 %fusion.6 = f32[32,24,2176]{2,1,0:T(8,128)S(1)} fusion(bf16[2048,768]{1,0:T(8,128)(2,1)S(1)} %bitcast.113, f32[32,24,768]{2,1,0:T(8,128)S(1)} %get-tuple-element.25, f32[32,24,1536]{2,1,0:T(8,128)S(1)} %fusion), kind=kOutput, calls=%fused_computation.12 | convolution fusion | flops 2572812288 | bytes 16908288 | tf_op jit(solution)/shard_map/esf,df->esd/dot_general | solution.py:96
  194.7 5.0 %select_convert_fusion = bf16[32,24,2176]{2,1,0:T(8,128)(2,1)} fusion(f32[32,24,2176]{2,1,0:T(8,128)S(1)} %fusion.6, f32[2176]{0:T(1024)S(1)} %pad_convert_fusion, bf16[2048,768]{1,0:T(8,128)(2,1)S(1)} %bitcast.115, f32[32,24]{1,0:T(8,128)S(1)} %convert_element_type.228, pred[2176]{0:T(1024)(128)(4,1)S(1)} %iota_compare_fusion.4, ...), kind=kOutput, calls=%fused_computation | convolution fusion | flops 2578808832 | bytes 17923072 | tf_op jit(solution)/shard_map/esf,df->esd/dot_general | solution.py:98
  199.6 5.7 %all-to-all-start.1 = ((bf16[32,24,2176]{2,1,0:T(8,128)(2,1)}), bf16[32,24,2176]{2,1,0:T(8,128)(2,1)}, u32[]{:S(2)}, u32[]{:S(2)}) async-start(bf16[32,24,2176]{2,1,0:T(8,128)(2,1)} %select_convert_fusion), calls=%async_computation.1 | async-start | bytes 6684672 | tf_op jit(solution)/shard_map/all_to_all | solution.py:69
  205.3 0.1 copy.46
  205.5 1.0 select_reduce_fusion.1
  206.5 1.4 fusion.27
  207.9 2.6 convolution_add_fusion.1
  210.5 74.8 %all-to-all-done.1 = bf16[32,24,2176]{2,1,0:T(8,128)(2,1)} async-done(((bf16[32,24,2176]{2,1,0:T(8,128)(2,1)}), bf16[32,24,2176]{2,1,0:T(8,128)(2,1)}, u32[]{:S(2)}, u32[]{:S(2)}) %all-to-all-start.1) | async-done | bytes 3342368 | tf_op jit(solution)/shard_map/all_to_all | solution.py:69
  285.3 0.9 slice.114
  286.2 0.2 copy.48
  286.5 0.8 select_reduce_fusion
  287.4 0.6 fusion.34
  288.0 3.9 %convolution_bitcast_fusion = f32[2,192,2176]{2,1,0:T(8,128)S(1)} fusion(bf16[2,192,32,24]{1,2,3,0:T(8,128)(2,1)} %pad_maximum_fusion, bf16[32,24,2176]{2,1,0:T(8,128)(2,1)} %all-to-all-done.1), kind=kOutput, calls=%fused_computation.6 | convolution fusion | flops 1283457024 | bytes 7274496 | tf_op jit(solution)/shard_map/ptes,esd->ptd/dot_general | solution.py:129
  292.0 2.6 fusion.22
  (29 shorter events, 0.5 us)
Async XLA Ops:
  0.6 185.1 %copy-start = (bf16[1,1,768,2048]{3,2,1,0:T(8,128)(2,1)S(1)}, bf16[1,1,768,2048]{3,2,1,0:T(8,128)(2,1)}, u32[]{:S(2)}) copy-start(bf16[1,1,768,2048]{3,2,1,0:T(8,128)(2,1)} %param.14) | copy-start | bytes 9437188
  0.6 19.7 %collective-permute-start = (bf16[1,192,2048]{2,1,0:T(8,128)(2,1)}, bf16[1,192,2048]{2,1,0:T(8,128)(2,1)}, u32[]{:S(2)}, u32[]{:S(2)}) collective-permute-start(bf16[1,192,2048]{2,1,0:T(8,128)(2,1)} %param.8), channel_id=1, source_target_pairs={{0,224},{32,0},{64,32},{96,64},{128,96},{160,128},{192,160},{224,1... | collective-permute-start | bytes 2359304 | tf_op jit(solution)/shard_map/ppermute | solution.py:9
  4.8 2.4 copy-start.3
  24.2 153.2 %all-to-all-start = ((bf16[32,24,4096]{2,1,0:T(8,128)(2,1)}), bf16[32,24,4096]{2,1,0:T(8,128)(2,1)}, u32[]{:S(2)}, u32[]{:S(2)}) async-start(bf16[32,24,4096]{2,1,0:T(8,128)(2,1)} %fusion.3), calls=%async_computation | async-start | bytes 12582912 | tf_op jit(solution)/shard_map/all_to_all | solution.py:69
  185.8 5.1 %copy-start.6 = (bf16[1,1,2048,768]{3,2,1,0:T(8,128)(2,1)S(1)}, bf16[1,1,2048,768]{3,2,1,0:T(8,128)(2,1)}, u32[]{:S(2)}) copy-start(bf16[1,1,2048,768]{3,2,1,0:T(8,128)(2,1)} %param.12) | copy-start | bytes 9437188
  190.9 3.7 %copy-start.7 = (bf16[1,1,2048,768]{3,2,1,0:T(8,128)(2,1)S(1)}, bf16[1,1,2048,768]{3,2,1,0:T(8,128)(2,1)}, u32[]{:S(2)}) copy-start(bf16[1,1,2048,768]{3,2,1,0:T(8,128)(2,1)} %param.13) | copy-start | bytes 9437188
  199.6 5.8 %copy-start.5 = (s32[1,192,8]{1,2,0:T(8,128)S(1)}, s32[1,192,8]{1,2,0:T(8,128)}, u32[]{:S(2)}) copy-start(s32[1,192,8]{1,2,0:T(8,128)} %param.10) | copy-start | bytes 18436
  199.6 85.6 %all-to-all-start.1 = ((bf16[32,24,2176]{2,1,0:T(8,128)(2,1)}), bf16[32,24,2176]{2,1,0:T(8,128)(2,1)}, u32[]{:S(2)}, u32[]{:S(2)}) async-start(bf16[32,24,2176]{2,1,0:T(8,128)(2,1)} %select_convert_fusion), calls=%async_computation.1 | async-start | bytes 6684672 | tf_op jit(solution)/shard_map/all_to_all | solution.py:69
  206.5 80.8 %copy-start.4 = (f32[1,192,8]{1,2,0:T(8,128)S(1)}, f32[1,192,8]{1,2,0:T(8,128)}, u32[]{:S(2)}) copy-start(f32[1,192,8]{1,2,0:T(8,128)} %param.11) | copy-start | bytes 18436
  288.0 4.0 %copy-start.1 = (bf16[1,2048,128]{2,1,0:T(8,128)(2,1)S(1)}, bf16[1,2048,128]{2,1,0:T(8,128)(2,1)}, u32[]{:S(2)}) copy-start(bf16[1,2048,128]{2,1,0:T(8,128)(2,1)} %param.15) | copy-start | bytes 1572868
  288.0 4.0 %copy-start.2 = (f32[192,2048]{1,0:T(8,128)S(1)}, f32[192,2048]{1,0:T(8,128)}, u32[]{:S(2)}) copy-start(f32[192,2048]{1,0:T(8,128)} %convolution_add_fusion.1) | copy-start | bytes 4718596

commit v12 on v11

--- a/solution.py
+++ b/solution.py
@@ -58,8 +58,8 @@
             chosen[:, None, None] == slot_ids[None, :, :], route_weight[:, k][:, None, None], 0.0
         )
     pack = pack.astype(jnp.bfloat16)
-    combine_parts = jnp.stack(split_bf16(combine, 2))
-    pack, combine_parts = lax.optimization_barrier((pack, combine_parts))
+    combine_bf16 = combine.astype(jnp.bfloat16)
+    pack, combine_bf16 = lax.optimization_barrier((pack, combine_bf16))
 
     def pack_rows(rows):
         sent = jnp.einsum("est,td->esd", pack, rows, preferred_element_type=jnp.float32)
@@ -126,10 +126,9 @@
         mean_column = mean_column + lax.dot_general(
             part, w_router, (((1,), (1,)), ((), ())), preferred_element_type=jnp.float32
         )
-    expert_both = jnp.einsum(
-        "ptes,esd->ptd", combine_parts, returned, preferred_element_type=jnp.float32
-    )
-    expert_sum = expert_both[0, :, :width_model] + expert_both[1, :, :width_model]
+    expert_sum = jnp.einsum(
+        "tes,esd->td", combine_bf16, returned, preferred_element_type=jnp.float32
+    )[:, :width_model]
     router_rest = -center * mean_column
     grad_in = (incoming.astype(jnp.float32) + expert_sum + router_rest).astype(jnp.bfloat16)
     return (grad_in[None], logit_grad[None])

time: 295 us -> 294 us (level)
  no operation moved by 1% of the time
where the time goes in v12:
time: 294 us
  waiting for transfers between devices  223 us (76%)
  matrix products  37.8 us (13%)
  starting transfers between devices  17.7 us (6%)
  other arithmetic  8.34 us (3%)
  local copies, waits for them, and re-layouts  6.34 us (2%)
    all_to_all x2, waiting for transfers between devices, exchange(): lax.all_to_all(block, 'expert', split_axis=0, concat_axis=0, tiled=True)  215 us
    all_to_all x2, starting transfers between devices, exchange(): lax.all_to_all(block, 'expert', split_axis=0, concat_axis=0, tiled=True)  17.6 us
    dot_general x1, matrix products, per_device(): jnp.einsum('esd,df->esf', inputs, jnp.concatenate([w_gate, w_up], axis=1)...  8.31 us
    ppermute x1, waiting for transfers between devices, from_behind(): lax.ppermute(shard, axis, [(i, (i + by) % size) for i in range(size)])  8.05 us
    dot_general x3, matrix products, per_device(): lax.dot_general(part, w_router, (((1,), (1,)), ((), ())), preferred_eleme...  6.47 us
    dot_general x2, matrix products, pack_rows(): jnp.einsum('est,td->esd', pack, rows, preferred_element_type=jnp.float32)  6 us
  transfers between devices with their start and end apart: 3, of which 3 were waited for; matrix products, arithmetic and copies ran while one was open for 6% of the time, Pallas kernels for 0%

profile of v12, /device:TPU:33, one launch (start us, length us, event | category | flops | bytes accessed | tf_op | source)
XLA Modules:
  0.0 293.6 jit_solution(15232805978217179018)
XLA Ops:
  0.7 0.9 convert_reduce_fusion
  1.6 0.1 convolution_convert_fusion.2
  1.8 0.8 select_reduce_fusion.2
  2.6 0.7 add_select_fusion
  3.3 0.7 exponential_reduce_fusion
  4.0 0.7 bitcast_divide_fusion
  4.8 0.7 add_convert_fusion.1
  5.5 1.4 add_convert_fusion
  6.9 2.1 convolution_convert_fusion.1
  9.0 3.3 %concatenate.17 = bf16[32,24,4096]{2,1,0:T(8,128)(2,1)} pad(bf16[32,24,2048]{2,1,0:T(8,128)(2,1)S(1)} %convolution_convert_fusion.1, bf16[]{:T(256)} %constant.9.clone.1), padding=0_0x0_0x0_2048 | pad | bytes 9437186 | tf_op jit(solution)/shard_map/concatenate | solution.py:71
  12.3 8.1 %collective-permute-done = bf16[1,192,2048]{2,1,0:T(8,128)(2,1)} collective-permute-done((bf16[1,192,2048]{2,1,0:T(8,128)(2,1)}, bf16[1,192,2048]{2,1,0:T(8,128)(2,1)}, u32[]{:S(2)}, u32[]{:S(2)}) %collective-permute-start) | collective-permute-done | bytes 786464 | tf_op jit(solution)/shard_map/ppermute | solution.py:9
  20.3 3.9 %fusion.3 = bf16[32,24,4096]{2,1,0:T(8,128)(2,1)} fusion(bf16[32,24,4096]{2,1,0:T(8,128)(2,1)} %concatenate.17, bf16[32,24,192]{2,1,0:T(8,128)(2,1)S(1)} %add_convert_fusion.1, bf16[1,192,2048]{2,1,0:T(8,128)(2,1)} %collective-permute-done), kind=kOutput, calls=%fused_computation.8 | convolution fusion | flops 605552640 | bytes 4227072 | tf_op jit(solution)/shard_map/est,td->esd/dot_general | solution.py:65
  24.2 12.0 %all-to-all-start = ((bf16[32,24,4096]{2,1,0:T(8,128)(2,1)}), bf16[32,24,4096]{2,1,0:T(8,128)(2,1)}, u32[]{:S(2)}, u32[]{:S(2)}) async-start(bf16[32,24,4096]{2,1,0:T(8,128)(2,1)} %fusion.3), calls=%async_computation | async-start | bytes 12582912 | tf_op jit(solution)/shard_map/all_to_all | solution.py:69
  36.2 1.4 dynamic-slice_reduce_fusion
  37.7 139.8 %all-to-all-done = bf16[32,24,4096]{2,1,0:T(8,128)(2,1)} async-done(((bf16[32,24,4096]{2,1,0:T(8,128)(2,1)}), bf16[32,24,4096]{2,1,0:T(8,128)(2,1)}, u32[]{:S(2)}, u32[]{:S(2)}) %all-to-all-start) | async-done | bytes 6291488 | tf_op jit(solution)/shard_map/all_to_all | solution.py:69
  177.4 8.3 %fusion = f32[32,24,1536]{2,1,0:T(8,128)S(1)} fusion(bf16[2048,768]{1,0:T(8,128)(2,1)} %bitcast.100, bf16[2048,768]{1,0:T(8,128)(2,1)} %bitcast.98, bf16[32,24,4096]{2,1,0:T(8,128)(2,1)} %all-to-all-done), kind=kOutput, calls=%fused_computation.2 | convolution fusion | flops 4844421120 | bytes 14155776 | tf_op jit(solution)/shard_map/esd,df->esf/dot_general | solution.py:82
  185.8 5.1 %multiply_reduce_fusion = (bf16[32,24]{1,0:T(8,128)(2,1)S(1)}, f32[32,24,768]{2,1,0:T(8,128)S(1)}) fusion(f32[32,24,1536]{2,1,0:T(8,128)S(1)} %fusion, bf16[1,1,768,2048]{3,2,1,0:T(8,128)(2,1)S(1)} %copy-done, bf16[32,24,4096]{2,1,0:T(8,128)(2,1)} %all-to-all-done), kind=kOutput, calls=%fused_computation.24 | convolution fusion | flops 2420047104 | bytes 13370880 | tf_op jit(solution)/shard_map/esd,fd->esf/dot_general | solution.py:88
  190.9 3.7 %fusion.5 = f32[32,24,2176]{2,1,0:T(8,128)S(1)} fusion(bf16[2048,768]{1,0:T(8,128)(2,1)S(1)} %bitcast.99, f32[32,24,768]{2,1,0:T(8,128)S(1)} %get-tuple-element.23, f32[32,24,1536]{2,1,0:T(8,128)S(1)} %fusion), kind=kOutput, calls=%fused_computation.11 | convolution fusion | flops 2572812288 | bytes 16908288 | tf_op jit(solution)/shard_map/esf,df->esd/dot_general | solution.py:96
  194.7 5.0 %select_convert_fusion = bf16[32,24,2176]{2,1,0:T(8,128)(2,1)} fusion(f32[32,24,2176]{2,1,0:T(8,128)S(1)} %fusion.5, f32[2176]{0:T(1024)S(1)} %pad_convert_fusion, bf16[2048,768]{1,0:T(8,128)(2,1)S(1)} %bitcast.101, f32[32,24]{1,0:T(8,128)S(1)} %convert_element_type.193, pred[2176]{0:T(1024)(128)(4,1)S(1)} %iota_compare_fusion.4, ...), kind=kOutput, calls=%fused_computation | convolution fusion | flops 2578808832 | bytes 17923072 | tf_op jit(solution)/shard_map/esf,df->esd/dot_general | solution.py:98
  199.6 5.7 %all-to-all-start.1 = ((bf16[32,24,2176]{2,1,0:T(8,128)(2,1)}), bf16[32,24,2176]{2,1,0:T(8,128)(2,1)}, u32[]{:S(2)}, u32[]{:S(2)}) async-start(bf16[32,24,2176]{2,1,0:T(8,128)(2,1)} %select_convert_fusion), calls=%async_computation.1 | async-start | bytes 6684672 | tf_op jit(solution)/shard_map/all_to_all | solution.py:69
  205.3 0.1 copy.46
  205.4 0.1 copy.45
  205.5 1.0 select_reduce_fusion.1
  206.5 1.4 fusion.24
  207.9 2.6 convolution_add_fusion.1
  210.5 74.8 %all-to-all-done.1 = bf16[32,24,2176]{2,1,0:T(8,128)(2,1)} async-done(((bf16[32,24,2176]{2,1,0:T(8,128)(2,1)}), bf16[32,24,2176]{2,1,0:T(8,128)(2,1)}, u32[]{:S(2)}, u32[]{:S(2)}) %all-to-all-start.1) | async-done | bytes 3342368 | tf_op jit(solution)/shard_map/all_to_all | solution.py:69
  285.3 0.9 slice.109
  286.2 0.2 copy.47
  286.5 0.8 select_reduce_fusion
  287.4 0.6 fusion.30
  288.0 3.1 %convolution_bitcast_fusion = f32[192,2176]{1,0:T(8,128)S(1)} fusion(bf16[192,32,24]{0,1,2:T(8,128)(2,1)} %add_convert_fusion, bf16[32,24,2176]{2,1,0:T(8,128)(2,1)} %all-to-all-done.1), kind=kOutput, calls=%fused_computation.6 | convolution fusion | flops 641728512 | bytes 5308416 | tf_op jit(solution)/shard_map/tes,esd->td/dot_general | solution.py:129
  291.1 2.5 fusion.19
  (26 shorter events, 0.4 us)
Async XLA Ops:
  0.6 185.1 %copy-start = (bf16[1,1,768,2048]{3,2,1,0:T(8,128)(2,1)S(1)}, bf16[1,1,768,2048]{3,2,1,0:T(8,128)(2,1)}, u32[]{:S(2)}) copy-start(bf16[1,1,768,2048]{3,2,1,0:T(8,128)(2,1)} %param.14) | copy-start | bytes 9437188
  0.6 19.7 %collective-permute-start = (bf16[1,192,2048]{2,1,0:T(8,128)(2,1)}, bf16[1,192,2048]{2,1,0:T(8,128)(2,1)}, u32[]{:S(2)}, u32[]{:S(2)}) collective-permute-start(bf16[1,192,2048]{2,1,0:T(8,128)(2,1)} %param.8), channel_id=1, source_target_pairs={{0,224},{32,0},{64,32},{96,64},{128,96},{160,128},{192,160},{224,1... | collective-permute-start | bytes 2359304 | tf_op jit(solution)/shard_map/ppermute | solution.py:9
  24.2 153.2 %all-to-all-start = ((bf16[32,24,4096]{2,1,0:T(8,128)(2,1)}), bf16[32,24,4096]{2,1,0:T(8,128)(2,1)}, u32[]{:S(2)}, u32[]{:S(2)}) async-start(bf16[32,24,4096]{2,1,0:T(8,128)(2,1)} %fusion.3), calls=%async_computation | async-start | bytes 12582912 | tf_op jit(solution)/shard_map/all_to_all | solution.py:69
  185.8 5.1 %copy-start.5 = (bf16[1,1,2048,768]{3,2,1,0:T(8,128)(2,1)S(1)}, bf16[1,1,2048,768]{3,2,1,0:T(8,128)(2,1)}, u32[]{:S(2)}) copy-start(bf16[1,1,2048,768]{3,2,1,0:T(8,128)(2,1)} %param.12) | copy-start | bytes 9437188
  190.9 3.7 %copy-start.6 = (bf16[1,1,2048,768]{3,2,1,0:T(8,128)(2,1)S(1)}, bf16[1,1,2048,768]{3,2,1,0:T(8,128)(2,1)}, u32[]{:S(2)}) copy-start(bf16[1,1,2048,768]{3,2,1,0:T(8,128)(2,1)} %param.13) | copy-start | bytes 9437188
  199.6 5.8 %copy-start.4 = (s32[1,192,8]{1,2,0:T(8,128)S(1)}, s32[1,192,8]{1,2,0:T(8,128)}, u32[]{:S(2)}) copy-start(s32[1,192,8]{1,2,0:T(8,128)} %param.10) | copy-start | bytes 18436
  199.6 85.7 %all-to-all-start.1 = ((bf16[32,24,2176]{2,1,0:T(8,128)(2,1)}), bf16[32,24,2176]{2,1,0:T(8,128)(2,1)}, u32[]{:S(2)}, u32[]{:S(2)}) async-start(bf16[32,24,2176]{2,1,0:T(8,128)(2,1)} %select_convert_fusion), calls=%async_computation.1 | async-start | bytes 6684672 | tf_op jit(solution)/shard_map/all_to_all | solution.py:69
  206.5 80.8 %copy-start.3 = (f32[1,192,8]{1,2,0:T(8,128)S(1)}, f32[1,192,8]{1,2,0:T(8,128)}, u32[]{:S(2)}) copy-start(f32[1,192,8]{1,2,0:T(8,128)} %param.11) | copy-start | bytes 18436
  288.0 3.1 %copy-start.1 = (bf16[1,2048,128]{2,1,0:T(8,128)(2,1)S(1)}, bf16[1,2048,128]{2,1,0:T(8,128)(2,1)}, u32[]{:S(2)}) copy-start(bf16[1,2048,128]{2,1,0:T(8,128)(2,1)} %param.15) | copy-start | bytes 1572868
  288.0 3.1 %copy-start.2 = (f32[192,2048]{1,0:T(8,128)S(1)}, f32[192,2048]{1,0:T(8,128)}, u32[]{:S(2)}) copy-start(f32[192,2048]{1,0:T(8,128)} %convolution_add_fusion.1) | copy-start | bytes 4718596

commit v13 on v12

--- a/solution.py
+++ b/solution.py
@@ -59,7 +59,10 @@
         )
     pack = pack.astype(jnp.bfloat16)
     combine_bf16 = combine.astype(jnp.bfloat16)
-    pack, combine_bf16 = lax.optimization_barrier((pack, combine_bf16))
+    pick_slot = (
+        slot_index.reshape(-1)[:, None, None] == slot_ids[None, :, :]
+    ).astype(jnp.bfloat16)
+    pack, combine_bf16, pick_slot = lax.optimization_barrier((pack, combine_bf16, pick_slot))
 
     def pack_rows(rows):
         sent = jnp.einsum("est,td->esd", pack, rows, preferred_element_type=jnp.float32)
@@ -106,17 +109,9 @@
         lane_ids == width_model, pair_dots.astype(jnp.float32)[:, :, None], pair_rows
     )
     returned = exchange(pair_rows.astype(jnp.bfloat16))
-    returned_dots = returned[:, :, width_model]
-
-    slot_dots = returned_dots.astype(jnp.float32)
-    weight_grad = jnp.sum(
-        jnp.where(
-            slot_index[:, :, None, None] == slot_ids[None, None, :, :],
-            slot_dots[None, None, :, :],
-            0.0,
-        ),
-        axis=(2, 3),
-    )
+    weight_grad = jnp.einsum(
+        "pes,esl->pl", pick_slot, returned[:, :, width_model:], preferred_element_type=jnp.float32
+    )[:, 0].reshape(token_count, top_count)
     center = jnp.sum(route_weight * weight_grad, axis=1, keepdims=True)
     logit_grad = route_weight * (weight_grad - center)
     matches = picks[:, :, None] == jnp.arange(every_expert, dtype=jnp.int32)[None, None, :]

time: 294 us -> 296 us (level)
  waiting for transfers between devices: 223 us -> 218 us
  local copies, waits for them, and re-layouts: 6.34 us -> 9.39 us
    ppermute x1, waiting for transfers between devices: 8.05 us -> 3.75 us  [from_behind(): lax.ppermute(shard, axis, [(i, (i + by) % size) for i in range(size)])]
  transfers between devices with their start and end apart: 3 -> 3, of which waited for: 3 -> 3; matrix products, arithmetic and copies ran while one was open for 6% -> 8% of each run, Pallas kernels for 0% -> 0%
where the time goes in v13:
time: 296 us; the launch traced here: 295 us
  waiting for transfers between devices  218 us (74%)
  matrix products  38.9 us (13%)
  starting transfers between devices  17.7 us (6%)
  other arithmetic  9.97 us (3%)
  local copies, waits for them, and re-layouts  9.39 us (3%)
    all_to_all x2, waiting for transfers between devices, exchange(): lax.all_to_all(block, 'expert', split_axis=0, concat_axis=0, tiled=True)  215 us
    all_to_all x2, starting transfers between devices, exchange(): lax.all_to_all(block, 'expert', split_axis=0, concat_axis=0, tiled=True)  17.6 us
    dot_general x1, matrix products, per_device(): jnp.einsum('esd,df->esf', inputs, jnp.concatenate([w_gate, w_up], axis=1)...  8.31 us
    dot_general x3, matrix products, per_device(): lax.dot_general(part, w_router, (((1,), (1,)), ((), ())), preferred_eleme...  6.46 us
  transfers between devices with their start and end apart: 3, of which 3 were waited for; matrix products, arithmetic and copies ran while one was open for 8% of the time, Pallas kernels for 0%

profile of v13, /device:TPU:33, one launch (start us, length us, event | category | flops | bytes accessed | tf_op | source)
XLA Modules:
  0.0 295.3 jit_solution(12268101318863153637)
XLA Ops:
  0.7 0.9 convert_reduce_fusion
  1.8 0.8 select_reduce_fusion.1
  2.6 0.7 add_select_fusion.1
  3.4 0.7 broadcast_multiply_fusion
  4.1 0.7 broadcast_compare_fusion
  4.8 0.8 copy.42
  5.8 1.1 slice_reduce_fusion.7
  7.7 0.7 add_convert_fusion.1
  8.3 2.1 add_convert_fusion
  10.4 1.9 compare_convert_fusion
  12.3 1.0 convolution_convert_fusion.1
  13.3 3.3 %concatenate.17 = bf16[32,24,4096]{2,1,0:T(8,128)(2,1)} pad(bf16[32,24,2048]{2,1,0:T(8,128)(2,1)S(1)} %convolution_convert_fusion.1, bf16[]{:T(256)} %constant.8.clone.1), padding=0_0x0_0x0_2048 | pad | bytes 9437186 | tf_op jit(solution)/shard_map/concatenate | solution.py:74
  16.6 3.7 %collective-permute-done = bf16[1,192,2048]{2,1,0:T(8,128)(2,1)} collective-permute-done((bf16[1,192,2048]{2,1,0:T(8,128)(2,1)}, bf16[1,192,2048]{2,1,0:T(8,128)(2,1)}, u32[]{:S(2)}, u32[]{:S(2)}) %collective-permute-start) | collective-permute-done | bytes 786464 | tf_op jit(solution)/shard_map/ppermute | solution.py:9
  20.3 3.9 %fusion.3 = bf16[32,24,4096]{2,1,0:T(8,128)(2,1)} fusion(bf16[32,24,4096]{2,1,0:T(8,128)(2,1)} %concatenate.17, bf16[32,24,192]{2,1,0:T(8,128)(2,1)S(1)} %add_convert_fusion.1, bf16[1,192,2048]{2,1,0:T(8,128)(2,1)} %collective-permute-done), kind=kOutput, calls=%fused_computation.8 | convolution fusion | flops 605552640 | bytes 4227072 | tf_op jit(solution)/shard_map/est,td->esd/dot_general | solution.py:68
  24.2 12.0 %all-to-all-start = ((bf16[32,24,4096]{2,1,0:T(8,128)(2,1)}), bf16[32,24,4096]{2,1,0:T(8,128)(2,1)}, u32[]{:S(2)}, u32[]{:S(2)}) async-start(bf16[32,24,4096]{2,1,0:T(8,128)(2,1)} %fusion.3), calls=%async_computation | async-start | bytes 12582912 | tf_op jit(solution)/shard_map/all_to_all | solution.py:72
  36.2 1.4 dynamic-slice_reduce_fusion
  37.7 139.8 %all-to-all-done = bf16[32,24,4096]{2,1,0:T(8,128)(2,1)} async-done(((bf16[32,24,4096]{2,1,0:T(8,128)(2,1)}), bf16[32,24,4096]{2,1,0:T(8,128)(2,1)}, u32[]{:S(2)}, u32[]{:S(2)}) %all-to-all-start) | async-done | bytes 6291488 | tf_op jit(solution)/shard_map/all_to_all | solution.py:72
  177.4 8.3 %fusion = f32[32,24,1536]{2,1,0:T(8,128)S(1)} fusion(bf16[2048,768]{1,0:T(8,128)(2,1)} %bitcast.80, bf16[2048,768]{1,0:T(8,128)(2,1)} %bitcast.78, bf16[32,24,4096]{2,1,0:T(8,128)(2,1)} %all-to-all-done), kind=kOutput, calls=%fused_computation.2 | convolution fusion | flops 4844421120 | bytes 14155776 | tf_op jit(solution)/shard_map/esd,df->esf/dot_general | solution.py:85
  185.8 5.1 %multiply_reduce_fusion = (bf16[32,24]{1,0:T(8,128)(2,1)S(1)}, f32[32,24,768]{2,1,0:T(8,128)S(1)}) fusion(f32[32,24,1536]{2,1,0:T(8,128)S(1)} %fusion, bf16[1,1,768,2048]{3,2,1,0:T(8,128)(2,1)S(1)} %copy-done, bf16[32,24,4096]{2,1,0:T(8,128)(2,1)} %all-to-all-done), kind=kOutput, calls=%fused_computation.25 | convolution fusion | flops 2420047104 | bytes 13370880 | tf_op jit(solution)/shard_map/esd,fd->esf/dot_general | solution.py:91
  190.9 3.7 %fusion.5 = f32[32,24,2176]{2,1,0:T(8,128)S(1)} fusion(bf16[2048,768]{1,0:T(8,128)(2,1)S(1)} %bitcast.79, f32[32,24,768]{2,1,0:T(8,128)S(1)} %get-tuple-element.31, f32[32,24,1536]{2,1,0:T(8,128)S(1)} %fusion), kind=kOutput, calls=%fused_computation.11 | convolution fusion | flops 2572812288 | bytes 16908288 | tf_op jit(solution)/shard_map/esf,df->esd/dot_general | solution.py:99
  194.7 5.0 %select_convert_fusion = bf16[32,24,2176]{2,1,0:T(8,128)(2,1)} fusion(f32[32,24,2176]{2,1,0:T(8,128)S(1)} %fusion.5, f32[2176]{0:T(1024)S(1)} %pad_convert_fusion, bf16[2048,768]{1,0:T(8,128)(2,1)S(1)} %bitcast.81, f32[32,24]{1,0:T(8,128)S(1)} %convert_element_type.185, pred[2176]{0:T(1024)(128)(4,1)S(1)} %iota_compare_fusion.4, ...), kind=kOutput, calls=%fused_computation | convolution fusion | flops 2578808832 | bytes 17923072 | tf_op jit(solution)/shard_map/esf,df->esd/dot_general | solution.py:101
  199.6 5.7 %all-to-all-start.1 = ((bf16[32,24,2176]{2,1,0:T(8,128)(2,1)}), bf16[32,24,2176]{2,1,0:T(8,128)(2,1)}, u32[]{:S(2)}, u32[]{:S(2)}) async-start(bf16[32,24,2176]{2,1,0:T(8,128)(2,1)} %select_convert_fusion), calls=%async_computation.1 | async-start | bytes 6684672 | tf_op jit(solution)/shard_map/all_to_all | solution.py:72
  205.4 1.0 select_reduce_fusion
  206.4 1.4 fusion.24
  207.8 2.6 convolution_add_fusion.1
  210.4 74.9 %all-to-all-done.1 = bf16[32,24,2176]{2,1,0:T(8,128)(2,1)} async-done(((bf16[32,24,2176]{2,1,0:T(8,128)(2,1)}), bf16[32,24,2176]{2,1,0:T(8,128)(2,1)}, u32[]{:S(2)}, u32[]{:S(2)}) %all-to-all-start.1) | async-done | bytes 3342368 | tf_op jit(solution)/shard_map/all_to_all | solution.py:72
  285.3 0.9 slice.113
  286.2 2.2 convolution_bitcast_fusion.1
  288.7 0.2 multiply_reduce_fusion.1
  289.0 0.7 copy.49
  289.7 3.1 %convolution_bitcast_fusion = f32[192,2176]{1,0:T(8,128)S(1)} fusion(bf16[192,32,24]{0,1,2:T(8,128)(2,1)} %add_convert_fusion, bf16[32,24,2176]{2,1,0:T(8,128)(2,1)} %all-to-all-done.1), kind=kOutput, calls=%fused_computation.6 | convolution fusion | flops 641728512 | bytes 5308416 | tf_op jit(solution)/shard_map/tes,esd->td/dot_general | solution.py:124
  292.8 2.5 fusion.19
  (37 shorter events, 1.7 us)
Async XLA Ops:
  0.6 185.1 %copy-start = (bf16[1,1,768,2048]{3,2,1,0:T(8,128)(2,1)S(1)}, bf16[1,1,768,2048]{3,2,1,0:T(8,128)(2,1)}, u32[]{:S(2)}) copy-start(bf16[1,1,768,2048]{3,2,1,0:T(8,128)(2,1)} %param.14) | copy-start | bytes 9437188
  0.6 19.7 %collective-permute-start = (bf16[1,192,2048]{2,1,0:T(8,128)(2,1)}, bf16[1,192,2048]{2,1,0:T(8,128)(2,1)}, u32[]{:S(2)}, u32[]{:S(2)}) collective-permute-start(bf16[1,192,2048]{2,1,0:T(8,128)(2,1)} %param.8), channel_id=1, source_target_pairs={{0,224},{32,0},{64,32},{96,64},{128,96},{160,128},{192,160},{224,1... | collective-permute-start | bytes 2359304 | tf_op jit(solution)/shard_map/ppermute | solution.py:9
  7.6 4.7 %copy-start.3 = (bf16[1,192,2048]{2,1,0:T(8,128)(2,1)S(1)}, bf16[1,192,2048]{2,1,0:T(8,128)(2,1)}, u32[]{:S(2)}) copy-start(bf16[1,192,2048]{2,1,0:T(8,128)(2,1)} %param.9) | copy-start | bytes 2359300
  24.2 153.2 %all-to-all-start = ((bf16[32,24,4096]{2,1,0:T(8,128)(2,1)}), bf16[32,24,4096]{2,1,0:T(8,128)(2,1)}, u32[]{:S(2)}, u32[]{:S(2)}) async-start(bf16[32,24,4096]{2,1,0:T(8,128)(2,1)} %fusion.3), calls=%async_computation | async-start | bytes 12582912 | tf_op jit(solution)/shard_map/all_to_all | solution.py:72
  185.8 5.1 %copy-start.5 = (bf16[1,1,2048,768]{3,2,1,0:T(8,128)(2,1)S(1)}, bf16[1,1,2048,768]{3,2,1,0:T(8,128)(2,1)}, u32[]{:S(2)}) copy-start(bf16[1,1,2048,768]{3,2,1,0:T(8,128)(2,1)} %param.12) | copy-start | bytes 9437188
  190.9 3.7 %copy-start.6 = (bf16[1,1,2048,768]{3,2,1,0:T(8,128)(2,1)S(1)}, bf16[1,1,2048,768]{3,2,1,0:T(8,128)(2,1)}, u32[]{:S(2)}) copy-start(bf16[1,1,2048,768]{3,2,1,0:T(8,128)(2,1)} %param.13) | copy-start | bytes 9437188
  199.6 5.7 %copy-start.4 = (s32[1,192,8]{1,2,0:T(8,128)S(1)}, s32[1,192,8]{1,2,0:T(8,128)}, u32[]{:S(2)}) copy-start(s32[1,192,8]{1,2,0:T(8,128)} %param.10) | copy-start | bytes 18436
  199.6 85.7 %all-to-all-start.1 = ((bf16[32,24,2176]{2,1,0:T(8,128)(2,1)}), bf16[32,24,2176]{2,1,0:T(8,128)(2,1)}, u32[]{:S(2)}, u32[]{:S(2)}) async-start(bf16[32,24,2176]{2,1,0:T(8,128)(2,1)} %select_convert_fusion), calls=%async_computation.1 | async-start | bytes 6684672 | tf_op jit(solution)/shard_map/all_to_all | solution.py:72
  289.7 3.1 %copy-start.1 = (bf16[1,2048,128]{2,1,0:T(8,128)(2,1)S(1)}, bf16[1,2048,128]{2,1,0:T(8,128)(2,1)}, u32[]{:S(2)}) copy-start(bf16[1,2048,128]{2,1,0:T(8,128)(2,1)} %param.15) | copy-start | bytes 1572868
  289.7 3.1 %copy-start.2 = (f32[192,2048]{1,0:T(8,128)S(1)}, f32[192,2048]{1,0:T(8,128)}, u32[]{:S(2)}) copy-start(f32[192,2048]{1,0:T(8,128)} %convolution_add_fusion.1) | copy-start | bytes 4718596
